TPU v7x, 128 devices: a whole 4x4x4 slice. The times are simulated.
128 devices in a mesh: pages: 32 (over y, x, core), mp: 4 (over z).
Axes of the slice: x: 4, y: 4, z: 4, core: 2. Of those that a mesh axis runs over, the one named last changes fastest.
Arguments:
- tokens: bfloat16 [4, 64, 3072], P(None, None, 'pages'), may hold values from -4.5 to 4.5
- norm_gains: float32 [2, 3072], P(None, 'pages'), may hold values from 0.1 to 1.9
- w_qkv: bfloat16 [3072, 3, 3072], P('pages', None, 'mp'), may hold values from -0.109375 to 0.109375
- w_out: bfloat16 [3072, 3072], P('pages', 'mp'), may hold values from -0.109375 to 0.109375
- w_gate_up: bfloat16 [2, 3072, 8192], P(None, 'pages', 'mp'), may hold values from -0.109375 to 0.109375
- w_down: bfloat16 [3072, 8192], P('pages', 'mp'), may hold values from -0.0625 to 0.0625
- k_cache: bfloat16 [1024, 64, 3072], P('pages', None, 'mp'), may hold values from -1000 to 1000, as said below
- v_cache: bfloat16 [1024, 64, 3072], P('pages', None, 'mp'), may hold values from -6 to 6
- lengths: int32 [64], replicated, may hold values from 1 to 4096, as said below
- slot_request: int32 [1024], replicated, may hold values from -1 to 63, as said below
- slot_page: int32 [1024], replicated, may hold values from 0 to 63
- move_slot: int32 [32, 31], replicated, may hold values from 0 to 31, as said below
- move_offset: int32 [31], replicated, may hold values from 1 to 31, as said below
Outputs:
- layer_out: bfloat16 [4, 64, 3072], P(None, None, 'pages')
- new_k_cache: bfloat16 [1024, 64, 3072], P('pages', None, 'mp')
- new_v_cache: bfloat16 [1024, 64, 3072], P('pages', None, 'mp')
Inputs may be any that keep to these rules, and one draw needn't show every extreme that they name: `lengths`: every request holds ceil(length / 64) pages, numbered from 0, each in exactly one slot; the longest holds 4096 tokens. `slot_request`: slots of requests and empty slots lie on holders in no fixed order. `move_slot`: each holder's row names 31 distinct local slots. `move_offset`: every offset from 1 to 31 appears exactly once. `k_cache`: cached keys lie within the range given in the table.
All inputs are finite; a program needn't handle non-finite values.
Results may differ from a plain program's by a relative error of at most 0.018.
The roundings to bfloat16 on the way count: a program that leaves them out, or rounds other values in their place, can miss the bound.
Values may be sent and summed in bfloat16 or wider, within the bound.
No kernel may reach another device: no remote copies, remote signals or barrier semaphores. Data moves between devices by JAX's collectives and lax.ppermute only.
A program may use at most 128 MiB of HBM per device.

v0:
```python
import jax
import jax.numpy as jnp
from jax import lax
from jax.sharding import PartitionSpec as P

D = 3072
HEAD_DIM = 96


EPSILON = 1e-05
NEGATIVE = -1e30
THETA = 10000.0
CONTRACT_LAST = (((1,), (1,)), ((), ()))


def merged(part, axis, combine):
    gathered = jax.tree.map(lambda a: lax.all_gather(a, axis), part)

    def take(source):
        return jax.tree.map(lambda a: lax.dynamic_index_in_dim(a, source, 0, False), gathered)

    return lax.fori_loop(
        1, lax.axis_size(axis), lambda source, state: combine(state, take(source)), take(0)
    )


def rotate(values, positions):
    half_dim = values.shape[-1] // 2
    exponent = jnp.arange(half_dim, dtype=jnp.float32) * (-2.0 / values.shape[-1])
    frequency = jnp.power(jnp.float32(THETA), exponent)
    angles = positions.astype(jnp.float32)[:, None, None] * frequency[None, None, :]
    cosine = jnp.cos(angles)
    sine = jnp.sin(angles)
    first = values[..., :half_dim]
    second = values[..., half_dim:]
    return jnp.concatenate(
        [first * cosine - second * sine, second * cosine + first * sine], axis=-1
    )


def merge_parts(first, second):
    top_a, total_a, accum_a = first
    top_b, total_b, accum_b = second
    joined = jnp.maximum(top_a, top_b)
    factor_a = jnp.exp(top_a - joined)
    factor_b = jnp.exp(top_b - joined)
    return (
        joined,
        total_a * factor_a + total_b * factor_b,
        accum_a * factor_a[..., None] + accum_b * factor_b[..., None],
    )


def reduce_rows(partial_value, squares, finish):
    total, total_sq = lax.psum((partial_value, squares), "pages")
    return finish(total, total_sq, 0)


def across_heads(term):
    return lax.psum(term, "mp")


def migrate_pool(key_local, value_local, move_slot, move_offset):
    holders = lax.axis_size("pages")
    myself = lax.axis_index("pages")
    mine = lax.dynamic_index_in_dim(move_slot, myself, 0, keepdims=False)
    targets = (myself + move_offset) % holders
    holder_ids = jnp.arange(holders, dtype=jnp.int32)
    aimed = holder_ids[:, None] == targets[None, :]
    chosen = jnp.sum(jnp.where(aimed, mine[None, :], 0), axis=1)
    sending = jnp.any(aimed, axis=1)[:, None, None]
    key_send = jnp.where(sending, key_local[chosen], jnp.zeros((), key_local.dtype))
    value_send = jnp.where(sending, value_local[chosen], jnp.zeros((), value_local.dtype))
    key_recv, value_recv = (
        lax.all_to_all(key_send, "pages", split_axis=0, concat_axis=0, tiled=True),
        lax.all_to_all(value_send, "pages", split_axis=0, concat_axis=0, tiled=True),
    )
    sources = (myself - move_offset) % holders
    slot_ids = jnp.arange(key_local.shape[0], dtype=jnp.int32)
    landing = slot_ids[:, None] == mine[None, :]
    came_from = jnp.sum(jnp.where(landing, sources[None, :], 0), axis=1)
    arriving = jnp.any(landing, axis=1)[:, None, None]
    return (
        jnp.where(arriving, key_recv[came_from], key_local),
        jnp.where(arriving, value_recv[came_from], value_local),
    )


def local_attention(queries, k_cache, v_cache, lengths, slot_request, slot_page):
    step_count, req_count, heads_here, head_dim = queries.shape
    slot_count, page_len, channels = k_cache.shape
    scale = head_dim ** (-0.5)
    myself = lax.axis_index("pages")
    own_request = lax.dynamic_slice_in_dim(slot_request, myself * slot_count, slot_count)
    own_page = lax.dynamic_slice_in_dim(slot_page, myself * slot_count, slot_count)
    owners = jnp.clip(own_request, 0, req_count - 1)
    key_pos = own_page[:, None] * page_len + jnp.arange(page_len, dtype=jnp.int32)[None, :]
    usable = (own_request >= 0)[:, None] & (key_pos < lengths[owners][:, None])
    keys_here = k_cache.reshape(slot_count, page_len, heads_here, head_dim)
    values_here = v_cache.reshape(slot_count, page_len, heads_here, head_dim)
    scores = (
        jnp.einsum(
            "tshd,skhd->tshk", queries[:, owners], keys_here, preferred_element_type=jnp.float32
        )
        * scale
    )
    live_mask = usable[None, :, None, :]
    scores = jnp.where(live_mask, scores, NEGATIVE)
    slot_top = jnp.max(scores, axis=3)
    belongs = own_request[None, :] == jnp.arange(req_count, dtype=jnp.int32)[:, None]
    request_top = jnp.max(
        jnp.where(belongs[None, :, :, None], slot_top[:, None, :, :], NEGATIVE), axis=2
    )
    weights = jnp.where(live_mask, jnp.exp(scores - request_top[:, owners][..., None]), 0.0)
    slot_total = jnp.sum(weights, axis=3)
    slot_acc = jnp.einsum(
        "tshk,skhd->tshd",
        weights.astype(jnp.bfloat16),
        values_here,
        preferred_element_type=jnp.float32,
    )
    indicator = belongs.astype(jnp.float32)
    totals = jnp.einsum("rs,tsh->trh", indicator, slot_total, precision=lax.Precision.HIGHEST)
    accums = jnp.einsum("rs,tshd->trhd", indicator, slot_acc, precision=lax.Precision.HIGHEST)
    return (request_top, totals, accums)


def shards(
    tokens,
    norm_gains,
    w_qkv,
    w_out,
    w_gate_up,
    w_down,
    k_cache,
    v_cache,
    lengths,
    slot_request,
    slot_page,
    move_slot,
    move_offset,
):
    step_count, req_count, width_here = tokens.shape
    row_count = step_count * req_count
    activ = tokens.reshape(row_count, width_here).astype(jnp.float32)
    row_ids = jnp.arange(row_count, dtype=jnp.int32)
    positions = lengths[row_ids % req_count] + row_ids // req_count

    def finish_qkv(total, squares, start):
        count = total.shape[0]
        inverse = lax.rsqrt(squares / D + EPSILON)
        scaled = total * inverse[:, None, None]
        heads_here = scaled.shape[2] // HEAD_DIM
        query_rows = rotate(scaled[:, 0].reshape(count, heads_here, HEAD_DIM), positions)
        key_rows = rotate(scaled[:, 1].reshape(count, heads_here, HEAD_DIM), positions)
        return (
            query_rows.reshape(count, -1).astype(jnp.bfloat16),
            key_rows.reshape(count, -1).astype(jnp.bfloat16),
            scaled[:, 2].astype(jnp.bfloat16),
        )

    def finish_mlp(total, squares, start):
        inverse = lax.rsqrt(squares / D + EPSILON)
        gate = total[:, 0] * inverse[:, None]
        upward = total[:, 1] * inverse[:, None]
        return ((jax.nn.silu(gate) * upward).astype(jnp.bfloat16),)

    normed_one = (activ * norm_gains[0]).astype(jnp.bfloat16)
    partial_one = jnp.einsum("bd,dcn->bcn", normed_one, w_qkv, preferred_element_type=jnp.float32)
    squares_one = jnp.sum(activ * activ, axis=1)
    query_all, key_all, value_all = reduce_rows(partial_one, squares_one, finish_qkv)
    heads_here = query_all.shape[1] // HEAD_DIM
    queries = query_all.reshape(step_count, req_count, heads_here, HEAD_DIM)
    key_fresh = key_all.reshape(step_count, req_count, heads_here, HEAD_DIM)
    value_fresh = value_all.reshape(step_count, req_count, heads_here, HEAD_DIM)
    cache_top, cache_total, cache_acc = local_attention(
        queries, k_cache, v_cache, lengths, slot_request, slot_page
    )
    cache_top, cache_total, cache_acc = merged(
        (cache_top, cache_total, cache_acc), "pages", merge_parts
    )
    scale = HEAD_DIM ** (-0.5)
    step_ids = jnp.arange(step_count, dtype=jnp.int32)
    causal = (step_ids[:, None] >= step_ids[None, :])[:, :, None, None]
    fresh = (
        jnp.einsum("trhd,urhd->turh", queries, key_fresh, preferred_element_type=jnp.float32)
        * scale
    )
    fresh = jnp.where(causal, fresh, NEGATIVE)
    row_top = jnp.maximum(cache_top, jnp.max(fresh, axis=1))
    carried = jnp.exp(cache_top - row_top)
    fresh_w = jnp.where(causal, jnp.exp(fresh - row_top[:, None]), 0.0)
    totals = cache_total * carried + jnp.sum(fresh_w, axis=1)
    accums = cache_acc * carried[..., None] + jnp.einsum(
        "turh,urhd->trhd",
        fresh_w.astype(jnp.bfloat16),
        value_fresh,
        preferred_element_type=jnp.float32,
    )
    attended = (
        (accums / totals[..., None]).astype(jnp.bfloat16).reshape(row_count, heads_here * HEAD_DIM)
    )
    mixed = activ + across_heads(
        lax.dot_general(attended, w_out, CONTRACT_LAST, preferred_element_type=jnp.float32)
    )
    normed_two = (mixed * norm_gains[1]).astype(jnp.bfloat16)
    partial_two = jnp.einsum(
        "bd,gdf->bgf", normed_two, w_gate_up, preferred_element_type=jnp.float32
    )
    squares_two = jnp.sum(mixed * mixed, axis=1)
    (hidden,) = reduce_rows(partial_two, squares_two, finish_mlp)
    feed = across_heads(
        lax.dot_general(hidden, w_down, CONTRACT_LAST, preferred_element_type=jnp.float32)
    )
    layer_out = (mixed + feed).astype(jnp.bfloat16).reshape(step_count, req_count, width_here)
    new_k_cache, new_v_cache = migrate_pool(k_cache, v_cache, move_slot, move_offset)
    return (layer_out, new_k_cache, new_v_cache)


def solution(mesh):
    in_specs = (
        P(None, None, "pages"),
        P(None, "pages"),
        P("pages", None, "mp"),
        P("pages", "mp"),
        P(None, "pages", "mp"),
        P("pages", "mp"),
        P("pages", None, "mp"),
        P("pages", None, "mp"),
        P(),
        P(),
        P(),
        P(),
        P(),
    )
    out_specs = (P(None, None, "pages"), P("pages", None, "mp"), P("pages", None, "mp"))
    return jax.shard_map(shards, mesh=mesh, in_specs=in_specs, out_specs=out_specs, check_vma=False)
```

profile of v0, /device:TPU:0, one launch (start us, length us, event | category | flops | bytes accessed | tf_op | source)
XLA Modules:
  0.0 611.6 jit_solution(16740435697585589592)
XLA Ops:
  8.5 2.9 fusion.41
  11.8 67.6 %psum.43 = f32[256]{0:T(256)S(1)} all-reduce(f32[256]{0:T(256)S(1)} %reduce_sum.61), channel_id=1, replica_groups=mesh['pages'=32,'mp'=4] {'pages'}, use_global_device_ids=true, to_apply=%region_2.3 | all-reduce | flops 256 | bytes 2048 | tf_op jit(solution)/shard_map/psum | solution.py:55
  79.4 8.3 %reshape.259 = bf16[32,64,8,96]{3,2,1,0:T(8,128)(2,1)} reshape(bf16[32,64,768]{2,1,0:T(8,128)(2,1)} %param.21) | data formatting | bytes 6291456 | tf_op jit(solution)/shard_map/reshape | solution.py:99
  91.1 8.2 %reshape.260 = bf16[32,64,8,96]{3,2,1,0:T(8,128)(2,1)} reshape(bf16[32,64,768]{2,1,0:T(8,128)(2,1)} %param.22) | data formatting | bytes 6291456 | tf_op jit(solution)/shard_map/reshape | solution.py:100
  101.1 20.7 %all-reduce.5.cloned.1.call-done = f32[256,3,768]{2,0,1:T(8,128)} async-done(((f32[256,3,768]{2,0,1:T(8,128)}), f32[256,3,768]{2,0,1:T(8,128)}) %all-reduce.5.cloned.1.call-update) | async-done | bytes 2359312 | tf_op jit(solution)/shard_map/psum | solution.py:55
  124.9 2.3 copy.126
  127.2 2.3 copy.115
  131.9 2.1 copy.116
  134.0 2.4 gather_fusion.2
  136.4 6.0 fusion.68
  146.0 2.3 gather_fusion.3
  150.0 3.7 fusion.11
  159.5 4.4 gather_fusion.6
  164.0 4.6 gather_fusion.4
  169.3 6.0 broadcast_select_fusion
  175.4 5.7 all-to-all-start.1
  182.7 1.9 fusion.29
  185.3 54.7 %all-gather = f32[128,64,8]{1,2,0:T(8,128)S(1)} all-gather(f32[4,64,8]{1,2,0:T(8,128)S(1)} %select_reduce_fusion), channel_id=2, replica_groups=mesh['pages'=32,'mp'=4] {'pages'}, dimensions={0}, use_global_device_ids=true | all-gather | bytes 270336 | tf_op jit(solution)/shard_map/all_gather | solution.py:17
  241.6 25.9 %all-gather.1 = f32[128,64,8]{1,2,0:T(8,128)S(1)} all-gather(f32[4,64,8]{1,2,0:T(8,128)S(1)} %convolution_bitcast_fusion.1), channel_id=3, replica_groups=mesh['pages'=32,'mp'=4] {'pages'}, dimensions={0}, use_global_device_ids=true | all-gather | bytes 270336 | tf_op jit(solution)/shard_map/all_gather | solution.py:17
  268.3 27.5 %all-gather.5.cloned.1.call-done = f32[128,64,8,96]{3,2,1,0:T(8,128)} async-done(((f32[4,64,8,96]{3,2,1,0:T(8,128)}), f32[128,64,8,96]{3,2,1,0:T(8,128)}) %all-gather.5.cloned.1.call-update) | async-done | bytes 25165840 | tf_op jit(solution)/shard_map/all_gather | solution.py:17
  297.1 88.7 %while.19 = (s32[]{:T(128)}, f32[4,64,8]{1,2,0:T(8,128)S(1)}, f32[4,64,8]{1,2,0:T(8,128)S(1)}, f32[4,64,8,96]{3,2,1,0:T(8,128)S(1)}, f32[32,4,64,8]{2,3,1,0:T(8,...) while((s32[]{:T(128)}, f32[4,64,8]{1,2,0:T(8,128)S(1)}, ...), condition=%wide.region_7.8_spmd, body=%wide.region_6.7_spmd.sunk | while | flops 602117 | bytes 2474135 | solution.py:22
  303.8 1.9 fusion.81
  390.8 4.8 all-to-all-start
  399.7 43.0 %all-reduce.7.cloned.1.call-done = f32[256,96]{0,1:T(8,128)} async-done(((f32[256,96]{0,1:T(8,128)}), f32[256,96]{0,1:T(8,128)}) %all-reduce.7.cloned.1.call-update) | async-done | bytes 98320 | tf_op jit(solution)/shard_map/psum | solution.py:60
  443.7 2.8 fusion.46
  447.3 4.3 gather_fusion.7
  451.6 4.4 gather_fusion.5
  455.9 65.1 %psum.46 = f32[256]{0:T(256)S(1)} all-reduce(f32[256]{0:T(256)S(1)} %get-tuple-element.221), channel_id=1, replica_groups=mesh['pages'=32,'mp'=4] {'pages'}, use_global_device_ids=true, to_apply=%region_13.14 | all-reduce | flops 256 | bytes 2048 | tf_op jit(solution)/shard_map/psum | solution.py:55
  521.0 37.1 %all-reduce.9.cloned.1.call-done = f32[256,2,2048]{2,0,1:T(8,128)} async-done(((f32[256,2,2048]{2,0,1:T(8,128)}), f32[256,2,2048]{2,0,1:T(8,128)}) %all-reduce.9.cloned.1.call-update) | async-done | bytes 4194320 | tf_op jit(solution)/shard_map/psum | solution.py:55
  558.2 3.7 fusion.25
  561.9 8.0 %broadcast_select_fusion.2 = (bf16[32,64,768]{2,1,0:T(8,128)(2,1)}, bf16[32,64,768]{2,1,0:T(8,128)(2,1)}) fusion(bf16[32,64,768]{2,1,0:T(8,128)(2,1)} %gather_fusion.7, bf16[32,64,768]{2,1,0:T(8,128)(2,1)} %param.22, pred[32]{0:T(512)(128)(4,1)S(1)} %fusion.52, bf16[32,64,768]{2,1,0:T(8,128)(2,1)} %gather_fusion.5, bf16[32,64,768]{2,1,0:T(8,128)(2,1)} %param.21), kind=kLoop, calls=%fused_computation.22 | loop fusion | flops 3145728 | bytes 18874400 | tf_op jit(solution)/shard_map/jit(_where)/select_n | solution.py:85
  569.9 33.5 %all-reduce.11.cloned.1.call-done = f32[256,96]{0,1:T(8,128)} async-done(((f32[256,96]{0,1:T(8,128)}), f32[256,96]{0,1:T(8,128)}) %all-reduce.11.cloned.1.call-update) | async-done | bytes 98320 | tf_op jit(solution)/shard_map/psum | solution.py:60
  (238 shorter events, 128.1 us)
Async XLA Ops:
  7.2 436.6 %copy-start = (bf16[2,96,2048]{2,1,0:T(8,128)(2,1)S(1)}, bf16[2,96,2048]{2,1,0:T(8,128)(2,1)}, u32[]{:S(2)}) copy-start(bf16[2,96,2048]{2,1,0:T(8,128)(2,1)} %param.19) | copy-start | bytes 2359300
  7.2 4.3 copy-start.4
  7.2 114.5 %all-reduce.5.cloned.1.call-start = ((), (), s32[]{:S(2)}) async-start(), calls=%async_computation.2 | async-start | bytes 4718592 | tf_op jit(solution)/shard_map/psum | solution.py:55
  11.5 284.3 %all-gather.5.cloned.1.call-start = ((), (), s32[]{:S(2)}) async-start(), calls=%async_computation.6 | async-start | bytes 34603008 | tf_op jit(solution)/shard_map/all_gather | solution.py:17
  79.4 9.1 %copy-start.1 = (s32[64]{0:T(128)S(1)}, s32[64]{0:T(128)}, u32[]{:S(2)}) copy-start(s32[64]{0:T(128)} %param.23) | copy-start | bytes 772
  88.4 11.6 %copy-start.11 = (s32[32]{0:T(128)}, s32[32]{0:T(128)S(1)}, u32[]{:S(2)}) copy-start(s32[32]{0:T(128)S(1)} %get-tuple-element.226) | copy-start | bytes 388
  88.5 45.5 %copy-start.10 = (s32[1024]{0:T(1024)}, s32[1024]{0:T(1024)S(1)}, u32[]{:S(2)}) copy-start(s32[1024]{0:T(1024)S(1)} %pad_clamp_fusion.3) | copy-start | bytes 12292
  100.8 35.6 %copy-start.8 = (pred[32,64]{1,0:T(8,128)(4,1)}, pred[32,64]{1,0:T(8,128)(4,1)S(1)}, u32[]{:S(2)}) copy-start(pred[32,64]{1,0:T(8,128)(4,1)S(1)} %fusion.53) | copy-start | bytes 6148
  150.0 3.7 copy-start.12
  157.0 1.9 copy-start.16
  157.7 0.6 copy-start.14
  175.4 215.4 %all-to-all-start.1 = ((bf16[32,64,768]{2,1,0:T(8,128)(2,1)}), bf16[32,64,768]{2,1,0:T(8,128)(2,1)}, u32[]{:S(2)}, u32[]{:S(2)}) async-start(bf16[32,64,768]{2,1,0:T(8,128)(2,1)} %get-tuple-element.243), calls=%async_computation.1 | async-start | bytes 6291456 | tf_op jit(solution)/shard_map/all_to_all | solution.py:76
  182.4 85.2 %copy-start.2 = (bf16[256,1,768]{2,0,1:T(8,128)(2,1)S(1)}, bf16[256,1,768]{2,0,1:T(8,128)(2,1)}, u32[]{:S(2)}) copy-start(bf16[256,1,768]{2,0,1:T(8,128)(2,1)} %slice.104) | copy-start | bytes 1179652
  182.7 57.4 %copy-start.6 = (f32[4,32,8,64]{3,0,2,1:T(4,128)S(1)}, f32[4,32,8,64]{3,0,2,1:T(4,128)}, u32[]{:S(2)}) copy-start(f32[4,32,8,64]{3,0,2,1:T(4,128)} %get-tuple-element.248) | copy-start | bytes 786436
  182.7 57.4 %copy-start.7 = (f32[4,32,8]{0,2,1:T(8,128)S(1)}, f32[4,32,8]{0,2,1:T(8,128)}, u32[]{:S(2)}) copy-start(f32[4,32,8]{0,2,1:T(8,128)} %copy.121) | copy-start | bytes 12292
  182.7 57.4 %copy-start.9 = (pred[32,64]{1,0:T(8,128)(4,1)S(1)}, pred[32,64]{1,0:T(8,128)(4,1)}, u32[]{:S(2)}) copy-start(pred[32,64]{1,0:T(8,128)(4,1)} %copy-done.8) | copy-start | bytes 6148
  182.7 85.4 %copy-start.13 = (pred[4,4]{1,0:T(4,128)(4,1)S(1)}, pred[4,4]{1,0:T(4,128)(4,1)}, u32[]{:S(2)}) copy-start(pred[4,4]{1,0:T(4,128)(4,1)} %iota_compare_fusion.5) | copy-start | bytes 52
  267.5 0.8 copy-start.3
  390.8 60.8 %all-to-all-start = ((bf16[32,64,768]{2,1,0:T(8,128)(2,1)}), bf16[32,64,768]{2,1,0:T(8,128)(2,1)}, u32[]{:S(2)}, u32[]{:S(2)}) async-start(bf16[32,64,768]{2,1,0:T(8,128)(2,1)} %get-tuple-element.244), calls=%async_computation | async-start | bytes 6291456 | tf_op jit(solution)/shard_map/all_to_all | solution.py:75
  395.6 4.0 copy-start.5
  395.7 48.1 %copy-start.15 = (f32[96]{0:T(128)S(1)}, f32[96]{0:T(128)}, u32[]{:S(2)}) copy-start(f32[96]{0:T(128)} %get-tuple-element.239) | copy-start | bytes 1156
  395.7 47.1 %all-reduce.7.cloned.1.call-start = ((), (), s32[]{:S(2)}) async-start(), calls=%async_computation.3 | async-start | bytes 196608 | tf_op jit(solution)/shard_map/psum | solution.py:60
  399.6 158.6 %all-reduce.9.cloned.1.call-start = ((), (), s32[]{:S(2)}) async-start(), calls=%async_computation.4 | async-start | bytes 8388608 | tf_op jit(solution)/shard_map/psum | solution.py:55
  446.5 0.6 copy-start.18
  446.5 0.7 copy-start.17
  446.5 156.9 %all-reduce.11.cloned.1.call-start = ((), (), s32[]{:S(2)}) async-start(), calls=%async_computation.5 | async-start | bytes 196608 | tf_op jit(solution)/shard_map/psum | solution.py:60
  451.6 106.6 %copy-start.19 = (bf16[96,2048]{1,0:T(8,128)(2,1)S(1)}, bf16[96,2048]{1,0:T(8,128)(2,1)}, u32[]{:S(2)}) copy-start(bf16[96,2048]{1,0:T(8,128)(2,1)} %param.20) | copy-start | bytes 1179652
Sparse Core Ops, SparseCore 0:
  11.9 109.8 all-reduce.4
  156.4 139.3 all-gather.4
  399.7 43.0 all-reduce.6
  446.6 111.4 all-reduce.8
  562.0 41.3 all-reduce.10
where the time goes:
time: 616 us; the launch traced here: 612 us
  blocking collectives  213 us (35%)
  waiting for transfers between devices  162 us (26%)
  other arithmetic  112 us (18%)
  local copies, waits for them, and re-layouts  72.5 us (12%)
  matrix products  26.2 us (4%)
  between operations  14.2 us (2%)
  starting transfers between devices  10.7 us (2%)
    psum x2, blocking collectives, reduce_rows(): total, total_sq = lax.psum((partial_value, squares), 'pages')  133 us
    all_gather x2, blocking collectives, merged(): gathered = jax.tree.map(lambda a: lax.all_gather(a, axis), part)  80.6 us
    psum x2, waiting for transfers between devices, across_heads(): return lax.psum(term, 'mp')  76.6 us
    add x31, other arithmetic, merge_parts(): accum_a * factor_a[..., None] + accum_b * factor_b[..., None]  58.7 us
    psum x2, waiting for transfers between devices, reduce_rows(): total, total_sq = lax.psum((partial_value, squares), 'pages')  57.8 us
    all_gather x1, waiting for transfers between devices, merged(): gathered = jax.tree.map(lambda a: lax.all_gather(a, axis), part)  27.5 us
    add x31, other arithmetic, merge_parts(): total_a * factor_a + total_b * factor_b  23.1 us
  transfers between devices with their start and end apart: 7, of which 5 were waited for; matrix products, arithmetic and copies ran while one was open for 27% of the time, Pallas kernels for 0%

commit v1 on v0

--- a/solution.py
+++ b/solution.py
@@ -52,8 +52,11 @@
 
 
 def reduce_rows(partial_value, squares, finish):
-    total, total_sq = lax.psum((partial_value, squares), "pages")
-    return finish(total, total_sq, 0)
+    rows = partial_value.shape[0]
+    packed = jnp.concatenate([partial_value.reshape(rows, -1), squares[:, None]], axis=1)
+    packed = lax.psum(packed, "pages")
+    total = packed[:, :-1].reshape(partial_value.shape)
+    return finish(total, packed[:, -1], 0)
 
 
 def across_heads(term):
@@ -176,29 +179,42 @@
     cache_top, cache_total, cache_acc = local_attention(
         queries, k_cache, v_cache, lengths, slot_request, slot_page
     )
-    cache_top, cache_total, cache_acc = merged(
-        (cache_top, cache_total, cache_acc), "pages", merge_parts
-    )
+    holders = lax.axis_size("pages")
+    myself = lax.axis_index("pages")
+    group = req_count // holders
+    packed = jnp.concatenate(
+        [cache_acc, cache_total[..., None], cache_top[..., None]], axis=-1
+    ).reshape(step_count, holders, group, heads_here, HEAD_DIM + 2)
+    packed = jnp.moveaxis(packed, 1, 0)
+    packed = lax.all_to_all(packed, "pages", split_axis=0, concat_axis=0, tiled=True)
+    part_acc = packed[..., :HEAD_DIM]
+    part_total = packed[..., HEAD_DIM]
+    part_top = packed[..., HEAD_DIM + 1]
+    mine = lambda a: lax.dynamic_slice_in_dim(a, myself * group, group, 1)
+    queries_mine = mine(queries)
+    key_mine = mine(key_fresh)
+    value_mine = mine(value_fresh)
     scale = HEAD_DIM ** (-0.5)
     step_ids = jnp.arange(step_count, dtype=jnp.int32)
     causal = (step_ids[:, None] >= step_ids[None, :])[:, :, None, None]
     fresh = (
-        jnp.einsum("trhd,urhd->turh", queries, key_fresh, preferred_element_type=jnp.float32)
+        jnp.einsum("trhd,urhd->turh", queries_mine, key_mine, preferred_element_type=jnp.float32)
         * scale
     )
     fresh = jnp.where(causal, fresh, NEGATIVE)
-    row_top = jnp.maximum(cache_top, jnp.max(fresh, axis=1))
-    carried = jnp.exp(cache_top - row_top)
+    row_top = jnp.maximum(jnp.max(part_top, axis=0), jnp.max(fresh, axis=1))
+    carried = jnp.exp(part_top - row_top[None])
     fresh_w = jnp.where(causal, jnp.exp(fresh - row_top[:, None]), 0.0)
-    totals = cache_total * carried + jnp.sum(fresh_w, axis=1)
-    accums = cache_acc * carried[..., None] + jnp.einsum(
+    totals = jnp.sum(part_total * carried, axis=0) + jnp.sum(fresh_w, axis=1)
+    accums = jnp.sum(part_acc * carried[..., None], axis=0) + jnp.einsum(
         "turh,urhd->trhd",
         fresh_w.astype(jnp.bfloat16),
-        value_fresh,
+        value_mine,
         preferred_element_type=jnp.float32,
     )
-    attended = (
-        (accums / totals[..., None]).astype(jnp.bfloat16).reshape(row_count, heads_here * HEAD_DIM)
+    attended_mine = (accums / totals[..., None]).astype(jnp.bfloat16)
+    attended = lax.all_gather(attended_mine, "pages", axis=1, tiled=True).reshape(
+        row_count, heads_here * HEAD_DIM
     )
     mixed = activ + across_heads(
         lax.dot_general(attended, w_out, CONTRACT_LAST, preferred_element_type=jnp.float32)

time: 616 us -> 472 us (0.77)
  blocking collectives: 213 us -> 45 us
  waiting for transfers between devices: 162 us -> 262 us
  other arithmetic: 112 us -> 34.6 us
  matrix products: 26.2 us -> 13.8 us
  local copies, waits for them, and re-layouts: 72.5 us -> 84 us
    psum x2, waiting for transfers between devices: 57.8 us -> 191 us  [reduce_rows(): packed = lax.psum(packed, 'pages')]
    psum x2 -> x0, blocking collectives: 133 us -> none  [reduce_rows(): total, total_sq = lax.psum((partial_value, squares), 'pages')]
    add x63 -> x1, other arithmetic: 81.9 us -> 0.01 us  [shards(): totals = jnp.sum(part_total * carried, axis=0) + jnp.sum(fresh_w, axis=1)]
    all_gather x2 -> x1, blocking collectives: 80.6 us -> 45 us  [shards(): lax.all_gather(attended_mine, 'pages', axis=1, tiled=True)]
    all_gather x1 -> x0, waiting for transfers between devices: 27.5 us -> none  [merged(): gathered = jax.tree.map(lambda a: lax.all_gather(a, axis), part)]
    slice x1 -> x4, local copies, waits for them, and re-layouts: 2.28 us -> 17.7 us  [the longest x3 9.88 us: reduce_rows(): total = packed[:, :-1].reshape(partial_value.shape)]
    reshape x1 -> x3, local copies, waits for them, and re-layouts: 0.41 us -> 9.2 us  [the longest x1 6.59 us: reduce_rows(): total = packed[:, :-1].reshape(partial_value.shape)]
    psum x2, waiting for transfers between devices: 76.6 us -> 69 us  [across_heads(): return lax.psum(term, 'mp')]
  transfers between devices with their start and end apart: 7 -> 7, of which waited for: 5 -> 5; matrix products, arithmetic and copies ran while one was open for 27% -> 16% of each run, Pallas kernels for 0% -> 0%
where the time goes in v1:
time: 472 us; the launch traced here: 470 us
  waiting for transfers between devices  262 us (56%)
  local copies, waits for them, and re-layouts  84 us (18%)
  blocking collectives  45 us (10%)
  other arithmetic  34.6 us (7%)
  starting transfers between devices  16.7 us (4%)
  between operations  14.2 us (3%)
  matrix products  13.8 us (3%)
    psum x2, waiting for transfers between devices, reduce_rows(): packed = lax.psum(packed, 'pages')  191 us
    psum x2, waiting for transfers between devices, across_heads(): return lax.psum(term, 'mp')  69 us
    all_gather x1, blocking collectives, shards(): lax.all_gather(attended_mine, 'pages', axis=1, tiled=True)  45 us
    slice x3, local copies, waits for them, and re-layouts, reduce_rows(): total = packed[:, :-1].reshape(partial_value.shape)  9.88 us
  transfers between devices with their start and end apart: 7, of which 5 were waited for; matrix products, arithmetic and copies ran while one was open for 16% of the time, Pallas kernels for 0%

profile of v1, /device:TPU:0, one launch (start us, length us, event | category | flops | bytes accessed | tf_op | source)
XLA Modules:
  0.0 470.5 jit_solution(8013426628908517009)
XLA Ops:
  13.1 1.9 gather_fusion.1
  16.4 8.3 %reshape.304 = bf16[32,64,8,96]{3,2,1,0:T(8,128)(2,1)} reshape(bf16[32,64,768]{2,1,0:T(8,128)(2,1)} %param.19) | data formatting | bytes 6291456 | tf_op jit(solution)/shard_map/reshape | solution.py:102
  24.7 8.3 %reshape.305 = bf16[32,64,8,96]{3,2,1,0:T(8,128)(2,1)} reshape(bf16[32,64,768]{2,1,0:T(8,128)(2,1)} %param.20) | data formatting | bytes 6291456 | tf_op jit(solution)/shard_map/reshape | solution.py:103
  34.7 88.1 %all-reduce.5.cloned.1.call-done = f32[256,2305]{1,0:T(8,128)} async-done(((f32[256,2305]{1,0:T(8,128)}), f32[256,2305]{1,0:T(8,128)}) %all-reduce.5.cloned.1.call-update) | async-done | bytes 2360336 | tf_op jit(solution)/shard_map/psum | solution.py:57
  122.9 3.2 slice.89
  126.1 2.0 copy.173
  131.9 4.5 fusion.70
  138.7 3.4 fusion.7
  145.7 2.5 copy.187
  148.2 2.8 maximum_bitcast_fusion
  151.1 5.8 %all-to-all-start = ((f32[32,4,2,8,98]{4,3,2,1,0:T(8,128)}), f32[32,4,2,8,98]{4,3,2,1,0:T(8,128)S(1)}, u32[]{:S(2)}, u32[]{:S(2)}) async-start(f32[32,4,2,8,98]{4,3,2,1,0:T(8,128)} %maximum_bitcast_fusion), calls=%async_computation | async-start | bytes 2097152 | tf_op jit(solution)/shard_map/all_to_all | solution.py:189
  156.9 4.3 gather_fusion.4
  161.2 4.3 gather_fusion.6
  165.6 6.0 %broadcast_select_fusion = (bf16[32,64,768]{2,1,0:T(8,128)(2,1)}, bf16[32,64,768]{2,1,0:T(8,128)(2,1)}) fusion(bf16[32,64,768]{2,1,0:T(8,128)(2,1)} %gather_fusion.6, pred[32]{0:T(512)(128)(4,1)S(1)} %fusion.48, bf16[32,64,768]{2,1,0:T(8,128)(2,1)} %gather_fusion.4), kind=kLoop, calls=%fused_computation.14 | loop fusion | flops 3145728 | bytes 12582944 | tf_op jit(solution)/shard_map/jit(_where)/select_n | solution.py:76
  171.6 2.4 all-to-all-done
  174.0 5.1 %all-to-all-start.1 = ((bf16[32,64,768]{2,1,0:T(8,128)(2,1)}), bf16[32,64,768]{2,1,0:T(8,128)(2,1)}, u32[]{:S(2)}, u32[]{:S(2)}) async-start(bf16[32,64,768]{2,1,0:T(8,128)(2,1)} %get-tuple-element.36), calls=%async_computation.1 | async-start | bytes 6291456 | tf_op jit(solution)/shard_map/all_to_all | solution.py:78
  179.2 1.9 slice.134
  182.4 1.8 reshape.381
  190.6 45.0 %all_gather.3 = bf16[4,64,8,96]{3,2,0,1:T(8,128)(2,1)S(1)} all-gather(bf16[4,2,8,96]{3,2,0,1:T(8,128)(2,1)S(1)} %copy.207), channel_id=1, replica_groups=mesh['pages'=32,'mp'=4] {'pages'}, dimensions={1}, use_global_device_ids=true | all-gather | bytes 405504 | tf_op jit(solution)/shard_map/all_gather | solution.py:216
  237.2 5.5 %all-to-all-start.2 = ((bf16[32,64,768]{2,1,0:T(8,128)(2,1)}), bf16[32,64,768]{2,1,0:T(8,128)(2,1)}, u32[]{:S(2)}, u32[]{:S(2)}) async-start(bf16[32,64,768]{2,1,0:T(8,128)(2,1)} %get-tuple-element.35), calls=%async_computation.2 | async-start | bytes 6291456 | tf_op jit(solution)/shard_map/all_to_all | solution.py:79
  242.7 35.6 %all-reduce.7.cloned.1.call-done = f32[256,96]{0,1:T(8,128)} async-done(((f32[256,96]{0,1:T(8,128)}), f32[256,96]{0,1:T(8,128)}) %all-reduce.7.cloned.1.call-update) | async-done | bytes 98320 | tf_op jit(solution)/shard_map/psum | solution.py:63
  280.0 2.2 copy.230
  282.4 4.5 pad_maximum_fusion
  287.3 4.3 gather_fusion.5
  291.7 4.3 gather_fusion.7
  296.0 102.5 %all-reduce.9.cloned.1.call-done = f32[256,4097]{1,0:T(8,128)} async-done(((f32[256,4097]{1,0:T(8,128)}), f32[256,4097]{1,0:T(8,128)}) %all-reduce.9.cloned.1.call-update) | async-done | bytes 4195344 | tf_op jit(solution)/shard_map/psum | solution.py:57
  398.5 4.6 slice.101
  403.1 6.6 %reshape.308 = f32[256,2,2048]{2,1,0:T(2,128)} reshape(f32[256,4096]{1,0:T(8,128)} %slice.101) | data formatting | bytes 8388608 | tf_op jit(solution)/shard_map/reshape | solution.py:58
  409.7 7.8 %fusion.67 = (f32[256,1,2048]{2,1,0:T(1,128)S(1)}, f32[256,1,2048]{2,1,0:T(1,128)S(1)}) fusion(f32[256,2,2048]{2,1,0:T(2,128)} %reshape.308), kind=kLoop, calls=%fused_computation.137 | loop fusion | bytes 8388608 | tf_op jit(solution)/shard_map/slice | solution.py:167
  418.5 2.2 fusion.20
  420.8 8.1 %broadcast_select_fusion.2 = (bf16[32,64,768]{2,1,0:T(8,128)(2,1)}, bf16[32,64,768]{2,1,0:T(8,128)(2,1)}) fusion(bf16[32,64,768]{2,1,0:T(8,128)(2,1)} %gather_fusion.7, bf16[32,64,768]{2,1,0:T(8,128)(2,1)} %param.20, pred[32]{0:T(512)(128)(4,1)S(1)} %fusion.49, bf16[32,64,768]{2,1,0:T(8,128)(2,1)} %gather_fusion.5, bf16[32,64,768]{2,1,0:T(8,128)(2,1)} %param.19), kind=kLoop, calls=%fused_computation.16 | loop fusion | flops 3145728 | bytes 18874400 | tf_op jit(solution)/shard_map/jit(_where)/select_n | solution.py:88
  428.9 33.4 %all-reduce.11.cloned.1.call-done = f32[256,96]{0,1:T(8,128)} async-done(((f32[256,96]{0,1:T(8,128)}), f32[256,96]{0,1:T(8,128)}) %all-reduce.11.cloned.1.call-update) | async-done | bytes 98320 | tf_op jit(solution)/shard_map/psum | solution.py:63
  (111 shorter events, 32.8 us)
Async XLA Ops:
  7.2 272.1 %copy-start = (bf16[2,96,2048]{2,1,0:T(8,128)(2,1)S(1)}, bf16[2,96,2048]{2,1,0:T(8,128)(2,1)}, u32[]{:S(2)}) copy-start(bf16[2,96,2048]{2,1,0:T(8,128)(2,1)} %param.17) | copy-start | bytes 2359300
  7.2 115.7 %all-reduce.5.cloned.1.call-start = ((), (), s32[]{:S(2)}) async-start(), calls=%async_computation.3 | async-start | bytes 4980736 | tf_op jit(solution)/shard_map/psum | solution.py:57
  10.6 2.5 copy-start.2
  24.7 9.0 %copy-start.8 = (s32[31]{0:T(128)S(1)}, s32[31]{0:T(128)}, u32[]{:S(2)}) copy-start(s32[31]{0:T(128)} %param.25) | copy-start | bytes 376
  129.4 1.5 copy-start.3
  131.2 5.5 %copy-start.4 = (bf16[256,8,96]{2,1,0:T(8,128)(2,1)}, bf16[256,8,96]{2,1,0:T(8,128)(2,1)S(1)}, u32[]{:S(2)}) copy-start(bf16[256,8,96]{2,1,0:T(8,128)(2,1)S(1)} %copy.174) | copy-start | bytes 1179652
  148.2 8.6 %copy-start.7 = (s32[32]{0:T(128)S(1)}, s32[32]{0:T(128)}, u32[]{:S(2)}) copy-start(s32[32]{0:T(128)} %get-tuple-element.7) | copy-start | bytes 388
  151.1 23.0 %all-to-all-start = ((f32[32,4,2,8,98]{4,3,2,1,0:T(8,128)}), f32[32,4,2,8,98]{4,3,2,1,0:T(8,128)S(1)}, u32[]{:S(2)}, u32[]{:S(2)}) async-start(f32[32,4,2,8,98]{4,3,2,1,0:T(8,128)} %maximum_bitcast_fusion), calls=%async_computation | async-start | bytes 2097152 | tf_op jit(solution)/shard_map/all_to_all | solution.py:189
  174.0 63.1 %all-to-all-start.1 = ((bf16[32,64,768]{2,1,0:T(8,128)(2,1)}), bf16[32,64,768]{2,1,0:T(8,128)(2,1)}, u32[]{:S(2)}, u32[]{:S(2)}) async-start(bf16[32,64,768]{2,1,0:T(8,128)(2,1)} %get-tuple-element.36), calls=%async_computation.1 | async-start | bytes 6291456 | tf_op jit(solution)/shard_map/all_to_all | solution.py:78
  179.1 99.2 %all-reduce.7.cloned.1.call-start = ((), (), s32[]{:S(2)}) async-start(), calls=%async_computation.4 | async-start | bytes 196608 | tf_op jit(solution)/shard_map/psum | solution.py:63
  186.9 49.2 %copy-start.6 = (bf16[96,768]{1,0:T(8,128)(2,1)S(1)}, bf16[96,768]{1,0:T(8,128)(2,1)}, u32[]{:S(2)}) copy-start(bf16[96,768]{1,0:T(8,128)(2,1)} %param.16) | copy-start | bytes 442372
  188.7 48.3 %copy-start.5 = (bf16[4,64,96]{2,1,0:T(8,128)(2,1)S(1)}, bf16[4,64,96]{2,1,0:T(8,128)(2,1)}, u32[]{:S(2)}) copy-start(bf16[4,64,96]{2,1,0:T(8,128)(2,1)} %param.13) | copy-start | bytes 147460
  237.2 54.5 %all-to-all-start.2 = ((bf16[32,64,768]{2,1,0:T(8,128)(2,1)}), bf16[32,64,768]{2,1,0:T(8,128)(2,1)}, u32[]{:S(2)}, u32[]{:S(2)}) async-start(bf16[32,64,768]{2,1,0:T(8,128)(2,1)} %get-tuple-element.35), calls=%async_computation.2 | async-start | bytes 6291456 | tf_op jit(solution)/shard_map/all_to_all | solution.py:79
  242.7 155.8 %all-reduce.9.cloned.1.call-start = ((), (), s32[]{:S(2)}) async-start(), calls=%async_computation.5 | async-start | bytes 8650752 | tf_op jit(solution)/shard_map/psum | solution.py:57
  286.9 175.4 %all-reduce.11.cloned.1.call-start = ((), (), s32[]{:S(2)}) async-start(), calls=%async_computation.6 | async-start | bytes 196608 | tf_op jit(solution)/shard_map/psum | solution.py:63
  409.7 8.8 %copy-start.9 = (bf16[96,2048]{1,0:T(8,128)(2,1)S(1)}, bf16[96,2048]{1,0:T(8,128)(2,1)}, u32[]{:S(2)}) copy-start(bf16[96,2048]{1,0:T(8,128)(2,1)} %param.18) | copy-start | bytes 1179652
  420.8 43.2 %copy-start.1 = (bf16[2,96,2048]{2,1,0:T(8,128)(2,1)S(1)}, bf16[2,96,2048]{2,1,0:T(8,128)(2,1)}, u32[]{:S(2)}) copy-start(bf16[2,96,2048]{2,1,0:T(8,128)(2,1)} %param.17) | copy-start | bytes 2359300
Sparse Core Ops, SparseCore 0:
  12.4 110.4 all-reduce.4
  237.2 41.0 all-reduce.6
  287.1 111.3 all-reduce.8
  420.9 41.3 all-reduce.10

commit v2 on v1

--- a/solution.py
+++ b/solution.py
@@ -59,8 +59,14 @@
     return finish(total, packed[:, -1], 0)
 
 
+def gather_blocks(block, axis):
+    count = lax.axis_size(axis)
+    spread = jnp.broadcast_to(block[None], (count,) + block.shape)
+    return lax.all_to_all(spread, axis, split_axis=0, concat_axis=0, tiled=True)
+
+
 def across_heads(term):
-    return lax.psum(term, "mp")
+    return jnp.sum(gather_blocks(term, "mp"), axis=0)
 
 
 def migrate_pool(key_local, value_local, move_slot, move_offset):
@@ -213,7 +219,7 @@
         preferred_element_type=jnp.float32,
     )
     attended_mine = (accums / totals[..., None]).astype(jnp.bfloat16)
-    attended = lax.all_gather(attended_mine, "pages", axis=1, tiled=True).reshape(
+    attended = jnp.moveaxis(gather_blocks(attended_mine, "pages"), 0, 1).reshape(
         row_count, heads_here * HEAD_DIM
     )
     mixed = activ + across_heads(

time: 472 us -> 487 us (1.032)
  blocking collectives: 45 us -> 0 us
  local copies, waits for them, and re-layouts: 84 us -> 118 us
  other arithmetic: 34.6 us -> 57.3 us
  waiting for transfers between devices: 262 us -> 245 us
  starting transfers between devices: 16.7 us -> 31.1 us
  matrix products: 13.8 us -> 18.8 us
    psum x2 -> x0, waiting for transfers between devices: 69 us -> none  [across_heads(): return lax.psum(term, 'mp')]
    all_gather x1 -> x0, blocking collectives: 45 us -> none  [shards(): lax.all_gather(attended_mine, 'pages', axis=1, tiled=True)]
    all_to_all x1, waiting for transfers between devices: 0.01 us -> 34.9 us  [migrate_pool(): lax.all_to_all(value_send, 'pages', split_axis=0, concat_axis=0, tiled=True)]
    all_to_all x1, waiting for transfers between devices: 0.01 us -> 34.2 us  [migrate_pool(): lax.all_to_all(key_send, 'pages', split_axis=0, concat_axis=0, tiled=True)]
    psum x2, waiting for transfers between devices: 191 us -> 167 us  [reduce_rows(): packed = lax.psum(packed, 'pages')]
    all_to_all x0 -> x3, starting transfers between devices: none -> 15.1 us  [gather_blocks(): return lax.all_to_all(spread, axis, split_axis=0, concat_axis=0, tiled=True)]
    all_to_all x0 -> x3, waiting for transfers between devices: none -> 7.75 us  [gather_blocks(): return lax.all_to_all(spread, axis, split_axis=0, concat_axis=0, tiled=True)]
  transfers between devices with their start and end apart: 7 -> 8, of which waited for: 5 -> 8; matrix products, arithmetic and copies ran while one was open for 16% -> 17% of each run, Pallas kernels for 0% -> 0%
where the time goes in v2:
time: 487 us; the launch traced here: 484 us
  waiting for transfers between devices  245 us (50%)
  local copies, waits for them, and re-layouts  118 us (24%)
  other arithmetic  57.3 us (12%)
  starting transfers between devices  31.1 us (6%)
  matrix products  18.8 us (4%)
  between operations  14.4 us (3%)
    psum x2, waiting for transfers between devices, reduce_rows(): packed = lax.psum(packed, 'pages')  167 us
    all_to_all x1, waiting for transfers between devices, migrate_pool(): lax.all_to_all(value_send, 'pages', split_axis=0, concat_axis=0, tiled=True)  34.9 us
    all_to_all x1, waiting for transfers between devices, migrate_pool(): lax.all_to_all(key_send, 'pages', split_axis=0, concat_axis=0, tiled=True)  34.2 us
    all_to_all x3, starting transfers between devices, gather_blocks(): return lax.all_to_all(spread, axis, split_axis=0, concat_axis=0, tiled=True)  15.1 us
    slice x3, local copies, waits for them, and re-layouts, reduce_rows(): total = packed[:, :-1].reshape(partial_value.shape)  10.9 us
  transfers between devices with their start and end apart: 8, of which 8 were waited for; matrix products, arithmetic and copies ran while one was open for 17% of the time, Pallas kernels for 0%

profile of v2, /device:TPU:0, one launch (start us, length us, event | category | flops | bytes accessed | tf_op | source)
XLA Modules:
  0.0 484.1 jit_solution(12781383139195260204)
XLA Ops:
  19.8 5.4 %reshape.314 = bf16[32,64,8,96]{3,2,1,0:T(8,128)(2,1)} reshape(bf16[32,64,768]{2,1,0:T(8,128)(2,1)S(1)} %copy-done.2) | data formatting | bytes 6291456 | tf_op jit(solution)/shard_map/reshape | solution.py:108
  25.2 8.3 %reshape.315 = bf16[32,64,8,96]{3,2,1,0:T(8,128)(2,1)} reshape(bf16[32,64,768]{2,1,0:T(8,128)(2,1)} %param.20) | data formatting | bytes 6291456 | tf_op jit(solution)/shard_map/reshape | solution.py:109
  39.0 84.4 %all-reduce.3.cloned.1.call-done = f32[256,2305]{1,0:T(8,128)} async-done(((f32[256,2305]{1,0:T(8,128)}), f32[256,2305]{1,0:T(8,128)}) %all-reduce.3.cloned.1.call-update) | async-done | bytes 2360336 | tf_op jit(solution)/shard_map/psum | solution.py:57
  123.4 3.2 slice.89
  126.6 3.0 copy.211
  138.8 6.0 %fusion.69 = (f32[4,32,8]{0,2,1:T(8,128)}, f32[4,32,8,64]{3,0,2,1:T(4,128)}) fusion(bf16[32,64,8,96]{3,2,1,0:T(8,128)(2,1)} %reshape.314, bf16[4,32,8,96]{3,2,0,1:T(8,128)(2,1)} %bitcast.128, pred[32,64]{1,0:T(8,128)(4,1)S(1)} %fusion.49), kind=kOutput, calls=%fused_computation.140 | convolution fusion | flops 12778496 | bytes 3610624 | tf_op jit(solution)/shard_map/tshd,skhd->tshk/dot_general | solution.py:111
  155.6 3.7 fusion.7
  165.7 3.4 copy.224
  169.1 3.4 copy.225
  172.5 3.5 maximum_bitcast_fusion
  176.0 5.9 %all-to-all-start = ((f32[32,4,2,8,98]{4,3,2,1,0:T(8,128)}), f32[32,4,2,8,98]{4,3,2,1,0:T(8,128)}, u32[]{:S(2)}, u32[]{:S(2)}) async-start(f32[32,4,2,8,98]{4,3,2,1,0:T(8,128)} %maximum_bitcast_fusion), calls=%async_computation | async-start | bytes 2097152 | tf_op jit(solution)/shard_map/all_to_all | solution.py:195
  189.5 2.5 reshape.387
  192.0 2.5 constant_dynamic-slice_fusion.1
  198.9 4.0 fusion.68
  219.1 6.3 %all-to-all-start.1 = ((bf16[32,4,2,8,96]{4,3,2,1,0:T(8,128)(2,1)}), bf16[32,4,2,8,96]{4,3,2,1,0:T(8,128)(2,1)}, u32[]{:S(2)}, u32[]{:S(2)}) async-start(bf16[32,4,2,8,96]{4,3,2,1,0:T(8,128)(2,1)} %broadcast_in_dim.183), calls=%async_computation.1 | async-start | bytes 1048576 | tf_op jit(solution)/shard_map/all_to_all | solution.py:65
  228.4 4.3 gather_fusion.6
  232.8 4.1 all-to-all-done.1
  243.2 4.4 all-to-all-start.2
  247.6 6.0 %broadcast_select_fusion = (bf16[32,64,768]{2,1,0:T(8,128)(2,1)}, bf16[32,64,768]{2,1,0:T(8,128)(2,1)}) fusion(bf16[32,64,768]{2,1,0:T(8,128)(2,1)} %gather_fusion.6, pred[32]{0:T(512)(128)(4,1)S(1)} %fusion.47, bf16[32,64,768]{2,1,0:T(8,128)(2,1)} %gather_fusion.4), kind=kLoop, calls=%fused_computation.13 | loop fusion | flops 3145728 | bytes 12582944 | tf_op jit(solution)/shard_map/jit(_where)/select_n | solution.py:82
  253.6 2.4 all-to-all-done.2
  256.1 5.0 %all-to-all-start.4 = ((bf16[32,64,768]{2,1,0:T(8,128)(2,1)}), bf16[32,64,768]{2,1,0:T(8,128)(2,1)}, u32[]{:S(2)}, u32[]{:S(2)}) async-start(bf16[32,64,768]{2,1,0:T(8,128)(2,1)} %get-tuple-element.33), calls=%async_computation.4 | async-start | bytes 6291456 | tf_op jit(solution)/shard_map/all_to_all | solution.py:84
  268.8 34.2 %all-to-all-done.4 = bf16[32,64,768]{2,1,0:T(8,128)(2,1)} async-done(((bf16[32,64,768]{2,1,0:T(8,128)(2,1)}), bf16[32,64,768]{2,1,0:T(8,128)(2,1)}, u32[]{:S(2)}, u32[]{:S(2)}) %all-to-all-start.4) | async-done | bytes 3145760 | tf_op jit(solution)/shard_map/all_to_all | solution.py:84
  303.0 4.8 all-to-all-start.5
  313.1 4.3 gather_fusion.5
  317.4 34.9 %all-to-all-done.5 = bf16[32,64,768]{2,1,0:T(8,128)(2,1)} async-done(((bf16[32,64,768]{2,1,0:T(8,128)(2,1)}), bf16[32,64,768]{2,1,0:T(8,128)(2,1)}, u32[]{:S(2)}, u32[]{:S(2)}) %all-to-all-start.5) | async-done | bytes 3145760 | tf_op jit(solution)/shard_map/all_to_all | solution.py:85
  352.4 4.3 gather_fusion.7
  356.7 82.8 %all-reduce.5.cloned.1.call-done = f32[256,4097]{1,0:T(8,128)} async-done(((f32[256,4097]{1,0:T(8,128)}), f32[256,4097]{1,0:T(8,128)}) %all-reduce.5.cloned.1.call-update) | async-done | bytes 4195344 | tf_op jit(solution)/shard_map/psum | solution.py:57
  439.4 4.6 slice.101
  444.1 6.6 %reshape.317 = f32[256,2,2048]{2,1,0:T(2,128)} reshape(f32[256,4096]{1,0:T(8,128)} %slice.101) | data formatting | bytes 8388608 | tf_op jit(solution)/shard_map/reshape | solution.py:58
  450.7 7.8 %fusion.66 = (f32[256,1,2048]{2,1,0:T(1,128)S(1)}, f32[256,1,2048]{2,1,0:T(1,128)S(1)}) fusion(f32[256,2,2048]{2,1,0:T(2,128)} %reshape.317), kind=kLoop, calls=%fused_computation.137 | loop fusion | bytes 8388608 | tf_op jit(solution)/shard_map/slice | solution.py:173
  461.8 4.4 all-to-all-start.3
  466.2 7.1 %broadcast_select_fusion.2 = (bf16[32,64,768]{2,1,0:T(8,128)(2,1)}, bf16[32,64,768]{2,1,0:T(8,128)(2,1)}) fusion(bf16[32,64,768]{2,1,0:T(8,128)(2,1)} %gather_fusion.7, bf16[32,64,768]{2,1,0:T(8,128)(2,1)} %param.20, pred[32]{0:T(512)(128)(4,1)S(1)} %fusion.48, bf16[32,64,768]{2,1,0:T(8,128)(2,1)} %gather_fusion.5, bf16[32,64,768]{2,1,0:T(8,128)(2,1)S(1)} %copy-done.2), kind=kLoop, calls=%fused_computation.15 | loop fusion | flops 3145728 | bytes 18874400 | tf_op jit(solution)/shard_map/jit(_where)/select_n | solution.py:94
  (130 shorter events, 102.2 us)
Async XLA Ops:
  7.2 452.3 %copy-start = (bf16[96,2048]{1,0:T(8,128)(2,1)S(1)}, bf16[96,2048]{1,0:T(8,128)(2,1)}, u32[]{:S(2)}) copy-start(bf16[96,2048]{1,0:T(8,128)(2,1)} %param.18) | copy-start | bytes 1179652
  7.2 116.2 %all-reduce.3.cloned.1.call-start = ((), (), s32[]{:S(2)}) async-start(), calls=%async_computation.6 | async-start | bytes 4980736 | tf_op jit(solution)/shard_map/psum | solution.py:57
  11.1 3.8 copy-start.1
  12.7 7.1 %copy-start.2 = (bf16[32,64,768]{2,1,0:T(8,128)(2,1)S(1)}, bf16[32,64,768]{2,1,0:T(8,128)(2,1)}, u32[]{:S(2)}) copy-start(bf16[32,64,768]{2,1,0:T(8,128)(2,1)} %param.19) | copy-start | bytes 9437188
  14.9 21.2 %copy-start.9 = (s32[32]{0:T(128)}, s32[32]{0:T(128)S(1)}, u32[]{:S(2)}) copy-start(s32[32]{0:T(128)S(1)} %get-tuple-element.6) | copy-start | bytes 388
  14.9 121.5 %copy-start.8 = (s32[1024]{0:T(1024)}, s32[1024]{0:T(1024)S(1)}, u32[]{:S(2)}) copy-start(s32[1024]{0:T(1024)S(1)} %pad_clamp_fusion.3) | copy-start | bytes 12292
  25.2 10.9 %copy-start.11 = (s32[256]{0:T(256)S(1)}, s32[256]{0:T(256)}, u32[]{:S(2)}) copy-start(s32[256]{0:T(256)} %gather_fusion.1) | copy-start | bytes 3076
  34.2 2.6 copy-start.15
  34.8 0.5 copy-start.13
  37.4 101.3 %copy-start.7 = (pred[32,64]{1,0:T(8,128)(4,1)}, pred[32,64]{1,0:T(8,128)(4,1)S(1)}, u32[]{:S(2)}) copy-start(pred[32,64]{1,0:T(8,128)(4,1)S(1)} %fusion.49) | copy-start | bytes 6148
  130.6 2.0 copy-start.5
  130.7 2.0 copy-start.6
  132.5 1.7 copy-start.3
  153.1 6.1 %copy-start.10 = (s32[32]{0:T(128)S(1)}, s32[32]{0:T(128)}, u32[]{:S(2)}) copy-start(s32[32]{0:T(128)} %copy-done.9) | copy-start | bytes 388
  176.0 22.9 %all-to-all-start = ((f32[32,4,2,8,98]{4,3,2,1,0:T(8,128)}), f32[32,4,2,8,98]{4,3,2,1,0:T(8,128)}, u32[]{:S(2)}, u32[]{:S(2)}) async-start(f32[32,4,2,8,98]{4,3,2,1,0:T(8,128)} %maximum_bitcast_fusion), calls=%async_computation | async-start | bytes 2097152 | tf_op jit(solution)/shard_map/all_to_all | solution.py:195
  219.1 17.8 %all-to-all-start.1 = ((bf16[32,4,2,8,96]{4,3,2,1,0:T(8,128)(2,1)}), bf16[32,4,2,8,96]{4,3,2,1,0:T(8,128)(2,1)}, u32[]{:S(2)}, u32[]{:S(2)}) async-start(bf16[32,4,2,8,96]{4,3,2,1,0:T(8,128)(2,1)} %broadcast_in_dim.183), calls=%async_computation.1 | async-start | bytes 1048576 | tf_op jit(solution)/shard_map/all_to_all | solution.py:65
  228.4 4.3 copy-start.14
  243.2 12.9 %all-to-all-start.2 = ((f32[4,256,96]{1,2,0:T(8,128)}), f32[4,256,96]{1,2,0:T(8,128)}, u32[]{:S(2)}, u32[]{:S(2)}) async-start(f32[4,256,96]{1,2,0:T(8,128)} %broadcast_in_dim.184), calls=%async_computation.2 | async-start | bytes 786432 | tf_op jit(solution)/shard_map/all_to_all | solution.py:65
  256.0 10.3 %copy-start.12 = (f32[96]{0:T(128)S(1)}, f32[96]{0:T(128)}, u32[]{:S(2)}) copy-start(f32[96]{0:T(128)} %get-tuple-element.28) | copy-start | bytes 1156
  256.1 47.0 %all-to-all-start.4 = ((bf16[32,64,768]{2,1,0:T(8,128)(2,1)}), bf16[32,64,768]{2,1,0:T(8,128)(2,1)}, u32[]{:S(2)}, u32[]{:S(2)}) async-start(bf16[32,64,768]{2,1,0:T(8,128)(2,1)} %get-tuple-element.33), calls=%async_computation.4 | async-start | bytes 6291456 | tf_op jit(solution)/shard_map/all_to_all | solution.py:84
  303.0 49.4 %all-to-all-start.5 = ((bf16[32,64,768]{2,1,0:T(8,128)(2,1)}), bf16[32,64,768]{2,1,0:T(8,128)(2,1)}, u32[]{:S(2)}, u32[]{:S(2)}) async-start(bf16[32,64,768]{2,1,0:T(8,128)(2,1)} %get-tuple-element.32), calls=%async_computation.5 | async-start | bytes 6291456 | tf_op jit(solution)/shard_map/all_to_all | solution.py:85
  307.8 131.6 %all-reduce.5.cloned.1.call-start = ((), (), s32[]{:S(2)}) async-start(), calls=%async_computation.7 | async-start | bytes 8650752 | tf_op jit(solution)/shard_map/psum | solution.py:57
  308.1 1.9 copy-start.4
  312.3 0.7 copy-start.17
  312.3 0.7 copy-start.16
  461.8 12.7 %all-to-all-start.3 = ((f32[4,256,96]{1,2,0:T(8,128)}), f32[4,256,96]{1,2,0:T(8,128)}, u32[]{:S(2)}, u32[]{:S(2)}) async-start(f32[4,256,96]{1,2,0:T(8,128)} %broadcast_in_dim.186), calls=%async_computation.3 | async-start | bytes 786432 | tf_op jit(solution)/shard_map/all_to_all | solution.py:65
Sparse Core Ops, SparseCore 0:
  12.9 110.4 all-reduce.2
  312.5 126.9 all-reduce.4

commit v3 on v2

--- a/solution.py
+++ b/solution.py
@@ -51,10 +51,13 @@
     )
 
 
-def reduce_rows(partial_value, squares, finish):
+def reduce_rows(partial_value, squares, finish, tied=()):
     rows = partial_value.shape[0]
     packed = jnp.concatenate([partial_value.reshape(rows, -1), squares[:, None]], axis=1)
     packed = lax.psum(packed, "pages")
+    if tied:
+        packed, tied = lax.optimization_barrier((packed, tied))
+        return finish(packed[:, :-1].reshape(partial_value.shape), packed[:, -1], 0), tied
     total = packed[:, :-1].reshape(partial_value.shape)
     return finish(total, packed[:, -1], 0)
 
@@ -80,10 +83,16 @@
     sending = jnp.any(aimed, axis=1)[:, None, None]
     key_send = jnp.where(sending, key_local[chosen], jnp.zeros((), key_local.dtype))
     value_send = jnp.where(sending, value_local[chosen], jnp.zeros((), value_local.dtype))
-    key_recv, value_recv = (
-        lax.all_to_all(key_send, "pages", split_axis=0, concat_axis=0, tiled=True),
-        lax.all_to_all(value_send, "pages", split_axis=0, concat_axis=0, tiled=True),
-    )
+    both = lax.all_to_all(
+        jnp.stack([key_send, value_send], axis=1), "pages", split_axis=0, concat_axis=0, tiled=True
+    )
+    return both[:, 0], both[:, 1]
+
+
+def land_pool(key_local, value_local, key_recv, value_recv, move_slot, move_offset):
+    holders = lax.axis_size("pages")
+    myself = lax.axis_index("pages")
+    mine = lax.dynamic_index_in_dim(move_slot, myself, 0, keepdims=False)
     sources = (myself - move_offset) % holders
     slot_ids = jnp.arange(key_local.shape[0], dtype=jnp.int32)
     landing = slot_ids[:, None] == mine[None, :]
@@ -177,7 +186,10 @@
     normed_one = (activ * norm_gains[0]).astype(jnp.bfloat16)
     partial_one = jnp.einsum("bd,dcn->bcn", normed_one, w_qkv, preferred_element_type=jnp.float32)
     squares_one = jnp.sum(activ * activ, axis=1)
-    query_all, key_all, value_all = reduce_rows(partial_one, squares_one, finish_qkv)
+    received = migrate_pool(k_cache, v_cache, move_slot, move_offset)
+    (query_all, key_all, value_all), received = reduce_rows(
+        partial_one, squares_one, finish_qkv, received
+    )
     heads_here = query_all.shape[1] // HEAD_DIM
     queries = query_all.reshape(step_count, req_count, heads_here, HEAD_DIM)
     key_fresh = key_all.reshape(step_count, req_count, heads_here, HEAD_DIM)
@@ -235,7 +247,7 @@
         lax.dot_general(hidden, w_down, CONTRACT_LAST, preferred_element_type=jnp.float32)
     )
     layer_out = (mixed + feed).astype(jnp.bfloat16).reshape(step_count, req_count, width_here)
-    new_k_cache, new_v_cache = migrate_pool(k_cache, v_cache, move_slot, move_offset)
+    new_k_cache, new_v_cache = land_pool(k_cache, v_cache, *received, move_slot, move_offset)
     return (layer_out, new_k_cache, new_v_cache)
 
 

time: 487 us -> 486 us (level)
  blocking collectives: 0 us -> 17.7 us
  waiting for transfers between devices: 245 us -> 230 us
  starting transfers between devices: 31.1 us -> 22.5 us
    all_to_all x2 -> x1, waiting for transfers between devices: 69.1 us -> 51.2 us  [migrate_pool(): lax.all_to_all(jnp.stack([key_send, value_send], axis=1), 'pages', split_...]
    all_to_all x0 -> x1, blocking collectives: none -> 17.7 us  [gather_blocks(): return lax.all_to_all(spread, axis, split_axis=0, concat_axis=0, tiled=True)]
    squeeze x0 -> x1, local copies, waits for them, and re-layouts: none -> 6.33 us  [migrate_pool(): return (both[:, 0], both[:, 1])]
    slice x3 -> x1, local copies, waits for them, and re-layouts: 10.9 us -> 4.63 us  [reduce_rows(): total = packed[:, :-1].reshape(partial_value.shape)]
    slice x0 -> x2, local copies, waits for them, and re-layouts: none -> 6.26 us  [reduce_rows(): packed[:, :-1].reshape(partial_value.shape)]
    all_to_all x3 -> x2, starting transfers between devices: 15.1 us -> 8.84 us  [gather_blocks(): return lax.all_to_all(spread, axis, split_axis=0, concat_axis=0, tiled=True)]
    all_to_all x2 -> x1, starting transfers between devices: 9.76 us -> 7.68 us  [migrate_pool(): lax.all_to_all(jnp.stack([key_send, value_send], axis=1), 'pages', split_...]
  transfers between devices with their start and end apart: 8 -> 6, of which waited for: 8 -> 6; matrix products, arithmetic and copies ran while one was open for 17% -> 15% of each run, Pallas kernels for 0% -> 0%
where the time goes in v3:
time: 486 us; the launch traced here: 483 us
  waiting for transfers between devices  230 us (47%)
  local copies, waits for them, and re-layouts  121 us (25%)
  other arithmetic  57.9 us (12%)
  starting transfers between devices  22.5 us (5%)
  matrix products  19.8 us (4%)
  blocking collectives  17.7 us (4%)
  between operations  14.4 us (3%)
    psum x2, waiting for transfers between devices, reduce_rows(): packed = lax.psum(packed, 'pages')  170 us
    all_to_all x1, waiting for transfers between devices, migrate_pool(): lax.all_to_all(jnp.stack([key_send, value_send], axis=1), 'pages', split_...  51.2 us
    all_to_all x1, blocking collectives, gather_blocks(): return lax.all_to_all(spread, axis, split_axis=0, concat_axis=0, tiled=True)  17.7 us
  transfers between devices with their start and end apart: 6, of which 6 were waited for; matrix products, arithmetic and copies ran while one was open for 15% of the time, Pallas kernels for 0%

profile of v3, /device:TPU:0, one launch (start us, length us, event | category | flops | bytes accessed | tf_op | source)
XLA Modules:
  0.0 483.5 jit_solution(16888025645534281078)
XLA Ops:
  9.4 4.5 gather_fusion.2
  16.3 3.3 bitcast_select_fusion.1
  19.6 3.2 pad_maximum_fusion
  22.9 7.7 %all-to-all-start = ((bf16[32,2,64,768]{3,2,1,0:T(8,128)(2,1)}), bf16[32,2,64,768]{3,2,1,0:T(8,128)(2,1)}, u32[]{:S(2)}, u32[]{:S(2)}) async-start(bf16[32,2,64,768]{3,2,1,0:T(8,128)(2,1)} %pad_maximum_fusion), calls=%async_computation | async-start | bytes 12582912 | tf_op jit(solution)/shard_map/all_to_all | solution.py:86
  37.6 2.4 gather_fusion.3
  43.8 5.4 %reshape.328 = bf16[32,64,8,96]{3,2,1,0:T(8,128)(2,1)} reshape(bf16[32,64,768]{2,1,0:T(8,128)(2,1)S(1)} %copy-done.2) | data formatting | bytes 6291456 | tf_op jit(solution)/shard_map/reshape | solution.py:117
  49.2 8.2 %reshape.329 = bf16[32,64,8,96]{3,2,1,0:T(8,128)(2,1)} reshape(bf16[32,64,768]{2,1,0:T(8,128)(2,1)} %param.20) | data formatting | bytes 6291456 | tf_op jit(solution)/shard_map/reshape | solution.py:118
  61.6 51.2 %all-to-all-done = bf16[32,2,64,768]{3,2,1,0:T(8,128)(2,1)} async-done(((bf16[32,2,64,768]{3,2,1,0:T(8,128)(2,1)}), bf16[32,2,64,768]{3,2,1,0:T(8,128)(2,1)}, u32[]{:S(2)}, u32[]{:S(2)}) %all-to-all-start) | async-done | bytes 6291488 | tf_op jit(solution)/shard_map/all_to_all | solution.py:86
  112.9 6.3 %slice_bitcast_fusion = (bf16[32,64,768]{2,1,0:T(8,128)(2,1)}, bf16[32,64,768]{2,1,0:T(8,128)(2,1)}) fusion(bf16[32,2,64,768]{3,2,1,0:T(8,128)(2,1)} %all-to-all-done), kind=kLoop, calls=%fused_computation.14 | loop fusion | bytes 12582912 | tf_op jit(solution)/shard_map/squeeze | solution.py:89
  119.2 72.4 %all-reduce.3.cloned.1.call-done = f32[256,2305]{1,0:T(8,128)} async-done(((f32[256,2305]{1,0:T(8,128)}), f32[256,2305]{1,0:T(8,128)}) %all-reduce.3.cloned.1.call-update) | async-done | bytes 2360336 | tf_op jit(solution)/shard_map/psum | solution.py:57
  192.6 3.2 slice.64
  195.8 3.0 copy.221
  206.8 6.0 %fusion.66 = (f32[4,32,8]{0,2,1:T(8,128)}, f32[4,32,8,64]{3,0,2,1:T(4,128)}) fusion(bf16[32,64,8,96]{3,2,1,0:T(8,128)(2,1)} %reshape.328, bf16[4,32,8,96]{3,2,0,1:T(8,128)(2,1)} %bitcast.141, pred[32,64]{1,0:T(8,128)(4,1)S(1)} %fusion.46), kind=kOutput, calls=%fused_computation.140 | convolution fusion | flops 12778496 | bytes 3610624 | tf_op jit(solution)/shard_map/tshd,skhd->tshk/dot_general | solution.py:120
  221.2 2.4 fusion.24
  228.2 3.4 copy.234
  231.7 3.5 copy.235
  235.1 3.7 fusion.7
  242.0 5.9 %all-to-all-start.1 = ((f32[32,4,2,8,98]{4,3,2,1,0:T(8,128)}), f32[32,4,2,8,98]{4,3,2,1,0:T(8,128)}, u32[]{:S(2)}, u32[]{:S(2)}) async-start(f32[32,4,2,8,98]{4,3,2,1,0:T(8,128)} %maximum_bitcast_fusion), calls=%async_computation.1 | async-start | bytes 2097152 | tf_op jit(solution)/shard_map/all_to_all | solution.py:207
  250.4 2.5 reshape.401
  252.9 2.5 constant_dynamic-slice_fusion
  264.9 4.1 fusion.65
  285.6 17.7 %all_to_all.25 = bf16[32,4,2,8,96]{4,3,2,1,0:T(8,128)(2,1)S(1)} all-to-all(bf16[32,4,2,8,96]{4,3,2,1,0:T(8,128)(2,1)S(1)} %broadcast_in_dim.192), channel_id=1, replica_groups=mesh['pages'=32,'mp'=4] {'pages'}, dimensions={0} | all-to-all | bytes 786432 | tf_op jit(solution)/shard_map/all_to_all | solution.py:68
  308.5 4.4 all-to-all-start.3
  315.0 6.4 %all-to-all-done.3 = f32[4,256,96]{1,2,0:T(8,128)} async-done(((f32[4,256,96]{1,2,0:T(8,128)}), f32[4,256,96]{1,2,0:T(8,128)}, u32[]{:S(2)}, u32[]{:S(2)}) %all-to-all-start.3) | async-done | bytes 393248 | tf_op jit(solution)/shard_map/all_to_all | solution.py:68
  332.2 4.3 gather_fusion.6
  336.5 4.3 gather_fusion.7
  340.8 98.0 %all-reduce.5.cloned.1.call-done = f32[256,4097]{1,0:T(8,128)} async-done(((f32[256,4097]{1,0:T(8,128)}), f32[256,4097]{1,0:T(8,128)}) %all-reduce.5.cloned.1.call-update) | async-done | bytes 4195344 | tf_op jit(solution)/shard_map/psum | solution.py:57
  438.8 4.6 slice.109
  443.4 6.6 %reshape.331 = f32[256,2,2048]{2,1,0:T(2,128)} reshape(f32[256,4096]{1,0:T(8,128)} %slice.109) | data formatting | bytes 8388608 | tf_op jit(solution)/shard_map/reshape | solution.py:61
  450.0 7.8 %fusion.63 = (f32[256,1,2048]{2,1,0:T(1,128)S(1)}, f32[256,1,2048]{2,1,0:T(1,128)S(1)}) fusion(f32[256,2,2048]{2,1,0:T(2,128)} %reshape.331), kind=kLoop, calls=%fused_computation.137 | loop fusion | bytes 8388608 | tf_op jit(solution)/shard_map/slice | solution.py:182
  461.2 4.4 all-to-all-start.4
  465.6 7.1 %broadcast_select_fusion = (bf16[32,64,768]{2,1,0:T(8,128)(2,1)}, bf16[32,64,768]{2,1,0:T(8,128)(2,1)}) fusion(bf16[32,64,768]{2,1,0:T(8,128)(2,1)} %gather_fusion.7, bf16[32,64,768]{2,1,0:T(8,128)(2,1)} %param.20, pred[32]{0:T(512)(128)(4,1)S(1)} %fusion.44, bf16[32,64,768]{2,1,0:T(8,128)(2,1)} %gather_fusion.6, bf16[32,64,768]{2,1,0:T(8,128)(2,1)S(1)} %copy-done.2), kind=kLoop, calls=%fused_computation.18 | loop fusion | flops 3145728 | bytes 18874400 | tf_op jit(solution)/shard_map/jit(_where)/select_n | solution.py:103
  (135 shorter events, 98.5 us)
Async XLA Ops:
  7.2 451.7 %copy-start = (bf16[96,2048]{1,0:T(8,128)(2,1)S(1)}, bf16[96,2048]{1,0:T(8,128)(2,1)}, u32[]{:S(2)}) copy-start(bf16[96,2048]{1,0:T(8,128)(2,1)} %param.18) | copy-start | bytes 1179652
  8.7 0.7 copy-start.18
  9.4 4.5 copy-start.2
  22.9 7.7 %copy-start.17 = (f32[2,96]{1,0:T(2,128)S(1)}, f32[2,96]{1,0:T(2,128)}, u32[]{:S(2)}) copy-start(f32[2,96]{1,0:T(2,128)} %param.14) | copy-start | bytes 2308
  22.9 90.0 %all-to-all-start = ((bf16[32,2,64,768]{3,2,1,0:T(8,128)(2,1)}), bf16[32,2,64,768]{3,2,1,0:T(8,128)(2,1)}, u32[]{:S(2)}, u32[]{:S(2)}) async-start(bf16[32,2,64,768]{3,2,1,0:T(8,128)(2,1)} %pad_maximum_fusion), calls=%async_computation | async-start | bytes 12582912 | tf_op jit(solution)/shard_map/all_to_all | solution.py:86
  30.6 161.0 %all-reduce.3.cloned.1.call-start = ((), (), s32[]{:S(2)}) async-start(), calls=%async_computation.5 | async-start | bytes 4980736 | tf_op jit(solution)/shard_map/psum | solution.py:57
  33.4 2.4 copy-start.7
  35.8 1.8 copy-start.1
  41.8 16.8 %copy-start.14 = (s32[32]{0:T(128)}, s32[32]{0:T(128)S(1)}, u32[]{:S(2)}) copy-start(s32[32]{0:T(128)S(1)} %get-tuple-element.12) | copy-start | bytes 388
  41.8 162.6 %copy-start.13 = (s32[1024]{0:T(1024)}, s32[1024]{0:T(1024)S(1)}, u32[]{:S(2)}) copy-start(s32[1024]{0:T(1024)S(1)} %pad_clamp_fusion.3) | copy-start | bytes 12292
  60.1 146.7 %copy-start.11 = (pred[32,64]{1,0:T(8,128)(4,1)}, pred[32,64]{1,0:T(8,128)(4,1)S(1)}, u32[]{:S(2)}) copy-start(pred[32,64]{1,0:T(8,128)(4,1)S(1)} %fusion.46) | copy-start | bytes 6148
  198.8 2.0 copy-start.8
  198.8 2.0 copy-start.9
  200.7 1.6 copy-start.3
  217.2 17.9 %copy-start.12 = (pred[32,64]{1,0:T(8,128)(4,1)S(1)}, pred[32,64]{1,0:T(8,128)(4,1)}, u32[]{:S(2)}) copy-start(pred[32,64]{1,0:T(8,128)(4,1)} %copy-done.11) | copy-start | bytes 6148
  235.1 3.7 copy-start.15
  238.8 1.6 copy-start.4
  238.8 1.6 copy-start.5
  242.0 22.9 %all-to-all-start.1 = ((f32[32,4,2,8,98]{4,3,2,1,0:T(8,128)}), f32[32,4,2,8,98]{4,3,2,1,0:T(8,128)}, u32[]{:S(2)}, u32[]{:S(2)}) async-start(f32[32,4,2,8,98]{4,3,2,1,0:T(8,128)} %maximum_bitcast_fusion), calls=%async_computation.1 | async-start | bytes 2097152 | tf_op jit(solution)/shard_map/all_to_all | solution.py:207
  272.0 1.9 copy-start.10
  303.3 21.4 %copy-start.16 = (f32[96]{0:T(128)S(1)}, f32[96]{0:T(128)}, u32[]{:S(2)}) copy-start(f32[96]{0:T(128)} %get-tuple-element.36) | copy-start | bytes 1156
  308.5 12.9 %all-to-all-start.3 = ((f32[4,256,96]{1,2,0:T(8,128)}), f32[4,256,96]{1,2,0:T(8,128)}, u32[]{:S(2)}, u32[]{:S(2)}) async-start(f32[4,256,96]{1,2,0:T(8,128)} %broadcast_in_dim.193), calls=%async_computation.3 | async-start | bytes 786432 | tf_op jit(solution)/shard_map/all_to_all | solution.py:68
  312.9 125.9 %all-reduce.5.cloned.1.call-start = ((), (), s32[]{:S(2)}) async-start(), calls=%async_computation.6 | async-start | bytes 8650752 | tf_op jit(solution)/shard_map/psum | solution.py:57
  327.1 1.9 copy-start.6
  331.4 0.7 copy-start.20
  331.4 0.7 copy-start.19
  461.2 12.7 %all-to-all-start.4 = ((f32[4,256,96]{1,2,0:T(8,128)}), f32[4,256,96]{1,2,0:T(8,128)}, u32[]{:S(2)}, u32[]{:S(2)}) async-start(f32[4,256,96]{1,2,0:T(8,128)} %broadcast_in_dim.195), calls=%async_computation.4 | async-start | bytes 786432 | tf_op jit(solution)/shard_map/all_to_all | solution.py:68
Sparse Core Ops, SparseCore 0:
  37.7 153.8 all-reduce.2
  331.5 107.2 all-reduce.4

commit v4 on v3

--- a/solution.py
+++ b/solution.py
@@ -51,11 +51,11 @@
     )
 
 
-def reduce_rows(partial_value, squares, finish, tied=()):
+def reduce_rows(partial_value, squares, finish, tied=None):
     rows = partial_value.shape[0]
     packed = jnp.concatenate([partial_value.reshape(rows, -1), squares[:, None]], axis=1)
     packed = lax.psum(packed, "pages")
-    if tied:
+    if tied is not None:
         packed, tied = lax.optimization_barrier((packed, tied))
         return finish(packed[:, :-1].reshape(partial_value.shape), packed[:, -1], 0), tied
     total = packed[:, :-1].reshape(partial_value.shape)
@@ -83,9 +83,11 @@
     sending = jnp.any(aimed, axis=1)[:, None, None]
     key_send = jnp.where(sending, key_local[chosen], jnp.zeros((), key_local.dtype))
     value_send = jnp.where(sending, value_local[chosen], jnp.zeros((), value_local.dtype))
-    both = lax.all_to_all(
-        jnp.stack([key_send, value_send], axis=1), "pages", split_axis=0, concat_axis=0, tiled=True
-    )
+    return jnp.stack([key_send, value_send], axis=1)
+
+
+def exchange_pool(both):
+    both = lax.all_to_all(both, "pages", split_axis=0, concat_axis=0, tiled=True)
     return both[:, 0], both[:, 1]
 
 
@@ -186,9 +188,9 @@
     normed_one = (activ * norm_gains[0]).astype(jnp.bfloat16)
     partial_one = jnp.einsum("bd,dcn->bcn", normed_one, w_qkv, preferred_element_type=jnp.float32)
     squares_one = jnp.sum(activ * activ, axis=1)
-    received = migrate_pool(k_cache, v_cache, move_slot, move_offset)
-    (query_all, key_all, value_all), received = reduce_rows(
-        partial_one, squares_one, finish_qkv, received
+    sending = migrate_pool(k_cache, v_cache, move_slot, move_offset)
+    (query_all, key_all, value_all), sending = reduce_rows(
+        partial_one, squares_one, finish_qkv, sending
     )
     heads_here = query_all.shape[1] // HEAD_DIM
     queries = query_all.reshape(step_count, req_count, heads_here, HEAD_DIM)
@@ -204,6 +206,7 @@
         [cache_acc, cache_total[..., None], cache_top[..., None]], axis=-1
     ).reshape(step_count, holders, group, heads_here, HEAD_DIM + 2)
     packed = jnp.moveaxis(packed, 1, 0)
+    packed, received = lax.optimization_barrier((packed, exchange_pool(sending)))
     packed = lax.all_to_all(packed, "pages", split_axis=0, concat_axis=0, tiled=True)
     part_acc = packed[..., :HEAD_DIM]
     part_total = packed[..., HEAD_DIM]

time: 486 us -> 456 us (0.938)
  waiting for transfers between devices: 230 us -> 207 us
    all_to_all x1, waiting for transfers between devices: 51.2 us -> 4.56 us  [exchange_pool(): lax.all_to_all(both, 'pages', split_axis=0, concat_axis=0, tiled=True)]
    psum x2, waiting for transfers between devices: 170 us -> 193 us  [reduce_rows(): packed = lax.psum(packed, 'pages')]
  transfers between devices with their start and end apart: 6 -> 6, of which waited for: 6 -> 6; matrix products, arithmetic and copies ran while one was open for 15% -> 27% of each run, Pallas kernels for 0% -> 0%
where the time goes in v4:
time: 456 us; the launch traced here: 453 us
  waiting for transfers between devices  207 us (45%)
  local copies, waits for them, and re-layouts  120 us (26%)
  other arithmetic  56.8 us (12%)
  starting transfers between devices  19.5 us (4%)
  matrix products  19 us (4%)
  blocking collectives  17.1 us (4%)
  between operations  14.4 us (3%)
    psum x2, waiting for transfers between devices, reduce_rows(): packed = lax.psum(packed, 'pages')  193 us
    all_to_all x1, blocking collectives, gather_blocks(): return lax.all_to_all(spread, axis, split_axis=0, concat_axis=0, tiled=True)  17.1 us
  transfers between devices with their start and end apart: 6, of which 6 were waited for; matrix products, arithmetic and copies ran while one was open for 27% of the time, Pallas kernels for 0%

profile of v4, /device:TPU:0, one launch (start us, length us, event | category | flops | bytes accessed | tf_op | source)
XLA Modules:
  0.0 453.3 jit_solution(7361005602246343268)
XLA Ops:
  14.6 4.4 gather_fusion.2
  19.1 2.4 gather_fusion.1
  21.6 3.5 bitcast_select_fusion.1
  25.2 3.2 pad_maximum_fusion
  28.4 95.0 %all-reduce.3.cloned.1.call-done = f32[256,2305]{1,0:T(8,128)} async-done(((f32[256,2305]{1,0:T(8,128)}), f32[256,2305]{1,0:T(8,128)}) %all-reduce.3.cloned.1.call-update) | async-done | bytes 2360336 | tf_op jit(solution)/shard_map/psum | solution.py:57
  123.4 5.7 %all-to-all-start = ((bf16[32,2,64,768]{3,2,1,0:T(8,128)(2,1)}), bf16[32,2,64,768]{3,2,1,0:T(8,128)(2,1)}, u32[]{:S(2)}, u32[]{:S(2)}) async-start(bf16[32,2,64,768]{3,2,1,0:T(8,128)(2,1)} %pad_maximum_fusion), calls=%async_computation | async-start | bytes 12582912 | tf_op jit(solution)/shard_map/all_to_all | solution.py:90
  129.1 5.4 %reshape.328 = bf16[32,64,8,96]{3,2,1,0:T(8,128)(2,1)} reshape(bf16[32,64,768]{2,1,0:T(8,128)(2,1)S(1)} %copy-done.2) | data formatting | bytes 6291456 | tf_op jit(solution)/shard_map/reshape | solution.py:119
  134.6 8.2 %reshape.329 = bf16[32,64,8,96]{3,2,1,0:T(8,128)(2,1)} reshape(bf16[32,64,768]{2,1,0:T(8,128)(2,1)} %param.20) | data formatting | bytes 6291456 | tf_op jit(solution)/shard_map/reshape | solution.py:120
  150.9 3.2 slice.62
  154.1 3.0 copy.219
  167.2 6.0 %fusion.66 = (f32[4,32,8]{0,2,1:T(8,128)}, f32[4,32,8,64]{3,0,2,1:T(4,128)}) fusion(bf16[32,64,8,96]{3,2,1,0:T(8,128)(2,1)} %reshape.328, bf16[4,32,8,96]{3,2,0,1:T(8,128)(2,1)} %bitcast.141, pred[32,64]{1,0:T(8,128)(4,1)S(1)} %fusion.46), kind=kOutput, calls=%fused_computation.140 | convolution fusion | flops 12778496 | bytes 3610624 | tf_op jit(solution)/shard_map/tshd,skhd->tshk/dot_general | solution.py:122
  181.6 2.4 fusion.24
  188.7 3.4 copy.232
  192.1 3.4 copy.233
  195.5 3.7 fusion.7
  202.5 4.6 %all-to-all-done = bf16[32,2,64,768]{3,2,1,0:T(8,128)(2,1)} async-done(((bf16[32,2,64,768]{3,2,1,0:T(8,128)(2,1)}), bf16[32,2,64,768]{3,2,1,0:T(8,128)(2,1)}, u32[]{:S(2)}, u32[]{:S(2)}) %all-to-all-start) | async-done | bytes 6291488 | tf_op jit(solution)/shard_map/all_to_all | solution.py:90
  207.0 6.3 %slice_bitcast_fusion = (bf16[32,64,768]{2,1,0:T(8,128)(2,1)}, bf16[32,64,768]{2,1,0:T(8,128)(2,1)}) fusion(bf16[32,2,64,768]{3,2,1,0:T(8,128)(2,1)} %all-to-all-done), kind=kLoop, calls=%fused_computation.14 | loop fusion | bytes 12582912 | tf_op jit(solution)/shard_map/squeeze | solution.py:91
  213.3 4.9 %all-to-all-start.1 = ((f32[32,4,2,8,98]{4,3,2,1,0:T(8,128)}), f32[32,4,2,8,98]{4,3,2,1,0:T(8,128)}, u32[]{:S(2)}, u32[]{:S(2)}) async-start(f32[32,4,2,8,98]{4,3,2,1,0:T(8,128)} %maximum_bitcast_fusion), calls=%async_computation.1 | async-start | bytes 2097152 | tf_op jit(solution)/shard_map/all_to_all | solution.py:210
  225.2 2.6 reshape.401
  227.8 2.5 constant_dynamic-slice_fusion
  235.2 4.1 fusion.65
  256.0 17.1 %all_to_all.25 = bf16[32,4,2,8,96]{4,3,2,1,0:T(8,128)(2,1)S(1)} all-to-all(bf16[32,4,2,8,96]{4,3,2,1,0:T(8,128)(2,1)S(1)} %broadcast_in_dim.192), channel_id=1, replica_groups=mesh['pages'=32,'mp'=4] {'pages'}, dimensions={0} | all-to-all | bytes 786432 | tf_op jit(solution)/shard_map/all_to_all | solution.py:68
  278.3 4.4 all-to-all-start.3
  284.8 6.4 %all-to-all-done.3 = f32[4,256,96]{1,2,0:T(8,128)} async-done(((f32[4,256,96]{1,2,0:T(8,128)}), f32[4,256,96]{1,2,0:T(8,128)}, u32[]{:S(2)}, u32[]{:S(2)}) %all-to-all-start.3) | async-done | bytes 393248 | tf_op jit(solution)/shard_map/all_to_all | solution.py:68
  302.0 4.3 gather_fusion.6
  306.2 4.3 gather_fusion.7
  310.5 98.1 %all-reduce.5.cloned.1.call-done = f32[256,4097]{1,0:T(8,128)} async-done(((f32[256,4097]{1,0:T(8,128)}), f32[256,4097]{1,0:T(8,128)}) %all-reduce.5.cloned.1.call-update) | async-done | bytes 4195344 | tf_op jit(solution)/shard_map/psum | solution.py:57
  408.6 4.6 %slice.109 = f32[256,4096]{1,0:T(8,128)} slice(f32[256,4097]{1,0:T(8,128)} %all-reduce.5.cloned.1.call-done), slice={[0:256], [0:4096]} | slice | bytes 8388608 | tf_op jit(solution)/shard_map/slice | solution.py:61
  413.2 6.6 %reshape.331 = f32[256,2,2048]{2,1,0:T(2,128)} reshape(f32[256,4096]{1,0:T(8,128)} %slice.109) | data formatting | bytes 8388608 | tf_op jit(solution)/shard_map/reshape | solution.py:61
  419.8 7.8 %fusion.63 = (f32[256,1,2048]{2,1,0:T(1,128)S(1)}, f32[256,1,2048]{2,1,0:T(1,128)S(1)}) fusion(f32[256,2,2048]{2,1,0:T(2,128)} %reshape.331), kind=kLoop, calls=%fused_computation.137 | loop fusion | bytes 8388608 | tf_op jit(solution)/shard_map/slice | solution.py:184
  431.0 4.4 all-to-all-start.4
  435.4 7.1 %broadcast_select_fusion = (bf16[32,64,768]{2,1,0:T(8,128)(2,1)}, bf16[32,64,768]{2,1,0:T(8,128)(2,1)}) fusion(bf16[32,64,768]{2,1,0:T(8,128)(2,1)} %gather_fusion.7, bf16[32,64,768]{2,1,0:T(8,128)(2,1)} %param.20, pred[32]{0:T(512)(128)(4,1)S(1)} %fusion.44, bf16[32,64,768]{2,1,0:T(8,128)(2,1)} %gather_fusion.6, bf16[32,64,768]{2,1,0:T(8,128)(2,1)S(1)} %copy-done.2), kind=kLoop, calls=%fused_computation.18 | loop fusion | flops 3145728 | bytes 18874400 | tf_op jit(solution)/shard_map/jit(_where)/select_n | solution.py:105
  (131 shorter events, 95.6 us)
Async XLA Ops:
  7.2 421.5 %copy-start = (bf16[96,2048]{1,0:T(8,128)(2,1)S(1)}, bf16[96,2048]{1,0:T(8,128)(2,1)}, u32[]{:S(2)}) copy-start(bf16[96,2048]{1,0:T(8,128)(2,1)} %param.18) | copy-start | bytes 1179652
  7.2 116.3 %all-reduce.3.cloned.1.call-start = ((), (), s32[]{:S(2)}) async-start(), calls=%async_computation.5 | async-start | bytes 4980736 | tf_op jit(solution)/shard_map/psum | solution.py:57
  11.1 1.7 copy-start.18
  13.5 0.5 copy-start.16
  14.6 4.5 copy-start.2
  123.4 83.6 %all-to-all-start = ((bf16[32,2,64,768]{3,2,1,0:T(8,128)(2,1)}), bf16[32,2,64,768]{3,2,1,0:T(8,128)(2,1)}, u32[]{:S(2)}, u32[]{:S(2)}) async-start(bf16[32,2,64,768]{3,2,1,0:T(8,128)(2,1)} %pad_maximum_fusion), calls=%async_computation | async-start | bytes 12582912 | tf_op jit(solution)/shard_map/all_to_all | solution.py:90
  134.6 8.3 %copy-start.1 = (s32[64]{0:T(128)S(1)}, s32[64]{0:T(128)}, u32[]{:S(2)}) copy-start(s32[64]{0:T(128)} %param.21) | copy-start | bytes 772
  146.0 11.2 %copy-start.12 = (s32[32]{0:T(128)}, s32[32]{0:T(128)S(1)}, u32[]{:S(2)}) copy-start(s32[32]{0:T(128)S(1)} %get-tuple-element.16) | copy-start | bytes 388
  146.0 18.8 %copy-start.11 = (s32[1024]{0:T(1024)}, s32[1024]{0:T(1024)S(1)}, u32[]{:S(2)}) copy-start(s32[1024]{0:T(1024)S(1)} %pad_clamp_fusion.3) | copy-start | bytes 12292
  150.0 17.2 %copy-start.9 = (pred[32,64]{1,0:T(8,128)(4,1)}, pred[32,64]{1,0:T(8,128)(4,1)S(1)}, u32[]{:S(2)}) copy-start(pred[32,64]{1,0:T(8,128)(4,1)S(1)} %fusion.46) | copy-start | bytes 6148
  160.0 0.9 copy-start.6
  160.1 0.9 copy-start.7
  177.6 17.9 %copy-start.10 = (pred[32,64]{1,0:T(8,128)(4,1)S(1)}, pred[32,64]{1,0:T(8,128)(4,1)}, u32[]{:S(2)}) copy-start(pred[32,64]{1,0:T(8,128)(4,1)} %copy-done.9) | copy-start | bytes 6148
  195.5 3.7 copy-start.13
  199.2 1.6 copy-start.3
  199.2 1.6 copy-start.4
  213.3 21.9 %all-to-all-start.1 = ((f32[32,4,2,8,98]{4,3,2,1,0:T(8,128)}), f32[32,4,2,8,98]{4,3,2,1,0:T(8,128)}, u32[]{:S(2)}, u32[]{:S(2)}) async-start(f32[32,4,2,8,98]{4,3,2,1,0:T(8,128)} %maximum_bitcast_fusion), calls=%async_computation.1 | async-start | bytes 2097152 | tf_op jit(solution)/shard_map/all_to_all | solution.py:210
  242.3 2.0 copy-start.8
  273.1 21.4 %copy-start.14 = (f32[96]{0:T(128)S(1)}, f32[96]{0:T(128)}, u32[]{:S(2)}) copy-start(f32[96]{0:T(128)} %get-tuple-element.40) | copy-start | bytes 1156
  278.3 12.9 %all-to-all-start.3 = ((f32[4,256,96]{1,2,0:T(8,128)}), f32[4,256,96]{1,2,0:T(8,128)}, u32[]{:S(2)}, u32[]{:S(2)}) async-start(f32[4,256,96]{1,2,0:T(8,128)} %broadcast_in_dim.193), calls=%async_computation.3 | async-start | bytes 786432 | tf_op jit(solution)/shard_map/all_to_all | solution.py:68
  282.7 125.9 %all-reduce.5.cloned.1.call-start = ((), (), s32[]{:S(2)}) async-start(), calls=%async_computation.6 | async-start | bytes 8650752 | tf_op jit(solution)/shard_map/psum | solution.py:57
  296.9 1.9 copy-start.5
  301.2 0.7 copy-start.15
  301.2 0.7 copy-start.17
  431.0 12.7 %all-to-all-start.4 = ((f32[4,256,96]{1,2,0:T(8,128)}), f32[4,256,96]{1,2,0:T(8,128)}, u32[]{:S(2)}, u32[]{:S(2)}) async-start(f32[4,256,96]{1,2,0:T(8,128)} %broadcast_in_dim.195), calls=%async_computation.4 | async-start | bytes 786432 | tf_op jit(solution)/shard_map/all_to_all | solution.py:68
Sparse Core Ops, SparseCore 0:
  12.9 110.4 all-reduce.2
  301.3 107.2 all-reduce.4

commit v5 on v4

--- a/solution.py
+++ b/solution.py
@@ -53,13 +53,24 @@
 
 def reduce_rows(partial_value, squares, finish, tied=None):
     rows = partial_value.shape[0]
+    holders = lax.axis_size("pages")
+    block = rows // holders
     packed = jnp.concatenate([partial_value.reshape(rows, -1), squares[:, None]], axis=1)
-    packed = lax.psum(packed, "pages")
+    packed = packed.reshape(holders, block, packed.shape[1])
+    packed = lax.all_to_all(packed, "pages", split_axis=0, concat_axis=0, tiled=True)
+    packed = jnp.sum(packed, axis=0)
+    start = lax.axis_index("pages") * block
+    done = finish(packed[:, :-1].reshape((block,) + partial_value.shape[1:]), packed[:, -1], start)
+    width = [part.shape[1] for part in done]
+    joined = gather_blocks(jnp.concatenate(done, axis=1), "pages").reshape(rows, sum(width))
+    pieces = []
+    offset = 0
+    for size in width:
+        pieces.append(joined[:, offset : offset + size])
+        offset += size
     if tied is not None:
-        packed, tied = lax.optimization_barrier((packed, tied))
-        return finish(packed[:, :-1].reshape(partial_value.shape), packed[:, -1], 0), tied
-    total = packed[:, :-1].reshape(partial_value.shape)
-    return finish(total, packed[:, -1], 0)
+        return lax.optimization_barrier((tuple(pieces), tied))
+    return tuple(pieces)
 
 
 def gather_blocks(block, axis):
@@ -168,11 +179,12 @@
 
     def finish_qkv(total, squares, start):
         count = total.shape[0]
+        rows_here = lax.dynamic_slice_in_dim(positions, start, count)
         inverse = lax.rsqrt(squares / D + EPSILON)
         scaled = total * inverse[:, None, None]
         heads_here = scaled.shape[2] // HEAD_DIM
-        query_rows = rotate(scaled[:, 0].reshape(count, heads_here, HEAD_DIM), positions)
-        key_rows = rotate(scaled[:, 1].reshape(count, heads_here, HEAD_DIM), positions)
+        query_rows = rotate(scaled[:, 0].reshape(count, heads_here, HEAD_DIM), rows_here)
+        key_rows = rotate(scaled[:, 1].reshape(count, heads_here, HEAD_DIM), rows_here)
         return (
             query_rows.reshape(count, -1).astype(jnp.bfloat16),
             key_rows.reshape(count, -1).astype(jnp.bfloat16),

time: 456 us -> 356 us (0.78)
  waiting for transfers between devices: 207 us -> 74.3 us
  blocking collectives: 17.1 us -> 71.6 us
  local copies, waits for them, and re-layouts: 120 us -> 101 us
  starting transfers between devices: 19.5 us -> 36.3 us
  between operations: 14.4 us -> 1.04 us
  other arithmetic: 56.8 us -> 50.1 us
    psum x2 -> x0, waiting for transfers between devices: 193 us -> none  [reduce_rows(): packed = lax.psum(packed, 'pages')]
    all_to_all x0 -> x1, blocking collectives: none -> 56.6 us  [reduce_rows(): lax.all_to_all(packed, 'pages', split_axis=0, concat_axis=0, tiled=True)]
    all_to_all x0 -> x1, waiting for transfers between devices: none -> 31.6 us  [reduce_rows(): lax.all_to_all(packed, 'pages', split_axis=0, concat_axis=0, tiled=True)]
    slice x6 -> x4, local copies, waits for them, and re-layouts: 19.5 us -> 3.2 us  [the longest x1 2.27 us: reduce_rows(): pieces.append(joined[:, offset:offset + size])]
    all_to_all x1, waiting for transfers between devices: 4.56 us -> 19.8 us  [exchange_pool(): lax.all_to_all(both, 'pages', split_axis=0, concat_axis=0, tiled=True)]
    all_to_all x2 -> x4, starting transfers between devices: 8.84 us -> 18.7 us  [gather_blocks(): return lax.all_to_all(spread, axis, split_axis=0, concat_axis=0, tiled=True)]
    all_to_all x2 -> x4, waiting for transfers between devices: 7.56 us -> 16.9 us  [gather_blocks(): return lax.all_to_all(spread, axis, split_axis=0, concat_axis=0, tiled=True)]
    all_to_all x0 -> x1, starting transfers between devices: none -> 7.57 us  [reduce_rows(): lax.all_to_all(packed, 'pages', split_axis=0, concat_axis=0, tiled=True)]
  transfers between devices with their start and end apart: 6 -> 7, of which waited for: 6 -> 7; matrix products, arithmetic and copies ran while one was open for 27% -> 30% of each run, Pallas kernels for 0% -> 0%
where the time goes in v5:
time: 356 us; the launch traced here: 353 us
  local copies, waits for them, and re-layouts  101 us (28%)
  waiting for transfers between devices  74.3 us (21%)
  blocking collectives  71.6 us (20%)
  other arithmetic  50.1 us (14%)
  starting transfers between devices  36.3 us (10%)
  matrix products  19.1 us (5%)
    all_to_all x1, blocking collectives, reduce_rows(): lax.all_to_all(packed, 'pages', split_axis=0, concat_axis=0, tiled=True)  56.6 us
    all_to_all x1, waiting for transfers between devices, reduce_rows(): lax.all_to_all(packed, 'pages', split_axis=0, concat_axis=0, tiled=True)  31.6 us
    all_to_all x1, waiting for transfers between devices, exchange_pool(): lax.all_to_all(both, 'pages', split_axis=0, concat_axis=0, tiled=True)  19.8 us
    all_to_all x4, starting transfers between devices, gather_blocks(): return lax.all_to_all(spread, axis, split_axis=0, concat_axis=0, tiled=True)  18.7 us
    all_to_all x4, waiting for transfers between devices, gather_blocks(): return lax.all_to_all(spread, axis, split_axis=0, concat_axis=0, tiled=True)  16.9 us
    all_to_all x1, blocking collectives, gather_blocks(): return lax.all_to_all(spread, axis, split_axis=0, concat_axis=0, tiled=True)  15 us
    reshape x1, local copies, waits for them, and re-layouts, local_attention(): values_here = v_cache.reshape(slot_count, page_len, heads_here, head_dim)  8.24 us
    all_to_all x1, starting transfers between devices, reduce_rows(): lax.all_to_all(packed, 'pages', split_axis=0, concat_axis=0, tiled=True)  7.57 us
  transfers between devices with their start and end apart: 7, of which 7 were waited for; matrix products, arithmetic and copies ran while one was open for 30% of the time, Pallas kernels for 0%

profile of v5, /device:TPU:0, one launch (start us, length us, event | category | flops | bytes accessed | tf_op | source)
XLA Modules:
  0.0 353.0 jit_solution(14119745977243943911)
XLA Ops:
  7.0 7.6 %all-to-all-start = ((f32[32,8,2305]{2,1,0:T(8,128)}), f32[32,8,2305]{2,1,0:T(8,128)S(1)}, u32[]{:S(2)}, u32[]{:S(2)}) async-start(f32[32,8,2305]{2,1,0:T(8,128)} %pad_maximum_fusion.2), calls=%async_computation | async-start | bytes 4980736 | tf_op jit(solution)/shard_map/all_to_all | solution.py:60
  17.7 31.6 %all-to-all-done = f32[32,8,2305]{2,1,0:T(8,128)S(1)} async-done(((f32[32,8,2305]{2,1,0:T(8,128)}), f32[32,8,2305]{2,1,0:T(8,128)S(1)}, u32[]{:S(2)}, u32[]{:S(2)}) %all-to-all-start) | async-done | bytes 2360352 | tf_op jit(solution)/shard_map/all_to_all | solution.py:60
  51.3 4.7 %all-to-all-start.1 = ((bf16[32,8,2304]{2,1,0:T(8,128)(2,1)}), bf16[32,8,2304]{2,1,0:T(8,128)(2,1)}, u32[]{:S(2)}, u32[]{:S(2)}) async-start(bf16[32,8,2304]{2,1,0:T(8,128)(2,1)} %broadcast_in_dim.186), calls=%async_computation.1 | async-start | bytes 2359296 | tf_op jit(solution)/shard_map/all_to_all | solution.py:79
  56.6 4.4 %gather_fusion.3 = bf16[32,64,768]{2,1,0:T(8,128)(2,1)} fusion(bf16[32,64,768]{2,1,0:T(8,128)(2,1)} %param.20, s32[1024]{0:T(1024)S(1)} %pad_clamp_fusion.1), kind=kCustom, calls=%fused_computation.3 | custom fusion | bytes 6291584 | tf_op jit(solution)/shard_map/gather | solution.py:96
  63.6 3.3 bitcast_select_fusion.1
  66.9 3.2 pad_maximum_fusion
  70.1 4.6 %all-to-all-done.1 = bf16[32,8,2304]{2,1,0:T(8,128)(2,1)} async-done(((bf16[32,8,2304]{2,1,0:T(8,128)(2,1)}), bf16[32,8,2304]{2,1,0:T(8,128)(2,1)}, u32[]{:S(2)}, u32[]{:S(2)}) %all-to-all-start.1) | async-done | bytes 1179680 | tf_op jit(solution)/shard_map/all_to_all | solution.py:79
  77.0 5.1 %all-to-all-start.2 = ((bf16[32,2,64,768]{3,2,1,0:T(8,128)(2,1)}), bf16[32,2,64,768]{3,2,1,0:T(8,128)(2,1)}, u32[]{:S(2)}, u32[]{:S(2)}) async-start(bf16[32,2,64,768]{3,2,1,0:T(8,128)(2,1)} %pad_maximum_fusion), calls=%async_computation.2 | async-start | bytes 12582912 | tf_op jit(solution)/shard_map/all_to_all | solution.py:101
  82.0 5.4 %reshape.374 = bf16[32,64,8,96]{3,2,1,0:T(8,128)(2,1)} reshape(bf16[32,64,768]{2,1,0:T(8,128)(2,1)S(1)} %copy-done.2) | data formatting | bytes 6291456 | tf_op jit(solution)/shard_map/reshape | solution.py:130
  87.5 8.2 %reshape.375 = bf16[32,64,8,96]{3,2,1,0:T(8,128)(2,1)} reshape(bf16[32,64,768]{2,1,0:T(8,128)(2,1)} %param.20) | data formatting | bytes 6291456 | tf_op jit(solution)/shard_map/reshape | solution.py:131
  104.6 6.0 %fusion.71 = (f32[4,32,8]{0,2,1:T(8,128)}, f32[4,32,8,64]{3,0,2,1:T(4,128)}) fusion(bf16[32,64,8,96]{3,2,1,0:T(8,128)(2,1)} %reshape.374, bf16[4,32,8,96]{3,2,0,1:T(8,128)(2,1)} %bitcast.139, pred[32,64]{1,0:T(8,128)(4,1)S(1)} %fusion.46), kind=kOutput, calls=%fused_computation.148 | convolution fusion | flops 12778496 | bytes 3610624 | tf_op jit(solution)/shard_map/tshd,skhd->tshk/dot_general | solution.py:133
  119.0 2.4 fusion.21
  126.1 3.4 copy.241
  129.5 3.4 copy.242
  133.0 3.7 %fusion.4 = f32[4,32,8,96]{3,0,2,1:T(4,128)S(1)} fusion(bf16[32,64,8,96]{3,2,1,0:T(8,128)(2,1)} %reshape.375, f32[4,32,8,64]{3,0,2,1:T(4,128)} %get-tuple-element.54, f32[4,32,8]{0,2,1:T(8,128)} %copy.234, pred[32,64]{1,0:T(8,128)(4,1)S(1)} %copy-done.8), kind=kOutput, calls=%fused_computation.21 | convolution fusion | flops 12779520 | bytes 3807232 | tf_op jit(solution)/shard_map/tshk,skhd->tshd/dot_general | solution.py:147
  139.9 19.8 %all-to-all-done.2 = bf16[32,2,64,768]{3,2,1,0:T(8,128)(2,1)} async-done(((bf16[32,2,64,768]{3,2,1,0:T(8,128)(2,1)}), bf16[32,2,64,768]{3,2,1,0:T(8,128)(2,1)}, u32[]{:S(2)}, u32[]{:S(2)}) %all-to-all-start.2) | async-done | bytes 6291488 | tf_op jit(solution)/shard_map/all_to_all | solution.py:101
  159.8 6.3 %slice_bitcast_fusion = (bf16[32,64,768]{2,1,0:T(8,128)(2,1)}, bf16[32,64,768]{2,1,0:T(8,128)(2,1)}) fusion(bf16[32,2,64,768]{3,2,1,0:T(8,128)(2,1)} %all-to-all-done.2), kind=kLoop, calls=%fused_computation.14 | loop fusion | bytes 12582912 | tf_op jit(solution)/shard_map/squeeze | solution.py:102
  166.0 4.9 %all-to-all-start.3 = ((f32[32,4,2,8,98]{4,3,2,1,0:T(8,128)}), f32[32,4,2,8,98]{4,3,2,1,0:T(8,128)}, u32[]{:S(2)}, u32[]{:S(2)}) async-start(f32[32,4,2,8,98]{4,3,2,1,0:T(8,128)} %maximum_bitcast_fusion), calls=%async_computation.3 | async-start | bytes 2097152 | tf_op jit(solution)/shard_map/all_to_all | solution.py:222
  181.9 6.0 %all-to-all-done.3 = f32[32,4,2,8,98]{4,3,2,1,0:T(8,128)} async-done(((f32[32,4,2,8,98]{4,3,2,1,0:T(8,128)}), f32[32,4,2,8,98]{4,3,2,1,0:T(8,128)}, u32[]{:S(2)}, u32[]{:S(2)}) %all-to-all-start.3) | async-done | bytes 802848 | tf_op jit(solution)/shard_map/all_to_all | solution.py:222
  187.9 4.1 %fusion.69 = (f32[32,4,2,8,1]{4,3,2,1,0:T(8,128)}, f32[4,2,8]{2,1,0:T(2,128)}, f32[32,4,2,8,1]{4,3,2,1,0:T(8,128)}) fusion(f32[32,4,2,8,98]{4,3,2,1,0:T(8,128)} %all-to-all-done.3), kind=kLoop, calls=%fused_computation.146 | loop fusion | flops 1984 | bytes 33024 | tf_op jit(solution)/shard_map/slice | solution.py:224
  208.6 15.0 %all_to_all.45 = bf16[32,4,2,8,96]{4,3,2,1,0:T(8,128)(2,1)S(1)} all-to-all(bf16[32,4,2,8,96]{4,3,2,1,0:T(8,128)(2,1)S(1)} %broadcast_in_dim.200), channel_id=1, replica_groups=mesh['pages'=32,'mp'=4] {'pages'}, dimensions={0} | all-to-all | bytes 786432 | tf_op jit(solution)/shard_map/all_to_all | solution.py:79
  228.8 5.3 %all-to-all-start.5 = ((f32[4,256,96]{1,2,0:T(8,128)}), f32[4,256,96]{1,2,0:T(8,128)}, u32[]{:S(2)}, u32[]{:S(2)}) async-start(f32[4,256,96]{1,2,0:T(8,128)} %broadcast_in_dim.201), calls=%async_computation.5 | async-start | bytes 786432 | tf_op jit(solution)/shard_map/all_to_all | solution.py:79
  234.1 2.8 copy.264
  237.0 3.2 reshape.451
  250.6 56.6 %all_to_all.46 = f32[32,8,4097]{2,1,0:T(8,128)} all-to-all(f32[32,8,4097]{2,1,0:T(8,128)S(1)} %pad_maximum_fusion.1), channel_id=1, replica_groups=mesh['pages'=32,'mp'=4] {'pages'}, dimensions={0} | all-to-all | bytes 8390656 | tf_op jit(solution)/shard_map/all_to_all | solution.py:60
  307.1 3.1 reduce_sum.127
  313.1 4.7 %all-to-all-start.7 = ((bf16[32,8,2048]{2,1,0:T(8,128)(2,1)}), bf16[32,8,2048]{2,1,0:T(8,128)(2,1)}, u32[]{:S(2)}, u32[]{:S(2)}) async-start(bf16[32,8,2048]{2,1,0:T(8,128)(2,1)} %broadcast_in_dim.202), calls=%async_computation.7 | async-start | bytes 2097152 | tf_op jit(solution)/shard_map/all_to_all | solution.py:79
  318.0 4.3 %gather_fusion.6 = bf16[32,64,768]{2,1,0:T(8,128)(2,1)} fusion(bf16[32,64,768]{2,1,0:T(8,128)(2,1)} %get-tuple-element.15, s32[1024]{0:T(1024)S(1)} %pad_clamp_fusion), kind=kCustom, calls=%fused_computation.6 | custom fusion | bytes 6291584 | tf_op jit(solution)/shard_map/gather | solution.py:115
  322.3 4.3 %gather_fusion.7 = bf16[32,64,768]{2,1,0:T(8,128)(2,1)} fusion(bf16[32,64,768]{2,1,0:T(8,128)(2,1)} %get-tuple-element.16, s32[1024]{0:T(1024)S(1)} %pad_clamp_fusion), kind=kCustom, calls=%fused_computation.7 | custom fusion | bytes 6291584 | tf_op jit(solution)/shard_map/gather | solution.py:116
  326.6 8.4 %all-to-all-done.7 = bf16[32,8,2048]{2,1,0:T(8,128)(2,1)} async-done(((bf16[32,8,2048]{2,1,0:T(8,128)(2,1)}), bf16[32,8,2048]{2,1,0:T(8,128)(2,1)}, u32[]{:S(2)}, u32[]{:S(2)}) %all-to-all-start.7) | async-done | bytes 1048608 | tf_op jit(solution)/shard_map/all_to_all | solution.py:79
  337.5 4.1 %all-to-all-start.8 = ((f32[4,256,96]{1,2,0:T(8,128)}), f32[4,256,96]{1,2,0:T(8,128)}, u32[]{:S(2)}, u32[]{:S(2)}) async-start(f32[4,256,96]{1,2,0:T(8,128)} %broadcast_in_dim.203), calls=%async_computation.8 | async-start | bytes 786432 | tf_op jit(solution)/shard_map/all_to_all | solution.py:79
  341.6 7.1 %broadcast_select_fusion = (bf16[32,64,768]{2,1,0:T(8,128)(2,1)}, bf16[32,64,768]{2,1,0:T(8,128)(2,1)}) fusion(bf16[32,64,768]{2,1,0:T(8,128)(2,1)} %gather_fusion.7, bf16[32,64,768]{2,1,0:T(8,128)(2,1)} %param.20, pred[32]{0:T(512)(128)(4,1)S(1)} %fusion.44, bf16[32,64,768]{2,1,0:T(8,128)(2,1)} %gather_fusion.6, bf16[32,64,768]{2,1,0:T(8,128)(2,1)S(1)} %copy-done.2), kind=kLoop, calls=%fused_computation.18 | loop fusion | flops 3145728 | bytes 18874400 | tf_op jit(solution)/shard_map/jit(_where)/select_n | solution.py:116
  (137 shorter events, 94.8 us)
Async XLA Ops:
  0.6 334.4 %copy-start = (bf16[96,2048]{1,0:T(8,128)(2,1)S(1)}, bf16[96,2048]{1,0:T(8,128)(2,1)}, u32[]{:S(2)}) copy-start(bf16[96,2048]{1,0:T(8,128)(2,1)} %param.18) | copy-start | bytes 1179652
  7.0 7.6 %copy-start.1 = (s32[64]{0:T(128)S(1)}, s32[64]{0:T(128)}, u32[]{:S(2)}) copy-start(s32[64]{0:T(128)} %param.21) | copy-start | bytes 772
  7.0 10.3 %copy-start.16 = (s32[31]{0:T(128)S(1)}, s32[31]{0:T(128)}, u32[]{:S(2)}) copy-start(s32[31]{0:T(128)} %param.25) | copy-start | bytes 376
  7.0 42.3 %all-to-all-start = ((f32[32,8,2305]{2,1,0:T(8,128)}), f32[32,8,2305]{2,1,0:T(8,128)S(1)}, u32[]{:S(2)}, u32[]{:S(2)}) async-start(f32[32,8,2305]{2,1,0:T(8,128)} %pad_maximum_fusion.2), calls=%async_computation | async-start | bytes 4980736 | tf_op jit(solution)/shard_map/all_to_all | solution.py:60
  17.2 0.5 copy-start.14
  51.3 23.4 %all-to-all-start.1 = ((bf16[32,8,2304]{2,1,0:T(8,128)(2,1)}), bf16[32,8,2304]{2,1,0:T(8,128)(2,1)}, u32[]{:S(2)}, u32[]{:S(2)}) async-start(bf16[32,8,2304]{2,1,0:T(8,128)(2,1)} %broadcast_in_dim.186), calls=%async_computation.1 | async-start | bytes 2359296 | tf_op jit(solution)/shard_map/all_to_all | solution.py:79
  56.6 4.5 %copy-start.2 = (bf16[32,64,768]{2,1,0:T(8,128)(2,1)S(1)}, bf16[32,64,768]{2,1,0:T(8,128)(2,1)}, u32[]{:S(2)}) copy-start(bf16[32,64,768]{2,1,0:T(8,128)(2,1)} %param.19) | copy-start | bytes 9437188
  77.0 82.8 %all-to-all-start.2 = ((bf16[32,2,64,768]{3,2,1,0:T(8,128)(2,1)}), bf16[32,2,64,768]{3,2,1,0:T(8,128)(2,1)}, u32[]{:S(2)}, u32[]{:S(2)}) async-start(bf16[32,2,64,768]{3,2,1,0:T(8,128)(2,1)} %pad_maximum_fusion), calls=%async_computation.2 | async-start | bytes 12582912 | tf_op jit(solution)/shard_map/all_to_all | solution.py:101
  96.5 14.2 %copy-start.10 = (s32[32]{0:T(128)}, s32[32]{0:T(128)S(1)}, u32[]{:S(2)}) copy-start(s32[32]{0:T(128)S(1)} %get-tuple-element.20) | copy-start | bytes 388
  96.5 14.2 %copy-start.9 = (s32[1024]{0:T(1024)}, s32[1024]{0:T(1024)S(1)}, u32[]{:S(2)}) copy-start(s32[1024]{0:T(1024)S(1)} %pad_clamp_fusion.3) | copy-start | bytes 12292
  99.9 10.8 %copy-start.7 = (pred[32,64]{1,0:T(8,128)(4,1)}, pred[32,64]{1,0:T(8,128)(4,1)S(1)}, u32[]{:S(2)}) copy-start(pred[32,64]{1,0:T(8,128)(4,1)S(1)} %fusion.46) | copy-start | bytes 6148
  115.1 17.9 %copy-start.8 = (pred[32,64]{1,0:T(8,128)(4,1)S(1)}, pred[32,64]{1,0:T(8,128)(4,1)}, u32[]{:S(2)}) copy-start(pred[32,64]{1,0:T(8,128)(4,1)} %copy-done.7) | copy-start | bytes 6148
  133.0 3.7 %copy-start.11 = (s32[32]{0:T(128)S(1)}, s32[32]{0:T(128)}, u32[]{:S(2)}) copy-start(s32[32]{0:T(128)} %copy-done.10) | copy-start | bytes 388
  136.6 1.6 copy-start.3
  136.6 1.6 copy-start.4
  166.0 21.9 %all-to-all-start.3 = ((f32[32,4,2,8,98]{4,3,2,1,0:T(8,128)}), f32[32,4,2,8,98]{4,3,2,1,0:T(8,128)}, u32[]{:S(2)}, u32[]{:S(2)}) async-start(f32[32,4,2,8,98]{4,3,2,1,0:T(8,128)} %maximum_bitcast_fusion), calls=%async_computation.3 | async-start | bytes 2097152 | tf_op jit(solution)/shard_map/all_to_all | solution.py:222
  195.0 1.9 copy-start.6
  224.5 21.4 %copy-start.12 = (f32[96]{0:T(128)S(1)}, f32[96]{0:T(128)}, u32[]{:S(2)}) copy-start(f32[96]{0:T(128)} %get-tuple-element.43) | copy-start | bytes 1156
  228.8 13.8 %all-to-all-start.5 = ((f32[4,256,96]{1,2,0:T(8,128)}), f32[4,256,96]{1,2,0:T(8,128)}, u32[]{:S(2)}, u32[]{:S(2)}) async-start(f32[4,256,96]{1,2,0:T(8,128)} %broadcast_in_dim.201), calls=%async_computation.5 | async-start | bytes 786432 | tf_op jit(solution)/shard_map/all_to_all | solution.py:79
  248.3 1.9 copy-start.5
  307.1 10.7 %copy-start.13 = (s32[32]{0:T(128)S(1)}, s32[32]{0:T(128)}, u32[]{:S(2)}) copy-start(s32[32]{0:T(128)} %get-tuple-element.56) | copy-start | bytes 388
  307.1 10.7 %copy-start.15 = (s32[31]{0:T(128)S(1)}, s32[31]{0:T(128)}, u32[]{:S(2)}) copy-start(s32[31]{0:T(128)} %copy-done.14) | copy-start | bytes 376
  313.1 21.9 %all-to-all-start.7 = ((bf16[32,8,2048]{2,1,0:T(8,128)(2,1)}), bf16[32,8,2048]{2,1,0:T(8,128)(2,1)}, u32[]{:S(2)}, u32[]{:S(2)}) async-start(bf16[32,8,2048]{2,1,0:T(8,128)(2,1)} %broadcast_in_dim.202), calls=%async_computation.7 | async-start | bytes 2097152 | tf_op jit(solution)/shard_map/all_to_all | solution.py:79
  337.5 12.8 %all-to-all-start.8 = ((f32[4,256,96]{1,2,0:T(8,128)}), f32[4,256,96]{1,2,0:T(8,128)}, u32[]{:S(2)}, u32[]{:S(2)}) async-start(f32[4,256,96]{1,2,0:T(8,128)} %broadcast_in_dim.203), calls=%async_computation.8 | async-start | bytes 786432 | tf_op jit(solution)/shard_map/all_to_all | solution.py:79

commit v6 on v5

--- a/solution.py
+++ b/solution.py
@@ -87,33 +87,27 @@
     holders = lax.axis_size("pages")
     myself = lax.axis_index("pages")
     mine = lax.dynamic_index_in_dim(move_slot, myself, 0, keepdims=False)
-    targets = (myself + move_offset) % holders
-    holder_ids = jnp.arange(holders, dtype=jnp.int32)
-    aimed = holder_ids[:, None] == targets[None, :]
-    chosen = jnp.sum(jnp.where(aimed, mine[None, :], 0), axis=1)
-    sending = jnp.any(aimed, axis=1)[:, None, None]
-    key_send = jnp.where(sending, key_local[chosen], jnp.zeros((), key_local.dtype))
-    value_send = jnp.where(sending, value_local[chosen], jnp.zeros((), value_local.dtype))
-    return jnp.stack([key_send, value_send], axis=1)
-
-
-def exchange_pool(both):
-    both = lax.all_to_all(both, "pages", split_axis=0, concat_axis=0, tiled=True)
-    return both[:, 0], both[:, 1]
-
-
-def land_pool(key_local, value_local, key_recv, value_recv, move_slot, move_offset):
-    holders = lax.axis_size("pages")
+    arrived = []
+    for shift in range(1, holders):
+        move = jnp.argmax(move_offset == shift)
+        slot = mine[move]
+        page = jnp.stack([key_local[slot], value_local[slot]])
+        ring = [(source, (source + shift) % holders) for source in range(holders)]
+        arrived.append(lax.ppermute(page, "pages", ring))
+    return jnp.stack(arrived)
+
+
+def land_pool(key_local, value_local, arrived, move_slot, move_offset):
     myself = lax.axis_index("pages")
     mine = lax.dynamic_index_in_dim(move_slot, myself, 0, keepdims=False)
-    sources = (myself - move_offset) % holders
     slot_ids = jnp.arange(key_local.shape[0], dtype=jnp.int32)
     landing = slot_ids[:, None] == mine[None, :]
-    came_from = jnp.sum(jnp.where(landing, sources[None, :], 0), axis=1)
+    came_from = jnp.sum(jnp.where(landing, move_offset[None, :] - 1, 0), axis=1)
     arriving = jnp.any(landing, axis=1)[:, None, None]
+    picked = arrived[came_from]
     return (
-        jnp.where(arriving, key_recv[came_from], key_local),
-        jnp.where(arriving, value_recv[came_from], value_local),
+        jnp.where(arriving, picked[:, 0], key_local),
+        jnp.where(arriving, picked[:, 1], value_local),
     )
 
 
@@ -200,10 +194,7 @@
     normed_one = (activ * norm_gains[0]).astype(jnp.bfloat16)
     partial_one = jnp.einsum("bd,dcn->bcn", normed_one, w_qkv, preferred_element_type=jnp.float32)
     squares_one = jnp.sum(activ * activ, axis=1)
-    sending = migrate_pool(k_cache, v_cache, move_slot, move_offset)
-    (query_all, key_all, value_all), sending = reduce_rows(
-        partial_one, squares_one, finish_qkv, sending
-    )
+    query_all, key_all, value_all = reduce_rows(partial_one, squares_one, finish_qkv)
     heads_here = query_all.shape[1] // HEAD_DIM
     queries = query_all.reshape(step_count, req_count, heads_here, HEAD_DIM)
     key_fresh = key_all.reshape(step_count, req_count, heads_here, HEAD_DIM)
@@ -218,7 +209,6 @@
         [cache_acc, cache_total[..., None], cache_top[..., None]], axis=-1
     ).reshape(step_count, holders, group, heads_here, HEAD_DIM + 2)
     packed = jnp.moveaxis(packed, 1, 0)
-    packed, received = lax.optimization_barrier((packed, exchange_pool(sending)))
     packed = lax.all_to_all(packed, "pages", split_axis=0, concat_axis=0, tiled=True)
     part_acc = packed[..., :HEAD_DIM]
     part_total = packed[..., HEAD_DIM]
@@ -262,7 +252,8 @@
         lax.dot_general(hidden, w_down, CONTRACT_LAST, preferred_element_type=jnp.float32)
     )
     layer_out = (mixed + feed).astype(jnp.bfloat16).reshape(step_count, req_count, width_here)
-    new_k_cache, new_v_cache = land_pool(k_cache, v_cache, *received, move_slot, move_offset)
+    arrived = migrate_pool(k_cache, v_cache, move_slot, move_offset)
+    new_k_cache, new_v_cache = land_pool(k_cache, v_cache, arrived, move_slot, move_offset)
     return (layer_out, new_k_cache, new_v_cache)
 
 

time: 356 us -> 637 us (1.79); the launches traced: 353 us -> 626 us
  between operations: 1.04 us -> 117 us
  starting transfers between devices: 36.3 us -> 141 us
  other arithmetic: 50.1 us -> 143 us
  blocking collectives: 71.6 us -> 0 us
  local copies, waits for them, and re-layouts: 101 us -> 143 us
  waiting for transfers between devices: 74.3 us -> 60.6 us
    ppermute x0 -> x31, starting transfers between devices: none -> 94.6 us  [migrate_pool(): arrived.append(lax.ppermute(page, 'pages', ring))]
    another operation x2 -> x63, other arithmetic: 3.34 us -> 88.2 us  [the longest x31 45.1 us: migrate_pool(): page = jnp.stack([key_local[slot], value_local[slot]])]
    all_to_all x2 -> x0, blocking collectives: 71.6 us -> none  [the longest x1 56.6 us: reduce_rows(): lax.all_to_all(packed, 'pages', split_axis=0, concat_axis=0, tiled=True)]
    ppermute x0 -> x31, waiting for transfers between devices: none -> 39.8 us  [migrate_pool(): arrived.append(lax.ppermute(page, 'pages', ring))]
    unnamed x36 -> x68, local copies, waits for them, and re-layouts: 4.99 us -> 41.9 us
    all_to_all x1 -> x2, waiting for transfers between devices: 31.6 us -> 0.01 us  [reduce_rows(): lax.all_to_all(packed, 'pages', split_axis=0, concat_axis=0, tiled=True)]
    all_to_all x1 -> x0, waiting for transfers between devices: 19.8 us -> none  [exchange_pool(): lax.all_to_all(both, 'pages', split_axis=0, concat_axis=0, tiled=True)]
    dynamic_slice x0 -> x5, local copies, waits for them, and re-layouts: none -> 10 us  [the longest x3 7.27 us: migrate_pool(): page = jnp.stack([key_local[slot], value_local[slot]])]
  transfers between devices with their start and end apart: 7 -> 39, of which waited for: 7 -> 7; matrix products, arithmetic and copies ran while one was open for 30% -> 44% of each run, Pallas kernels for 0% -> 0%
where the time goes in v6:
time: 637 us; the launch traced here: 626 us
  local copies, waits for them, and re-layouts  143 us (22%)
  other arithmetic  143 us (22%)
  starting transfers between devices  141 us (22%)
  between operations  117 us (18%)
  waiting for transfers between devices  60.6 us (10%)
  matrix products  20 us (3%)
    ppermute x31, starting transfers between devices, migrate_pool(): arrived.append(lax.ppermute(page, 'pages', ring))  94.6 us
    another operation x31, other arithmetic, migrate_pool(): page = jnp.stack([key_local[slot], value_local[slot]])  45.1 us
    unnamed x68, local copies, waits for them, and re-layouts  41.9 us
    another operation x31, other arithmetic, migrate_pool(): move = jnp.argmax(move_offset == shift)  41.6 us
    ppermute x31, waiting for transfers between devices, migrate_pool(): arrived.append(lax.ppermute(page, 'pages', ring))  39.8 us
    all_to_all x5, starting transfers between devices, gather_blocks(): return lax.all_to_all(spread, axis, split_axis=0, concat_axis=0, tiled=True)  26.3 us
    all_to_all x5, waiting for transfers between devices, gather_blocks(): return lax.all_to_all(spread, axis, split_axis=0, concat_axis=0, tiled=True)  17.4 us
    all_to_all x2, starting transfers between devices, reduce_rows(): lax.all_to_all(packed, 'pages', split_axis=0, concat_axis=0, tiled=True)  15.3 us
  transfers between devices with their start and end apart: 39, of which 7 were waited for; matrix products, arithmetic and copies ran while one was open for 44% of the time, Pallas kernels for 0%

profile of v6, /device:TPU:0, one launch (start us, length us, event | category | flops | bytes accessed | tf_op | source)
XLA Modules:
  0.0 625.5 jit_solution(18402863230477977700)
XLA Ops:
  92.7 5.6 all-to-all-start
  192.3 5.4 reshape.408
  197.7 8.2 %reshape.409 = bf16[32,64,8,96]{3,2,1,0:T(8,128)(2,1)} reshape(bf16[32,64,768]{2,1,0:T(8,128)(2,1)} %param.20) | data formatting | bytes 6291456 | tf_op jit(solution)/shard_map/reshape | solution.py:125
  217.1 3.2 reshape.461
  278.7 7.6 %all-to-all-start.1 = ((bf16[32,8,2304]{2,1,0:T(8,128)(2,1)}), bf16[32,8,2304]{2,1,0:T(8,128)(2,1)}, u32[]{:S(2)}, u32[]{:S(2)}) async-start(bf16[32,8,2304]{2,1,0:T(8,128)(2,1)} %broadcast_in_dim.95), calls=%async_computation.1 | async-start | bytes 2359296 | tf_op jit(solution)/shard_map/all_to_all | solution.py:79
  299.3 6.2 all-to-all-done.1
  312.6 6.0 fusion.71
  328.7 3.7 fusion.6
  342.5 3.4 copy.237
  345.9 3.4 copy.238
  349.4 3.5 maximum_bitcast_fusion
  352.9 4.7 all-to-all-start.2
  371.2 3.5 all-to-all-done.2
  374.7 4.0 fusion.67
  395.0 4.6 all-to-all-start.3
  407.4 3.8 all-to-all-done.3
  417.4 5.3 all-to-all-start.4
  439.0 3.2 pad_maximum_fusion
  442.3 9.7 %all-to-all-start.5 = ((f32[32,8,4097]{2,1,0:T(8,128)}), f32[32,8,4097]{2,1,0:T(8,128)}, u32[]{:S(2)}, u32[]{:S(2)}) async-start(f32[32,8,4097]{2,1,0:T(8,128)} %pad_maximum_fusion), calls=%async_computation.5 | async-start | bytes 8650752 | tf_op jit(solution)/shard_map/all_to_all | solution.py:60
  452.0 3.9 collective-permute-start.13
  470.9 39.7 %collective-permute-done.13 = bf16[2,64,768]{2,1,0:T(8,128)(2,1)S(1)} collective-permute-done((bf16[2,64,768]{2,1,0:T(8,128)(2,1)}, bf16[2,64,768]{2,1,0:T(8,128)(2,1)S(1)}, u32[]{:S(2)}, u32[]{:S(2)}) %collective-permute-start.13) | collective-permute-done | bytes 196640 | tf_op jit(solution)/shard_map/ppermute | solution.py:96
  510.5 4.7 collective-permute-start.18
  516.0 6.0 collective-permute-start.19
  522.7 11.4 %collective-permute-start.20 = (bf16[2,64,768]{2,1,0:T(8,128)(2,1)}, bf16[2,64,768]{2,1,0:T(8,128)(2,1)S(1)}, u32[]{:S(2)}, u32[]{:S(2)}) collective-permute-start(bf16[2,64,768]{2,1,0:T(8,128)(2,1)} %pad_maximum_fusion.22), channel_id=1, source_target_pairs={{0,84},{4,88},{8,92},{12,96},{16,100},{20,104},{24,108},{28,112},{... | collective-permute-start | bytes 589832 | tf_op jit(solution)/shard_map/ppermute | solution.py:96
  534.8 12.6 %collective-permute-start.21 = (bf16[2,64,768]{2,1,0:T(8,128)(2,1)}, bf16[2,64,768]{2,1,0:T(8,128)(2,1)S(1)}, u32[]{:S(2)}, u32[]{:S(2)}) collective-permute-start(bf16[2,64,768]{2,1,0:T(8,128)(2,1)} %pad_maximum_fusion.23), channel_id=1, source_target_pairs={{0,88},{4,92},{8,96},{12,100},{16,104},{20,108},{24,112},{28,116},... | collective-permute-start | bytes 589832 | tf_op jit(solution)/shard_map/ppermute | solution.py:96
  555.9 10.9 %collective-permute-start.27 = (bf16[2,64,768]{2,1,0:T(8,128)(2,1)}, bf16[2,64,768]{2,1,0:T(8,128)(2,1)}, u32[]{:S(2)}, u32[]{:S(2)}) collective-permute-start(bf16[2,64,768]{2,1,0:T(8,128)(2,1)} %pad_maximum_fusion.29), channel_id=1, source_target_pairs={{0,112},{4,116},{8,120},{12,124},{16,0},{20,4},{24,8},{28,12},{32,... | collective-permute-start | bytes 589832 | tf_op jit(solution)/shard_map/ppermute | solution.py:96
  567.5 9.0 %collective-permute-start.28 = (bf16[2,64,768]{2,1,0:T(8,128)(2,1)}, bf16[2,64,768]{2,1,0:T(8,128)(2,1)}, u32[]{:S(2)}, u32[]{:S(2)}) collective-permute-start(bf16[2,64,768]{2,1,0:T(8,128)(2,1)} %pad_maximum_fusion.30), channel_id=1, source_target_pairs={{0,116},{4,120},{8,124},{12,0},{16,4},{20,8},{24,12},{28,16},{32,2... | collective-permute-start | bytes 589832 | tf_op jit(solution)/shard_map/ppermute | solution.py:96
  579.4 3.1 reduce_sum.114
  585.4 4.7 all-to-all-start.6
  598.2 6.5 %gather_fusion.4 = bf16[32,2,64,768]{3,2,1,0:T(8,128)(2,1)} fusion(bf16[31,2,64,768]{3,2,1,0:T(8,128)(2,1)} %bitcast_dynamic-update-slice_fusion, s32[1024]{0:T(1024)} %pad_clamp_fusion), kind=kCustom, calls=%fused_computation.4 | custom fusion | bytes 12583040 | tf_op jit(solution)/shard_map/gather | solution.py:107
  609.8 4.1 all-to-all-start.7
  613.9 5.8 fusion.4
  (291 shorter events, 290.8 us)
Async XLA Ops:
  76.0 212.3 %collective-permute-start = (bf16[2,64,768]{2,1,0:T(8,128)(2,1)}, bf16[2,64,768]{2,1,0:T(8,128)(2,1)}, u32[]{:S(2)}, u32[]{:S(2)}) collective-permute-start(bf16[2,64,768]{2,1,0:T(8,128)(2,1)} %pad_maximum_fusion.2), channel_id=1, source_target_pairs={{0,4},{4,8},{8,12},{12,16},{16,20},{20,24},{24,28},{28,32},{32,36}... | collective-permute-start | bytes 589832 | tf_op jit(solution)/shard_map/ppermute | solution.py:96
  76.8 216.2 %collective-permute-start.1 = (bf16[2,64,768]{2,1,0:T(8,128)(2,1)}, bf16[2,64,768]{2,1,0:T(8,128)(2,1)}, u32[]{:S(2)}, u32[]{:S(2)}) collective-permute-start(bf16[2,64,768]{2,1,0:T(8,128)(2,1)} %pad_maximum_fusion.3), channel_id=1, source_target_pairs={{0,8},{4,12},{8,16},{12,20},{16,24},{20,28},{24,32},{28,36},{32,40... | collective-permute-start | bytes 589832 | tf_op jit(solution)/shard_map/ppermute | solution.py:96
  79.1 216.7 %collective-permute-start.2 = (bf16[2,64,768]{2,1,0:T(8,128)(2,1)}, bf16[2,64,768]{2,1,0:T(8,128)(2,1)}, u32[]{:S(2)}, u32[]{:S(2)}) collective-permute-start(bf16[2,64,768]{2,1,0:T(8,128)(2,1)} %pad_maximum_fusion.4), channel_id=1, source_target_pairs={{0,12},{4,16},{8,20},{12,24},{16,28},{20,32},{24,36},{28,40},{32,4... | collective-permute-start | bytes 589832 | tf_op jit(solution)/shard_map/ppermute | solution.py:96
  81.9 275.7 %collective-permute-start.3 = (bf16[2,64,768]{2,1,0:T(8,128)(2,1)}, bf16[2,64,768]{2,1,0:T(8,128)(2,1)}, u32[]{:S(2)}, u32[]{:S(2)}) collective-permute-start(bf16[2,64,768]{2,1,0:T(8,128)(2,1)} %pad_maximum_fusion.5), channel_id=1, source_target_pairs={{0,16},{4,20},{8,24},{12,28},{16,32},{20,36},{24,40},{28,44},{32,4... | collective-permute-start | bytes 589832 | tf_op jit(solution)/shard_map/ppermute | solution.py:96
  85.6 314.0 %collective-permute-start.4 = (bf16[2,64,768]{2,1,0:T(8,128)(2,1)}, bf16[2,64,768]{2,1,0:T(8,128)(2,1)}, u32[]{:S(2)}, u32[]{:S(2)}) collective-permute-start(bf16[2,64,768]{2,1,0:T(8,128)(2,1)} %pad_maximum_fusion.6), channel_id=1, source_target_pairs={{0,20},{4,24},{8,28},{12,32},{16,36},{20,40},{24,44},{28,48},{32,5... | collective-permute-start | bytes 589832 | tf_op jit(solution)/shard_map/ppermute | solution.py:96
  92.7 170.0 %all-to-all-start = ((f32[32,8,2305]{2,1,0:T(8,128)}), f32[32,8,2305]{2,1,0:T(8,128)}, u32[]{:S(2)}, u32[]{:S(2)}) async-start(f32[32,8,2305]{2,1,0:T(8,128)} %pad_maximum_fusion.1), calls=%async_computation | async-start | bytes 4980736 | tf_op jit(solution)/shard_map/all_to_all | solution.py:60
  278.7 26.8 %all-to-all-start.1 = ((bf16[32,8,2304]{2,1,0:T(8,128)(2,1)}), bf16[32,8,2304]{2,1,0:T(8,128)(2,1)}, u32[]{:S(2)}, u32[]{:S(2)}) async-start(bf16[32,8,2304]{2,1,0:T(8,128)(2,1)} %broadcast_in_dim.95), calls=%async_computation.1 | async-start | bytes 2359296 | tf_op jit(solution)/shard_map/all_to_all | solution.py:79
  288.4 115.5 %collective-permute-start.5 = (bf16[2,64,768]{2,1,0:T(8,128)(2,1)}, bf16[2,64,768]{2,1,0:T(8,128)(2,1)}, u32[]{:S(2)}, u32[]{:S(2)}) collective-permute-start(bf16[2,64,768]{2,1,0:T(8,128)(2,1)} %pad_maximum_fusion.7), channel_id=1, source_target_pairs={{0,24},{4,28},{8,32},{12,36},{16,40},{20,44},{24,48},{28,52},{32,5... | collective-permute-start | bytes 589832 | tf_op jit(solution)/shard_map/ppermute | solution.py:96
  292.9 129.8 %collective-permute-start.6 = (bf16[2,64,768]{2,1,0:T(8,128)(2,1)}, bf16[2,64,768]{2,1,0:T(8,128)(2,1)}, u32[]{:S(2)}, u32[]{:S(2)}) collective-permute-start(bf16[2,64,768]{2,1,0:T(8,128)(2,1)} %pad_maximum_fusion.8), channel_id=1, source_target_pairs={{0,28},{4,32},{8,36},{12,40},{16,44},{20,48},{24,52},{28,56},{32,6... | collective-permute-start | bytes 589832 | tf_op jit(solution)/shard_map/ppermute | solution.py:96
  295.7 129.9 %collective-permute-start.7 = (bf16[2,64,768]{2,1,0:T(8,128)(2,1)}, bf16[2,64,768]{2,1,0:T(8,128)(2,1)}, u32[]{:S(2)}, u32[]{:S(2)}) collective-permute-start(bf16[2,64,768]{2,1,0:T(8,128)(2,1)} %pad_maximum_fusion.9), channel_id=1, source_target_pairs={{0,32},{4,36},{8,40},{12,44},{16,48},{20,52},{24,56},{28,60},{32,6... | collective-permute-start | bytes 589832 | tf_op jit(solution)/shard_map/ppermute | solution.py:96
  352.9 21.9 %all-to-all-start.2 = ((f32[32,4,2,8,98]{4,3,2,1,0:T(8,128)}), f32[32,4,2,8,98]{4,3,2,1,0:T(8,128)}, u32[]{:S(2)}, u32[]{:S(2)}) async-start(f32[32,4,2,8,98]{4,3,2,1,0:T(8,128)} %maximum_bitcast_fusion), calls=%async_computation.2 | async-start | bytes 2097152 | tf_op jit(solution)/shard_map/all_to_all | solution.py:212
  357.5 94.5 %collective-permute-start.8 = (bf16[2,64,768]{2,1,0:T(8,128)(2,1)}, bf16[2,64,768]{2,1,0:T(8,128)(2,1)}, u32[]{:S(2)}, u32[]{:S(2)}) collective-permute-start(bf16[2,64,768]{2,1,0:T(8,128)(2,1)} %pad_maximum_fusion.10), channel_id=1, source_target_pairs={{0,36},{4,40},{8,44},{12,48},{16,52},{20,56},{24,60},{28,64},{32,6... | collective-permute-start | bytes 589832 | tf_op jit(solution)/shard_map/ppermute | solution.py:96
  399.6 57.9 %collective-permute-start.9 = (bf16[2,64,768]{2,1,0:T(8,128)(2,1)}, bf16[2,64,768]{2,1,0:T(8,128)(2,1)}, u32[]{:S(2)}, u32[]{:S(2)}) collective-permute-start(bf16[2,64,768]{2,1,0:T(8,128)(2,1)} %pad_maximum_fusion.11), channel_id=1, source_target_pairs={{0,40},{4,44},{8,48},{12,52},{16,56},{20,60},{24,64},{28,68},{32,7... | collective-permute-start | bytes 589832 | tf_op jit(solution)/shard_map/ppermute | solution.py:96
  403.9 57.1 %collective-permute-start.10 = (bf16[2,64,768]{2,1,0:T(8,128)(2,1)}, bf16[2,64,768]{2,1,0:T(8,128)(2,1)}, u32[]{:S(2)}, u32[]{:S(2)}) collective-permute-start(bf16[2,64,768]{2,1,0:T(8,128)(2,1)} %pad_maximum_fusion.12), channel_id=1, source_target_pairs={{0,44},{4,48},{8,52},{12,56},{16,60},{20,64},{24,68},{28,72},{32,7... | collective-permute-start | bytes 589832 | tf_op jit(solution)/shard_map/ppermute | solution.py:96
  422.7 42.0 %collective-permute-start.11 = (bf16[2,64,768]{2,1,0:T(8,128)(2,1)}, bf16[2,64,768]{2,1,0:T(8,128)(2,1)}, u32[]{:S(2)}, u32[]{:S(2)}) collective-permute-start(bf16[2,64,768]{2,1,0:T(8,128)(2,1)} %pad_maximum_fusion.13), channel_id=1, source_target_pairs={{0,48},{4,52},{8,56},{12,60},{16,64},{20,68},{24,72},{28,76},{32,8... | collective-permute-start | bytes 589832 | tf_op jit(solution)/shard_map/ppermute | solution.py:96
  425.6 42.6 %collective-permute-start.12 = (bf16[2,64,768]{2,1,0:T(8,128)(2,1)}, bf16[2,64,768]{2,1,0:T(8,128)(2,1)}, u32[]{:S(2)}, u32[]{:S(2)}) collective-permute-start(bf16[2,64,768]{2,1,0:T(8,128)(2,1)} %pad_maximum_fusion.14), channel_id=1, source_target_pairs={{0,52},{4,56},{8,60},{12,64},{16,68},{20,72},{24,76},{28,80},{32,8... | collective-permute-start | bytes 589832 | tf_op jit(solution)/shard_map/ppermute | solution.py:96
  442.3 137.2 %all-to-all-start.5 = ((f32[32,8,4097]{2,1,0:T(8,128)}), f32[32,8,4097]{2,1,0:T(8,128)}, u32[]{:S(2)}, u32[]{:S(2)}) async-start(f32[32,8,4097]{2,1,0:T(8,128)} %pad_maximum_fusion), calls=%async_computation.5 | async-start | bytes 8650752 | tf_op jit(solution)/shard_map/all_to_all | solution.py:60
  452.0 58.5 %collective-permute-start.13 = (bf16[2,64,768]{2,1,0:T(8,128)(2,1)}, bf16[2,64,768]{2,1,0:T(8,128)(2,1)S(1)}, u32[]{:S(2)}, u32[]{:S(2)}) collective-permute-start(bf16[2,64,768]{2,1,0:T(8,128)(2,1)} %pad_maximum_fusion.15), channel_id=1, source_target_pairs={{0,56},{4,60},{8,64},{12,68},{16,72},{20,76},{24,80},{28,84},{32,8... | collective-permute-start | bytes 589832 | tf_op jit(solution)/shard_map/ppermute | solution.py:96
  457.5 58.4 %collective-permute-start.14 = (bf16[2,64,768]{2,1,0:T(8,128)(2,1)}, bf16[2,64,768]{2,1,0:T(8,128)(2,1)S(1)}, u32[]{:S(2)}, u32[]{:S(2)}) collective-permute-start(bf16[2,64,768]{2,1,0:T(8,128)(2,1)} %pad_maximum_fusion.16), channel_id=1, source_target_pairs={{0,60},{4,64},{8,68},{12,72},{16,76},{20,80},{24,84},{28,88},{32,9... | collective-permute-start | bytes 589832 | tf_op jit(solution)/shard_map/ppermute | solution.py:96
  461.0 61.7 %collective-permute-start.15 = (bf16[2,64,768]{2,1,0:T(8,128)(2,1)}, bf16[2,64,768]{2,1,0:T(8,128)(2,1)S(1)}, u32[]{:S(2)}, u32[]{:S(2)}) collective-permute-start(bf16[2,64,768]{2,1,0:T(8,128)(2,1)} %pad_maximum_fusion.17), channel_id=1, source_target_pairs={{0,64},{4,68},{8,72},{12,76},{16,80},{20,84},{24,88},{28,92},{32,9... | collective-permute-start | bytes 589832 | tf_op jit(solution)/shard_map/ppermute | solution.py:96
  464.7 70.1 %collective-permute-start.16 = (bf16[2,64,768]{2,1,0:T(8,128)(2,1)}, bf16[2,64,768]{2,1,0:T(8,128)(2,1)S(1)}, u32[]{:S(2)}, u32[]{:S(2)}) collective-permute-start(bf16[2,64,768]{2,1,0:T(8,128)(2,1)} %pad_maximum_fusion.18), channel_id=1, source_target_pairs={{0,68},{4,72},{8,76},{12,80},{16,84},{20,88},{24,92},{28,96},{32,1... | collective-permute-start | bytes 589832 | tf_op jit(solution)/shard_map/ppermute | solution.py:96
  468.2 79.9 %collective-permute-start.17 = (bf16[2,64,768]{2,1,0:T(8,128)(2,1)}, bf16[2,64,768]{2,1,0:T(8,128)(2,1)S(1)}, u32[]{:S(2)}, u32[]{:S(2)}) collective-permute-start(bf16[2,64,768]{2,1,0:T(8,128)(2,1)} %pad_maximum_fusion.19), channel_id=1, source_target_pairs={{0,72},{4,76},{8,80},{12,84},{16,88},{20,92},{24,96},{28,100},{32,... | collective-permute-start | bytes 589832 | tf_op jit(solution)/shard_map/ppermute | solution.py:96
  510.5 38.4 %collective-permute-start.18 = (bf16[2,64,768]{2,1,0:T(8,128)(2,1)}, bf16[2,64,768]{2,1,0:T(8,128)(2,1)S(1)}, u32[]{:S(2)}, u32[]{:S(2)}) collective-permute-start(bf16[2,64,768]{2,1,0:T(8,128)(2,1)} %pad_maximum_fusion.20), channel_id=1, source_target_pairs={{0,76},{4,80},{8,84},{12,88},{16,92},{20,96},{24,100},{28,104},{32... | collective-permute-start | bytes 589832 | tf_op jit(solution)/shard_map/ppermute | solution.py:96
  516.0 33.6 %collective-permute-start.19 = (bf16[2,64,768]{2,1,0:T(8,128)(2,1)}, bf16[2,64,768]{2,1,0:T(8,128)(2,1)S(1)}, u32[]{:S(2)}, u32[]{:S(2)}) collective-permute-start(bf16[2,64,768]{2,1,0:T(8,128)(2,1)} %pad_maximum_fusion.21), channel_id=1, source_target_pairs={{0,80},{4,84},{8,88},{12,92},{16,96},{20,100},{24,104},{28,108},{3... | collective-permute-start | bytes 589832 | tf_op jit(solution)/shard_map/ppermute | solution.py:96
  522.7 30.3 %collective-permute-start.20 = (bf16[2,64,768]{2,1,0:T(8,128)(2,1)}, bf16[2,64,768]{2,1,0:T(8,128)(2,1)S(1)}, u32[]{:S(2)}, u32[]{:S(2)}) collective-permute-start(bf16[2,64,768]{2,1,0:T(8,128)(2,1)} %pad_maximum_fusion.22), channel_id=1, source_target_pairs={{0,84},{4,88},{8,92},{12,96},{16,100},{20,104},{24,108},{28,112},{... | collective-permute-start | bytes 589832 | tf_op jit(solution)/shard_map/ppermute | solution.py:96
  534.8 19.0 %collective-permute-start.21 = (bf16[2,64,768]{2,1,0:T(8,128)(2,1)}, bf16[2,64,768]{2,1,0:T(8,128)(2,1)S(1)}, u32[]{:S(2)}, u32[]{:S(2)}) collective-permute-start(bf16[2,64,768]{2,1,0:T(8,128)(2,1)} %pad_maximum_fusion.23), channel_id=1, source_target_pairs={{0,88},{4,92},{8,96},{12,100},{16,104},{20,108},{24,112},{28,116},... | collective-permute-start | bytes 589832 | tf_op jit(solution)/shard_map/ppermute | solution.py:96
  549.6 27.6 %collective-permute-start.24 = (bf16[2,64,768]{2,1,0:T(8,128)(2,1)}, bf16[2,64,768]{2,1,0:T(8,128)(2,1)S(1)}, u32[]{:S(2)}, u32[]{:S(2)}) collective-permute-start(bf16[2,64,768]{2,1,0:T(8,128)(2,1)} %pad_maximum_fusion.26), channel_id=1, source_target_pairs={{0,100},{4,104},{8,108},{12,112},{16,116},{20,120},{24,124},{28,0}... | collective-permute-start | bytes 589832 | tf_op jit(solution)/shard_map/ppermute | solution.py:96
  553.0 24.9 %collective-permute-start.25 = (bf16[2,64,768]{2,1,0:T(8,128)(2,1)}, bf16[2,64,768]{2,1,0:T(8,128)(2,1)S(1)}, u32[]{:S(2)}, u32[]{:S(2)}) collective-permute-start(bf16[2,64,768]{2,1,0:T(8,128)(2,1)} %pad_maximum_fusion.27), channel_id=1, source_target_pairs={{0,104},{4,108},{8,112},{12,116},{16,120},{20,124},{24,0},{28,4},{... | collective-permute-start | bytes 589832 | tf_op jit(solution)/shard_map/ppermute | solution.py:96
  553.7 36.4 %collective-permute-start.26 = (bf16[2,64,768]{2,1,0:T(8,128)(2,1)}, bf16[2,64,768]{2,1,0:T(8,128)(2,1)}, u32[]{:S(2)}, u32[]{:S(2)}) collective-permute-start(bf16[2,64,768]{2,1,0:T(8,128)(2,1)} %pad_maximum_fusion.28), channel_id=1, source_target_pairs={{0,108},{4,112},{8,116},{12,120},{16,124},{20,0},{24,4},{28,8},{32... | collective-permute-start | bytes 589832 | tf_op jit(solution)/shard_map/ppermute | solution.py:96
  555.9 35.8 %collective-permute-start.27 = (bf16[2,64,768]{2,1,0:T(8,128)(2,1)}, bf16[2,64,768]{2,1,0:T(8,128)(2,1)}, u32[]{:S(2)}, u32[]{:S(2)}) collective-permute-start(bf16[2,64,768]{2,1,0:T(8,128)(2,1)} %pad_maximum_fusion.29), channel_id=1, source_target_pairs={{0,112},{4,116},{8,120},{12,124},{16,0},{20,4},{24,8},{28,12},{32,... | collective-permute-start | bytes 589832 | tf_op jit(solution)/shard_map/ppermute | solution.py:96
  567.5 25.9 %collective-permute-start.28 = (bf16[2,64,768]{2,1,0:T(8,128)(2,1)}, bf16[2,64,768]{2,1,0:T(8,128)(2,1)}, u32[]{:S(2)}, u32[]{:S(2)}) collective-permute-start(bf16[2,64,768]{2,1,0:T(8,128)(2,1)} %pad_maximum_fusion.30), channel_id=1, source_target_pairs={{0,116},{4,120},{8,124},{12,0},{16,4},{20,8},{24,12},{28,16},{32,2... | collective-permute-start | bytes 589832 | tf_op jit(solution)/shard_map/ppermute | solution.py:96
  585.4 21.9 %all-to-all-start.6 = ((bf16[32,8,2048]{2,1,0:T(8,128)(2,1)}), bf16[32,8,2048]{2,1,0:T(8,128)(2,1)}, u32[]{:S(2)}, u32[]{:S(2)}) async-start(bf16[32,8,2048]{2,1,0:T(8,128)(2,1)} %broadcast_in_dim.166), calls=%async_computation.6 | async-start | bytes 2097152 | tf_op jit(solution)/shard_map/all_to_all | solution.py:79
  (25 other events, 1409.8 us)

commit v7 on v5

--- a/solution.py
+++ b/solution.py
@@ -51,14 +51,14 @@
     )
 
 
-def reduce_rows(partial_value, squares, finish, tied=None):
+def reduce_rows(partial_value, squares, finish, tied=None, carrier=jnp.float32):
     rows = partial_value.shape[0]
     holders = lax.axis_size("pages")
     block = rows // holders
     packed = jnp.concatenate([partial_value.reshape(rows, -1), squares[:, None]], axis=1)
-    packed = packed.reshape(holders, block, packed.shape[1])
+    packed = packed.reshape(holders, block, packed.shape[1]).astype(carrier)
     packed = lax.all_to_all(packed, "pages", split_axis=0, concat_axis=0, tiled=True)
-    packed = jnp.sum(packed, axis=0)
+    packed = jnp.sum(packed.astype(jnp.float32), axis=0)
     start = lax.axis_index("pages") * block
     done = finish(packed[:, :-1].reshape((block,) + partial_value.shape[1:]), packed[:, -1], start)
     width = [part.shape[1] for part in done]
@@ -257,7 +257,7 @@
         "bd,gdf->bgf", normed_two, w_gate_up, preferred_element_type=jnp.float32
     )
     squares_two = jnp.sum(mixed * mixed, axis=1)
-    (hidden,) = reduce_rows(partial_two, squares_two, finish_mlp)
+    (hidden,) = reduce_rows(partial_two, squares_two, finish_mlp, carrier=jnp.bfloat16)
     feed = across_heads(
         lax.dot_general(hidden, w_down, CONTRACT_LAST, preferred_element_type=jnp.float32)
     )

time: 356 us -> 329 us (0.924)
  blocking collectives: 71.6 us -> 48.5 us
    all_to_all x1, blocking collectives: 56.6 us -> 33.5 us  [reduce_rows(): lax.all_to_all(packed, 'pages', split_axis=0, concat_axis=0, tiled=True)]
  transfers between devices with their start and end apart: 7 -> 7, of which waited for: 7 -> 7; matrix products, arithmetic and copies ran while one was open for 30% -> 33% of each run, Pallas kernels for 0% -> 0%
where the time goes in v7:
time: 329 us; the launch traced here: 326 us
  local copies, waits for them, and re-layouts  99.6 us (30%)
  waiting for transfers between devices  74.3 us (23%)
  blocking collectives  48.5 us (15%)
  other arithmetic  47.4 us (14%)
  starting transfers between devices  36.3 us (11%)
  matrix products  19 us (6%)
    all_to_all x1, blocking collectives, reduce_rows(): lax.all_to_all(packed, 'pages', split_axis=0, concat_axis=0, tiled=True)  33.5 us
    all_to_all x1, waiting for transfers between devices, reduce_rows(): lax.all_to_all(packed, 'pages', split_axis=0, concat_axis=0, tiled=True)  31.6 us
    all_to_all x1, waiting for transfers between devices, exchange_pool(): lax.all_to_all(both, 'pages', split_axis=0, concat_axis=0, tiled=True)  19.8 us
    all_to_all x4, starting transfers between devices, gather_blocks(): return lax.all_to_all(spread, axis, split_axis=0, concat_axis=0, tiled=True)  18.7 us
    all_to_all x4, waiting for transfers between devices, gather_blocks(): return lax.all_to_all(spread, axis, split_axis=0, concat_axis=0, tiled=True)  16.9 us
    all_to_all x1, blocking collectives, gather_blocks(): return lax.all_to_all(spread, axis, split_axis=0, concat_axis=0, tiled=True)  15 us
    reshape x1, local copies, waits for them, and re-layouts, local_attention(): values_here = v_cache.reshape(slot_count, page_len, heads_here, head_dim)  8.24 us
    all_to_all x1, starting transfers between devices, reduce_rows(): lax.all_to_all(packed, 'pages', split_axis=0, concat_axis=0, tiled=True)  7.57 us
  transfers between devices with their start and end apart: 7, of which 7 were waited for; matrix products, arithmetic and copies ran while one was open for 33% of the time, Pallas kernels for 0%

profile of v7, /device:TPU:0, one launch (start us, length us, event | category | flops | bytes accessed | tf_op | source)
XLA Modules:
  0.0 326.2 jit_solution(7566795568249857272)
XLA Ops:
  7.0 7.6 %all-to-all-start = ((f32[32,8,2305]{2,1,0:T(8,128)}), f32[32,8,2305]{2,1,0:T(8,128)S(1)}, u32[]{:S(2)}, u32[]{:S(2)}) async-start(f32[32,8,2305]{2,1,0:T(8,128)} %pad_maximum_fusion.1), calls=%async_computation | async-start | bytes 4980736 | tf_op jit(solution)/shard_map/all_to_all | solution.py:60
  17.7 31.6 %all-to-all-done = f32[32,8,2305]{2,1,0:T(8,128)S(1)} async-done(((f32[32,8,2305]{2,1,0:T(8,128)}), f32[32,8,2305]{2,1,0:T(8,128)S(1)}, u32[]{:S(2)}, u32[]{:S(2)}) %all-to-all-start) | async-done | bytes 2360352 | tf_op jit(solution)/shard_map/all_to_all | solution.py:60
  51.3 4.7 %all-to-all-start.1 = ((bf16[32,8,2304]{2,1,0:T(8,128)(2,1)}), bf16[32,8,2304]{2,1,0:T(8,128)(2,1)}, u32[]{:S(2)}, u32[]{:S(2)}) async-start(bf16[32,8,2304]{2,1,0:T(8,128)(2,1)} %broadcast_in_dim.186), calls=%async_computation.1 | async-start | bytes 2359296 | tf_op jit(solution)/shard_map/all_to_all | solution.py:79
  56.6 4.4 %gather_fusion.3 = bf16[32,64,768]{2,1,0:T(8,128)(2,1)} fusion(bf16[32,64,768]{2,1,0:T(8,128)(2,1)} %param.20, s32[1024]{0:T(1024)S(1)} %pad_clamp_fusion.1), kind=kCustom, calls=%fused_computation.3 | custom fusion | bytes 6291584 | tf_op jit(solution)/shard_map/gather | solution.py:96
  61.0 2.4 gather_fusion.2
  63.6 3.3 %bitcast_select_fusion.1 = (bf16[32,1,64,768]{3,2,1,0:T(8,128)(2,1)S(1)}, bf16[32,1,64,768]{3,2,1,0:T(8,128)(2,1)S(1)}) fusion(bf16[32,64,768]{2,1,0:T(8,128)(2,1)} %gather_fusion.2, pred[32]{0:T(512)(128)(4,1)S(1)} %fusion.45, bf16[32,64,768]{2,1,0:T(8,128)(2,1)} %gather_fusion.3), kind=kLoop, calls=%fused_computation.18 | loop fusion | flops 3145728 | bytes 12582944 | tf_op jit(solution)/shard_map/jit(_where)/select_n | solution.py:95
  66.9 3.2 pad_maximum_fusion
  70.1 4.6 %all-to-all-done.1 = bf16[32,8,2304]{2,1,0:T(8,128)(2,1)} async-done(((bf16[32,8,2304]{2,1,0:T(8,128)(2,1)}), bf16[32,8,2304]{2,1,0:T(8,128)(2,1)}, u32[]{:S(2)}, u32[]{:S(2)}) %all-to-all-start.1) | async-done | bytes 1179680 | tf_op jit(solution)/shard_map/all_to_all | solution.py:79
  77.0 5.1 %all-to-all-start.2 = ((bf16[32,2,64,768]{3,2,1,0:T(8,128)(2,1)}), bf16[32,2,64,768]{3,2,1,0:T(8,128)(2,1)}, u32[]{:S(2)}, u32[]{:S(2)}) async-start(bf16[32,2,64,768]{3,2,1,0:T(8,128)(2,1)} %pad_maximum_fusion), calls=%async_computation.2 | async-start | bytes 12582912 | tf_op jit(solution)/shard_map/all_to_all | solution.py:101
  82.0 5.4 %reshape.375 = bf16[32,64,8,96]{3,2,1,0:T(8,128)(2,1)} reshape(bf16[32,64,768]{2,1,0:T(8,128)(2,1)S(1)} %copy-done.2) | data formatting | bytes 6291456 | tf_op jit(solution)/shard_map/reshape | solution.py:130
  87.5 8.2 %reshape.376 = bf16[32,64,8,96]{3,2,1,0:T(8,128)(2,1)} reshape(bf16[32,64,768]{2,1,0:T(8,128)(2,1)} %param.20) | data formatting | bytes 6291456 | tf_op jit(solution)/shard_map/reshape | solution.py:131
  104.6 6.0 %fusion.71 = (f32[4,32,8]{0,2,1:T(8,128)}, f32[4,32,8,64]{3,0,2,1:T(4,128)}) fusion(bf16[32,64,8,96]{3,2,1,0:T(8,128)(2,1)} %reshape.375, bf16[4,32,8,96]{3,2,0,1:T(8,128)(2,1)} %bitcast.138, pred[32,64]{1,0:T(8,128)(4,1)S(1)} %fusion.46), kind=kOutput, calls=%fused_computation.150 | convolution fusion | flops 12778496 | bytes 3610624 | tf_op jit(solution)/shard_map/tshd,skhd->tshk/dot_general | solution.py:133
  119.0 2.4 fusion.21
  126.1 3.4 %copy.241 = f32[4,32,2,8,1]{4,3,2,0,1:T(8,128)} copy(f32[4,32,2,8,1]{3,2,1,0,4:T(2,128)} %bitcast.134) | data formatting | bytes 16384 | tf_op jit(solution)/shard_map/concatenate | solution.py:217
  129.5 3.4 %copy.242 = f32[4,32,2,8,1]{4,3,2,0,1:T(8,128)} copy(f32[4,32,2,8,1]{3,2,1,0,4:T(2,128)} %bitcast.133) | data formatting | bytes 16384 | tf_op jit(solution)/shard_map/concatenate | solution.py:217
  133.0 3.7 %fusion.4 = f32[4,32,8,96]{3,0,2,1:T(4,128)S(1)} fusion(bf16[32,64,8,96]{3,2,1,0:T(8,128)(2,1)} %reshape.376, f32[4,32,8,64]{3,0,2,1:T(4,128)} %get-tuple-element.54, f32[4,32,8]{0,2,1:T(8,128)} %copy.234, pred[32,64]{1,0:T(8,128)(4,1)S(1)} %copy-done.7), kind=kOutput, calls=%fused_computation.23 | convolution fusion | flops 12779520 | bytes 3807232 | tf_op jit(solution)/shard_map/tshk,skhd->tshd/dot_general | solution.py:147
  139.9 19.8 %all-to-all-done.2 = bf16[32,2,64,768]{3,2,1,0:T(8,128)(2,1)} async-done(((bf16[32,2,64,768]{3,2,1,0:T(8,128)(2,1)}), bf16[32,2,64,768]{3,2,1,0:T(8,128)(2,1)}, u32[]{:S(2)}, u32[]{:S(2)}) %all-to-all-start.2) | async-done | bytes 6291488 | tf_op jit(solution)/shard_map/all_to_all | solution.py:101
  159.8 6.3 %slice_bitcast_fusion = (bf16[32,64,768]{2,1,0:T(8,128)(2,1)}, bf16[32,64,768]{2,1,0:T(8,128)(2,1)}) fusion(bf16[32,2,64,768]{3,2,1,0:T(8,128)(2,1)} %all-to-all-done.2), kind=kLoop, calls=%fused_computation.15 | loop fusion | bytes 12582912 | tf_op jit(solution)/shard_map/squeeze | solution.py:102
  166.0 4.9 %all-to-all-start.3 = ((f32[32,4,2,8,98]{4,3,2,1,0:T(8,128)}), f32[32,4,2,8,98]{4,3,2,1,0:T(8,128)}, u32[]{:S(2)}, u32[]{:S(2)}) async-start(f32[32,4,2,8,98]{4,3,2,1,0:T(8,128)} %maximum_bitcast_fusion), calls=%async_computation.3 | async-start | bytes 2097152 | tf_op jit(solution)/shard_map/all_to_all | solution.py:222
  181.9 6.0 %all-to-all-done.3 = f32[32,4,2,8,98]{4,3,2,1,0:T(8,128)} async-done(((f32[32,4,2,8,98]{4,3,2,1,0:T(8,128)}), f32[32,4,2,8,98]{4,3,2,1,0:T(8,128)}, u32[]{:S(2)}, u32[]{:S(2)}) %all-to-all-start.3) | async-done | bytes 802848 | tf_op jit(solution)/shard_map/all_to_all | solution.py:222
  187.9 4.1 %fusion.69 = (f32[32,4,2,8,1]{4,3,2,1,0:T(8,128)}, f32[4,2,8]{2,1,0:T(2,128)}, f32[32,4,2,8,1]{4,3,2,1,0:T(8,128)}) fusion(f32[32,4,2,8,98]{4,3,2,1,0:T(8,128)} %all-to-all-done.3), kind=kLoop, calls=%fused_computation.148 | loop fusion | flops 1984 | bytes 33024 | tf_op jit(solution)/shard_map/slice | solution.py:224
  208.6 15.0 %all_to_all.45 = bf16[32,4,2,8,96]{4,3,2,1,0:T(8,128)(2,1)S(1)} all-to-all(bf16[32,4,2,8,96]{4,3,2,1,0:T(8,128)(2,1)S(1)} %broadcast_in_dim.200), channel_id=1, replica_groups=mesh['pages'=32,'mp'=4] {'pages'}, dimensions={0} | all-to-all | bytes 786432 | tf_op jit(solution)/shard_map/all_to_all | solution.py:79
  228.8 5.3 %all-to-all-start.5 = ((f32[4,256,96]{1,2,0:T(8,128)}), f32[4,256,96]{1,2,0:T(8,128)}, u32[]{:S(2)}, u32[]{:S(2)}) async-start(f32[4,256,96]{1,2,0:T(8,128)} %broadcast_in_dim.201), calls=%async_computation.5 | async-start | bytes 786432 | tf_op jit(solution)/shard_map/all_to_all | solution.py:79
  234.1 2.8 copy.264
  237.0 3.2 reshape.452
  251.2 33.5 %all_to_all.46 = bf16[32,8,4097]{2,1,0:T(8,128)(2,1)S(1)} all-to-all(bf16[32,8,4097]{2,1,0:T(8,128)(2,1)S(1)} %pad_maximum_fusion.2), channel_id=1, replica_groups=mesh['pages'=32,'mp'=4] {'pages'}, dimensions={0} | all-to-all | bytes 4195328 | tf_op jit(solution)/shard_map/all_to_all | solution.py:60
  286.3 4.7 %all-to-all-start.7 = ((bf16[32,8,2048]{2,1,0:T(8,128)(2,1)}), bf16[32,8,2048]{2,1,0:T(8,128)(2,1)}, u32[]{:S(2)}, u32[]{:S(2)}) async-start(bf16[32,8,2048]{2,1,0:T(8,128)(2,1)} %broadcast_in_dim.202), calls=%async_computation.7 | async-start | bytes 2097152 | tf_op jit(solution)/shard_map/all_to_all | solution.py:79
  291.1 4.3 %gather_fusion.6 = bf16[32,64,768]{2,1,0:T(8,128)(2,1)} fusion(bf16[32,64,768]{2,1,0:T(8,128)(2,1)} %get-tuple-element.15, s32[1024]{0:T(1024)S(1)} %pad_clamp_fusion), kind=kCustom, calls=%fused_computation.6 | custom fusion | bytes 6291584 | tf_op jit(solution)/shard_map/gather | solution.py:115
  295.5 4.3 %gather_fusion.7 = bf16[32,64,768]{2,1,0:T(8,128)(2,1)} fusion(bf16[32,64,768]{2,1,0:T(8,128)(2,1)} %get-tuple-element.16, s32[1024]{0:T(1024)S(1)} %pad_clamp_fusion), kind=kCustom, calls=%fused_computation.7 | custom fusion | bytes 6291584 | tf_op jit(solution)/shard_map/gather | solution.py:116
  299.8 8.4 %all-to-all-done.7 = bf16[32,8,2048]{2,1,0:T(8,128)(2,1)} async-done(((bf16[32,8,2048]{2,1,0:T(8,128)(2,1)}), bf16[32,8,2048]{2,1,0:T(8,128)(2,1)}, u32[]{:S(2)}, u32[]{:S(2)}) %all-to-all-start.7) | async-done | bytes 1048608 | tf_op jit(solution)/shard_map/all_to_all | solution.py:79
  310.6 4.1 %all-to-all-start.8 = ((f32[4,256,96]{1,2,0:T(8,128)}), f32[4,256,96]{1,2,0:T(8,128)}, u32[]{:S(2)}, u32[]{:S(2)}) async-start(f32[4,256,96]{1,2,0:T(8,128)} %broadcast_in_dim.203), calls=%async_computation.8 | async-start | bytes 786432 | tf_op jit(solution)/shard_map/all_to_all | solution.py:79
  314.8 7.1 %broadcast_select_fusion = (bf16[32,64,768]{2,1,0:T(8,128)(2,1)}, bf16[32,64,768]{2,1,0:T(8,128)(2,1)}) fusion(bf16[32,64,768]{2,1,0:T(8,128)(2,1)} %gather_fusion.7, bf16[32,64,768]{2,1,0:T(8,128)(2,1)} %param.20, pred[32]{0:T(512)(128)(4,1)S(1)} %fusion.44, bf16[32,64,768]{2,1,0:T(8,128)(2,1)} %gather_fusion.6, bf16[32,64,768]{2,1,0:T(8,128)(2,1)S(1)} %copy-done.2), kind=kLoop, calls=%fused_computation.19 | loop fusion | flops 3145728 | bytes 18874400 | tf_op jit(solution)/shard_map/jit(_where)/select_n | solution.py:116
  (135 shorter events, 91.8 us)
Async XLA Ops:
  0.6 307.6 %copy-start = (bf16[96,2048]{1,0:T(8,128)(2,1)S(1)}, bf16[96,2048]{1,0:T(8,128)(2,1)}, u32[]{:S(2)}) copy-start(bf16[96,2048]{1,0:T(8,128)(2,1)} %param.18) | copy-start | bytes 1179652
  7.0 7.6 %copy-start.1 = (s32[64]{0:T(128)S(1)}, s32[64]{0:T(128)}, u32[]{:S(2)}) copy-start(s32[64]{0:T(128)} %param.21) | copy-start | bytes 772
  7.0 10.3 %copy-start.15 = (s32[31]{0:T(128)S(1)}, s32[31]{0:T(128)}, u32[]{:S(2)}) copy-start(s32[31]{0:T(128)} %param.25) | copy-start | bytes 376
  7.0 42.3 %all-to-all-start = ((f32[32,8,2305]{2,1,0:T(8,128)}), f32[32,8,2305]{2,1,0:T(8,128)S(1)}, u32[]{:S(2)}, u32[]{:S(2)}) async-start(f32[32,8,2305]{2,1,0:T(8,128)} %pad_maximum_fusion.1), calls=%async_computation | async-start | bytes 4980736 | tf_op jit(solution)/shard_map/all_to_all | solution.py:60
  17.2 0.5 copy-start.13
  51.3 23.4 %all-to-all-start.1 = ((bf16[32,8,2304]{2,1,0:T(8,128)(2,1)}), bf16[32,8,2304]{2,1,0:T(8,128)(2,1)}, u32[]{:S(2)}, u32[]{:S(2)}) async-start(bf16[32,8,2304]{2,1,0:T(8,128)(2,1)} %broadcast_in_dim.186), calls=%async_computation.1 | async-start | bytes 2359296 | tf_op jit(solution)/shard_map/all_to_all | solution.py:79
  56.6 4.5 %copy-start.2 = (bf16[32,64,768]{2,1,0:T(8,128)(2,1)S(1)}, bf16[32,64,768]{2,1,0:T(8,128)(2,1)}, u32[]{:S(2)}) copy-start(bf16[32,64,768]{2,1,0:T(8,128)(2,1)} %param.19) | copy-start | bytes 9437188
  77.0 82.8 %all-to-all-start.2 = ((bf16[32,2,64,768]{3,2,1,0:T(8,128)(2,1)}), bf16[32,2,64,768]{3,2,1,0:T(8,128)(2,1)}, u32[]{:S(2)}, u32[]{:S(2)}) async-start(bf16[32,2,64,768]{3,2,1,0:T(8,128)(2,1)} %pad_maximum_fusion), calls=%async_computation.2 | async-start | bytes 12582912 | tf_op jit(solution)/shard_map/all_to_all | solution.py:101
  96.5 14.2 %copy-start.9 = (s32[32]{0:T(128)}, s32[32]{0:T(128)S(1)}, u32[]{:S(2)}) copy-start(s32[32]{0:T(128)S(1)} %get-tuple-element.20) | copy-start | bytes 388
  96.5 14.2 %copy-start.8 = (s32[1024]{0:T(1024)}, s32[1024]{0:T(1024)S(1)}, u32[]{:S(2)}) copy-start(s32[1024]{0:T(1024)S(1)} %pad_clamp_fusion.3) | copy-start | bytes 12292
  99.9 10.8 %copy-start.6 = (pred[32,64]{1,0:T(8,128)(4,1)}, pred[32,64]{1,0:T(8,128)(4,1)S(1)}, u32[]{:S(2)}) copy-start(pred[32,64]{1,0:T(8,128)(4,1)S(1)} %fusion.46) | copy-start | bytes 6148
  115.1 17.9 %copy-start.7 = (pred[32,64]{1,0:T(8,128)(4,1)S(1)}, pred[32,64]{1,0:T(8,128)(4,1)}, u32[]{:S(2)}) copy-start(pred[32,64]{1,0:T(8,128)(4,1)} %copy-done.6) | copy-start | bytes 6148
  133.0 3.7 %copy-start.10 = (s32[32]{0:T(128)S(1)}, s32[32]{0:T(128)}, u32[]{:S(2)}) copy-start(s32[32]{0:T(128)} %copy-done.9) | copy-start | bytes 388
  136.6 1.6 copy-start.3
  136.7 1.6 copy-start.4
  166.0 21.9 %all-to-all-start.3 = ((f32[32,4,2,8,98]{4,3,2,1,0:T(8,128)}), f32[32,4,2,8,98]{4,3,2,1,0:T(8,128)}, u32[]{:S(2)}, u32[]{:S(2)}) async-start(f32[32,4,2,8,98]{4,3,2,1,0:T(8,128)} %maximum_bitcast_fusion), calls=%async_computation.3 | async-start | bytes 2097152 | tf_op jit(solution)/shard_map/all_to_all | solution.py:222
  195.0 1.9 copy-start.5
  224.5 21.4 %copy-start.11 = (f32[96]{0:T(128)S(1)}, f32[96]{0:T(128)}, u32[]{:S(2)}) copy-start(f32[96]{0:T(128)} %get-tuple-element.43) | copy-start | bytes 1156
  228.8 13.8 %all-to-all-start.5 = ((f32[4,256,96]{1,2,0:T(8,128)}), f32[4,256,96]{1,2,0:T(8,128)}, u32[]{:S(2)}, u32[]{:S(2)}) async-start(f32[4,256,96]{1,2,0:T(8,128)} %broadcast_in_dim.201), calls=%async_computation.5 | async-start | bytes 786432 | tf_op jit(solution)/shard_map/all_to_all | solution.py:79
  284.7 6.3 %copy-start.12 = (s32[32]{0:T(128)S(1)}, s32[32]{0:T(128)}, u32[]{:S(2)}) copy-start(s32[32]{0:T(128)} %get-tuple-element.56) | copy-start | bytes 388
  284.7 6.3 %copy-start.14 = (s32[31]{0:T(128)S(1)}, s32[31]{0:T(128)}, u32[]{:S(2)}) copy-start(s32[31]{0:T(128)} %copy-done.13) | copy-start | bytes 376
  286.3 21.9 %all-to-all-start.7 = ((bf16[32,8,2048]{2,1,0:T(8,128)(2,1)}), bf16[32,8,2048]{2,1,0:T(8,128)(2,1)}, u32[]{:S(2)}, u32[]{:S(2)}) async-start(bf16[32,8,2048]{2,1,0:T(8,128)(2,1)} %broadcast_in_dim.202), calls=%async_computation.7 | async-start | bytes 2097152 | tf_op jit(solution)/shard_map/all_to_all | solution.py:79
  310.6 12.8 %all-to-all-start.8 = ((f32[4,256,96]{1,2,0:T(8,128)}), f32[4,256,96]{1,2,0:T(8,128)}, u32[]{:S(2)}, u32[]{:S(2)}) async-start(f32[4,256,96]{1,2,0:T(8,128)} %broadcast_in_dim.203), calls=%async_computation.8 | async-start | bytes 786432 | tf_op jit(solution)/shard_map/all_to_all | solution.py:79

commit v8 on v7

--- a/solution.py
+++ b/solution.py
@@ -174,12 +174,9 @@
     step_count, req_count, width_here = tokens.shape
     row_count = step_count * req_count
     activ = tokens.reshape(row_count, width_here).astype(jnp.float32)
-    row_ids = jnp.arange(row_count, dtype=jnp.int32)
-    positions = lengths[row_ids % req_count] + row_ids // req_count
-
-    def finish_qkv(total, squares, start):
+
+    def finish_qkv(total, squares, rows_here):
         count = total.shape[0]
-        rows_here = lax.dynamic_slice_in_dim(positions, start, count)
         inverse = lax.rsqrt(squares / D + EPSILON)
         scaled = total * inverse[:, None, None]
         heads_here = scaled.shape[2] // HEAD_DIM
@@ -201,13 +198,27 @@
     partial_one = jnp.einsum("bd,dcn->bcn", normed_one, w_qkv, preferred_element_type=jnp.float32)
     squares_one = jnp.sum(activ * activ, axis=1)
     sending = migrate_pool(k_cache, v_cache, move_slot, move_offset)
-    (query_all, key_all, value_all), sending = reduce_rows(
-        partial_one, squares_one, finish_qkv, sending
-    )
-    heads_here = query_all.shape[1] // HEAD_DIM
-    queries = query_all.reshape(step_count, req_count, heads_here, HEAD_DIM)
-    key_fresh = key_all.reshape(step_count, req_count, heads_here, HEAD_DIM)
-    value_fresh = value_all.reshape(step_count, req_count, heads_here, HEAD_DIM)
+    holders = lax.axis_size("pages")
+    myself = lax.axis_index("pages")
+    group = req_count // holders
+    packed = jnp.concatenate([partial_one.reshape(row_count, -1), squares_one[:, None]], axis=1)
+    packed = jnp.moveaxis(packed.reshape(step_count, holders, group, -1), 1, 0)
+    packed = lax.all_to_all(packed, "pages", split_axis=0, concat_axis=0, tiled=True)
+    packed = jnp.sum(packed, axis=0).reshape(step_count * group, -1)
+    own_lengths = lax.dynamic_slice_in_dim(lengths, myself * group, group)
+    own_positions = (
+        own_lengths[None, :] + jnp.arange(step_count, dtype=jnp.int32)[:, None]
+    ).reshape(-1)
+    query_own, key_own, value_own = finish_qkv(
+        packed[:, :-1].reshape((step_count * group,) + partial_one.shape[1:]), packed[:, -1], own_positions
+    )
+    heads_here = query_own.shape[1] // HEAD_DIM
+    query_gathered = gather_blocks(query_own.reshape(step_count, group, -1), "pages")
+    query_gathered, sending = lax.optimization_barrier((query_gathered, sending))
+    queries = jnp.moveaxis(query_gathered, 0, 1).reshape(step_count, req_count, heads_here, HEAD_DIM)
+    queries_mine = query_own.reshape(step_count, group, heads_here, HEAD_DIM)
+    key_mine = key_own.reshape(step_count, group, heads_here, HEAD_DIM)
+    value_mine = value_own.reshape(step_count, group, heads_here, HEAD_DIM)
     cache_top, cache_total, cache_acc = local_attention(
         queries, k_cache, v_cache, lengths, slot_request, slot_page
     )
@@ -223,10 +234,6 @@
     part_acc = packed[..., :HEAD_DIM]
     part_total = packed[..., HEAD_DIM]
     part_top = packed[..., HEAD_DIM + 1]
-    mine = lambda a: lax.dynamic_slice_in_dim(a, myself * group, group, 1)
-    queries_mine = mine(queries)
-    key_mine = mine(key_fresh)
-    value_mine = mine(value_fresh)
     scale = HEAD_DIM ** (-0.5)
     step_ids = jnp.arange(step_count, dtype=jnp.int32)
     causal = (step_ids[:, None] >= step_ids[None, :])[:, :, None, None]

time: 329 us -> 330 us (level)
  waiting for transfers between devices: 74.3 us -> 66.8 us
  local copies, waits for them, and re-layouts: 99.6 us -> 104 us
  other arithmetic: 47.4 us -> 51.8 us
    all_to_all x1 -> x0, waiting for transfers between devices: 31.6 us -> none  [reduce_rows(): lax.all_to_all(packed, 'pages', split_axis=0, concat_axis=0, tiled=True)]
    all_to_all x1 -> x2, waiting for transfers between devices: 6.01 us -> 34 us  [shards(): lax.all_to_all(packed, 'pages', split_axis=0, concat_axis=0, tiled=True)]
    all_to_all x1 -> x2, starting transfers between devices: 4.88 us -> 12.7 us  [shards(): lax.all_to_all(packed, 'pages', split_axis=0, concat_axis=0, tiled=True)]
    all_to_all x1 -> x0, starting transfers between devices: 7.57 us -> none  [reduce_rows(): lax.all_to_all(packed, 'pages', split_axis=0, concat_axis=0, tiled=True)]
    transpose x0 -> x2, local copies, waits for them, and re-layouts: none -> 5.39 us  [the longest x1 3.38 us: shards(): packed = jnp.moveaxis(packed.reshape(step_count, holders, group, -1), 1, 0)]
    reshape x3 -> x2, local copies, waits for them, and re-layouts: 7.07 us -> 3.83 us  [the longest x1 2.27 us: shards(): jnp.moveaxis(query_gathered, 0, 1)]
where the time goes in v8:
time: 330 us; the launch traced here: 327 us
  local copies, waits for them, and re-layouts  104 us (32%)
  waiting for transfers between devices  66.8 us (20%)
  other arithmetic  51.8 us (16%)
  blocking collectives  48.5 us (15%)
  starting transfers between devices  36.4 us (11%)
  matrix products  19 us (6%)
    all_to_all x2, waiting for transfers between devices, shards(): lax.all_to_all(packed, 'pages', split_axis=0, concat_axis=0, tiled=True)  34 us
    all_to_all x1, blocking collectives, reduce_rows(): lax.all_to_all(packed, 'pages', split_axis=0, concat_axis=0, tiled=True)  33.5 us
    all_to_all x4, starting transfers between devices, gather_blocks(): return lax.all_to_all(spread, axis, split_axis=0, concat_axis=0, tiled=True)  18.7 us
    all_to_all x1, waiting for transfers between devices, exchange_pool(): lax.all_to_all(both, 'pages', split_axis=0, concat_axis=0, tiled=True)  16.9 us
    all_to_all x4, waiting for transfers between devices, gather_blocks(): return lax.all_to_all(spread, axis, split_axis=0, concat_axis=0, tiled=True)  16 us
    all_to_all x1, blocking collectives, gather_blocks(): return lax.all_to_all(spread, axis, split_axis=0, concat_axis=0, tiled=True)  15 us
    all_to_all x2, starting transfers between devices, shards(): lax.all_to_all(packed, 'pages', split_axis=0, concat_axis=0, tiled=True)  12.7 us
    concatenate x3, local copies, waits for them, and re-layouts, shards(): jnp.concatenate([cache_acc, cache_total[..., None], cache_top[..., None]]...  8.43 us
  transfers between devices with their start and end apart: 7, of which 7 were waited for; matrix products, arithmetic and copies ran while one was open for 33% of the time, Pallas kernels for 0%

profile of v8, /device:TPU:0, one launch (start us, length us, event | category | flops | bytes accessed | tf_op | source)
XLA Modules:
  0.0 327.2 jit_solution(7672511631534028282)
XLA Ops:
  6.2 3.4 %copy.240 = f32[32,4,2,2305]{3,2,1,0:T(2,128)} copy(f32[32,4,2,2305]{3,0,2,1:T(8,128)S(1)} %maximum_bitcast_fusion) | data formatting | bytes 4720640 | tf_op jit(solution)/shard_map/transpose | solution.py:205
  9.5 7.8 %all-to-all-start = ((f32[32,4,2,2305]{3,2,1,0:T(2,128)}), f32[32,4,2,2305]{3,2,1,0:T(2,128)}, u32[]{:S(2)}, u32[]{:S(2)}) async-start(f32[32,4,2,2305]{3,2,1,0:T(2,128)} %copy.240), calls=%async_computation | async-start | bytes 4980736 | tf_op jit(solution)/shard_map/all_to_all | solution.py:206
  21.2 4.3 %gather_fusion.2 = bf16[32,64,768]{2,1,0:T(8,128)(2,1)} fusion(bf16[32,64,768]{2,1,0:T(8,128)(2,1)} %param.20, s32[1024]{0:T(1024)S(1)} %pad_clamp_fusion.1), kind=kCustom, calls=%fused_computation.2 | custom fusion | bytes 6291584 | tf_op jit(solution)/shard_map/gather | solution.py:96
  26.5 25.6 %all-to-all-done = f32[32,4,2,2305]{3,2,1,0:T(2,128)} async-done(((f32[32,4,2,2305]{3,2,1,0:T(2,128)}), f32[32,4,2,2305]{3,2,1,0:T(2,128)}, u32[]{:S(2)}, u32[]{:S(2)}) %all-to-all-start) | async-done | bytes 2360352 | tf_op jit(solution)/shard_map/all_to_all | solution.py:206
  52.0 3.0 reduce_sum.117
  64.5 4.6 %all-to-all-start.1 = ((bf16[32,4,2,768]{3,2,1,0:T(2,128)(2,1)}), bf16[32,4,2,768]{3,2,1,0:T(2,128)(2,1)}, u32[]{:S(2)}, u32[]{:S(2)}) async-start(bf16[32,4,2,768]{3,2,1,0:T(2,128)(2,1)} %broadcast_in_dim.186), calls=%async_computation.1 | async-start | bytes 786432 | tf_op jit(solution)/shard_map/all_to_all | solution.py:79
  69.1 3.3 %bitcast_select_fusion.1 = (bf16[32,1,64,768]{3,2,1,0:T(8,128)(2,1)S(1)}, bf16[32,1,64,768]{3,2,1,0:T(8,128)(2,1)S(1)}) fusion(bf16[32,64,768]{2,1,0:T(8,128)(2,1)} %gather_fusion.1, pred[32]{0:T(512)(128)(4,1)} %fusion.48, bf16[32,64,768]{2,1,0:T(8,128)(2,1)} %gather_fusion.2), kind=kLoop, calls=%fused_computation.17 | loop fusion | flops 3145728 | bytes 12582944 | tf_op jit(solution)/shard_map/jit(_where)/select_n | solution.py:95
  72.4 3.2 pad_maximum_fusion
  75.7 3.6 %all-to-all-done.1 = bf16[32,4,2,768]{3,2,1,0:T(2,128)(2,1)} async-done(((bf16[32,4,2,768]{3,2,1,0:T(2,128)(2,1)}), bf16[32,4,2,768]{3,2,1,0:T(2,128)(2,1)}, u32[]{:S(2)}, u32[]{:S(2)}) %all-to-all-start.1) | async-done | bytes 393248 | tf_op jit(solution)/shard_map/all_to_all | solution.py:79
  79.3 5.1 %all-to-all-start.2 = ((bf16[32,2,64,768]{3,2,1,0:T(8,128)(2,1)}), bf16[32,2,64,768]{3,2,1,0:T(8,128)(2,1)}, u32[]{:S(2)}, u32[]{:S(2)}) async-start(bf16[32,2,64,768]{3,2,1,0:T(8,128)(2,1)} %pad_maximum_fusion), calls=%async_computation.2 | async-start | bytes 12582912 | tf_op jit(solution)/shard_map/all_to_all | solution.py:101
  84.4 5.4 %reshape.369 = bf16[32,64,8,96]{3,2,1,0:T(8,128)(2,1)} reshape(bf16[32,64,768]{2,1,0:T(8,128)(2,1)S(1)} %copy-done.2) | data formatting | bytes 6291456 | tf_op jit(solution)/shard_map/reshape | solution.py:130
  89.8 8.2 %reshape.370 = bf16[32,64,8,96]{3,2,1,0:T(8,128)(2,1)} reshape(bf16[32,64,768]{2,1,0:T(8,128)(2,1)} %param.20) | data formatting | bytes 6291456 | tf_op jit(solution)/shard_map/reshape | solution.py:131
  108.9 6.0 %fusion.70 = (f32[4,32,8]{0,2,1:T(8,128)}, f32[4,32,8,64]{3,0,2,1:T(4,128)}) fusion(bf16[32,64,8,96]{3,2,1,0:T(8,128)(2,1)} %reshape.369, bf16[4,32,8,96]{3,2,0,1:T(8,128)(2,1)} %bitcast.143, pred[32,64]{1,0:T(8,128)(4,1)S(1)} %fusion.49), kind=kOutput, calls=%fused_computation.137 | convolution fusion | flops 12778496 | bytes 3610624 | tf_op jit(solution)/shard_map/tshd,skhd->tshk/dot_general | solution.py:133
  123.2 3.7 %fusion.4 = f32[4,32,8,96]{3,0,2,1:T(4,128)S(1)} fusion(bf16[32,64,8,96]{3,2,1,0:T(8,128)(2,1)} %reshape.370, f32[4,32,8,64]{3,0,2,1:T(4,128)} %get-tuple-element.45, f32[4,32,8]{0,2,1:T(8,128)} %copy.246, pred[32,64]{1,0:T(8,128)(4,1)} %copy-done.9), kind=kOutput, calls=%fused_computation.22 | convolution fusion | flops 12779520 | bytes 3807232 | tf_op jit(solution)/shard_map/tshk,skhd->tshd/dot_general | solution.py:147
  134.8 3.4 %copy.253 = f32[4,32,2,8,1]{4,3,2,0,1:T(8,128)} copy(f32[4,32,2,8,1]{3,2,1,0,4:T(2,128)} %bitcast.139) | data formatting | bytes 16384 | tf_op jit(solution)/shard_map/concatenate | solution.py:228
  138.2 3.4 %copy.254 = f32[4,32,2,8,1]{4,3,2,0,1:T(8,128)} copy(f32[4,32,2,8,1]{3,2,1,0,4:T(2,128)} %bitcast.138) | data formatting | bytes 16384 | tf_op jit(solution)/shard_map/concatenate | solution.py:228
  141.6 3.5 %maximum_bitcast_fusion.1 = f32[32,4,2,8,98]{4,3,2,1,0:T(8,128)} fusion(f32[4,32,2,8,1]{4,3,2,0,1:T(8,128)} %copy.254, f32[4,32,2,8,1]{4,3,2,0,1:T(8,128)} %copy.253, f32[4,32,2,8,96]{4,3,2,0,1:T(8,128)} %copy.252), kind=kLoop, calls=%fused_computation.29 | loop fusion | flops 401408 | bytes 1605632 | tf_op jit(solution)/shard_map/transpose | solution.py:231
  145.2 16.9 %all-to-all-done.2 = bf16[32,2,64,768]{3,2,1,0:T(8,128)(2,1)} async-done(((bf16[32,2,64,768]{3,2,1,0:T(8,128)(2,1)}), bf16[32,2,64,768]{3,2,1,0:T(8,128)(2,1)}, u32[]{:S(2)}, u32[]{:S(2)}) %all-to-all-start.2) | async-done | bytes 6291488 | tf_op jit(solution)/shard_map/all_to_all | solution.py:101
  162.1 6.3 %slice_bitcast_fusion = (bf16[32,64,768]{2,1,0:T(8,128)(2,1)}, bf16[32,64,768]{2,1,0:T(8,128)(2,1)}) fusion(bf16[32,2,64,768]{3,2,1,0:T(8,128)(2,1)} %all-to-all-done.2), kind=kLoop, calls=%fused_computation.14 | loop fusion | bytes 12582912 | tf_op jit(solution)/shard_map/squeeze | solution.py:102
  168.4 4.9 %all-to-all-start.3 = ((f32[32,4,2,8,98]{4,3,2,1,0:T(8,128)}), f32[32,4,2,8,98]{4,3,2,1,0:T(8,128)}, u32[]{:S(2)}, u32[]{:S(2)}) async-start(f32[32,4,2,8,98]{4,3,2,1,0:T(8,128)} %maximum_bitcast_fusion.1), calls=%async_computation.3 | async-start | bytes 2097152 | tf_op jit(solution)/shard_map/all_to_all | solution.py:233
  181.8 8.4 %all-to-all-done.3 = f32[32,4,2,8,98]{4,3,2,1,0:T(8,128)} async-done(((f32[32,4,2,8,98]{4,3,2,1,0:T(8,128)}), f32[32,4,2,8,98]{4,3,2,1,0:T(8,128)}, u32[]{:S(2)}, u32[]{:S(2)}) %all-to-all-start.3) | async-done | bytes 802848 | tf_op jit(solution)/shard_map/all_to_all | solution.py:233
  190.2 4.1 %fusion.68 = (f32[32,4,2,8,1]{4,3,2,1,0:T(8,128)}, f32[4,2,8]{2,1,0:T(2,128)}, f32[32,4,2,8,1]{4,3,2,1,0:T(8,128)}) fusion(f32[32,4,2,8,98]{4,3,2,1,0:T(8,128)} %all-to-all-done.3), kind=kLoop, calls=%fused_computation.135 | loop fusion | flops 1984 | bytes 33024 | tf_op jit(solution)/shard_map/slice | solution.py:235
  209.7 15.0 %all_to_all.45 = bf16[32,4,2,8,96]{4,3,2,1,0:T(8,128)(2,1)S(1)} all-to-all(bf16[32,4,2,8,96]{4,3,2,1,0:T(8,128)(2,1)S(1)} %broadcast_in_dim.200), channel_id=1, replica_groups=mesh['pages'=32,'mp'=4] {'pages'}, dimensions={0} | all-to-all | bytes 786432 | tf_op jit(solution)/shard_map/all_to_all | solution.py:79
  229.9 5.3 %all-to-all-start.5 = ((f32[4,256,96]{1,2,0:T(8,128)}), f32[4,256,96]{1,2,0:T(8,128)}, u32[]{:S(2)}, u32[]{:S(2)}) async-start(f32[4,256,96]{1,2,0:T(8,128)} %broadcast_in_dim.201), calls=%async_computation.5 | async-start | bytes 786432 | tf_op jit(solution)/shard_map/all_to_all | solution.py:79
  238.0 3.2 reshape.436
  252.2 33.5 %all_to_all.46 = bf16[32,8,4097]{2,1,0:T(8,128)(2,1)S(1)} all-to-all(bf16[32,8,4097]{2,1,0:T(8,128)(2,1)S(1)} %pad_maximum_fusion.1), channel_id=1, replica_groups=mesh['pages'=32,'mp'=4] {'pages'}, dimensions={0} | all-to-all | bytes 4195328 | tf_op jit(solution)/shard_map/all_to_all | solution.py:60
  287.4 4.7 %all-to-all-start.7 = ((bf16[32,8,2048]{2,1,0:T(8,128)(2,1)}), bf16[32,8,2048]{2,1,0:T(8,128)(2,1)}, u32[]{:S(2)}, u32[]{:S(2)}) async-start(bf16[32,8,2048]{2,1,0:T(8,128)(2,1)} %broadcast_in_dim.202), calls=%async_computation.7 | async-start | bytes 2097152 | tf_op jit(solution)/shard_map/all_to_all | solution.py:79
  292.2 4.3 %gather_fusion.5 = bf16[32,64,768]{2,1,0:T(8,128)(2,1)} fusion(bf16[32,64,768]{2,1,0:T(8,128)(2,1)} %get-tuple-element.11, s32[1024]{0:T(1024)S(1)} %pad_clamp_fusion), kind=kCustom, calls=%fused_computation.5 | custom fusion | bytes 6291584 | tf_op jit(solution)/shard_map/gather | solution.py:115
  296.5 4.3 %gather_fusion.6 = bf16[32,64,768]{2,1,0:T(8,128)(2,1)} fusion(bf16[32,64,768]{2,1,0:T(8,128)(2,1)} %get-tuple-element.12, s32[1024]{0:T(1024)S(1)} %pad_clamp_fusion), kind=kCustom, calls=%fused_computation.6 | custom fusion | bytes 6291584 | tf_op jit(solution)/shard_map/gather | solution.py:116
  300.8 8.4 %all-to-all-done.7 = bf16[32,8,2048]{2,1,0:T(8,128)(2,1)} async-done(((bf16[32,8,2048]{2,1,0:T(8,128)(2,1)}), bf16[32,8,2048]{2,1,0:T(8,128)(2,1)}, u32[]{:S(2)}, u32[]{:S(2)}) %all-to-all-start.7) | async-done | bytes 1048608 | tf_op jit(solution)/shard_map/all_to_all | solution.py:79
  311.7 4.1 %all-to-all-start.8 = ((f32[4,256,96]{1,2,0:T(8,128)}), f32[4,256,96]{1,2,0:T(8,128)}, u32[]{:S(2)}, u32[]{:S(2)}) async-start(f32[4,256,96]{1,2,0:T(8,128)} %broadcast_in_dim.203), calls=%async_computation.8 | async-start | bytes 786432 | tf_op jit(solution)/shard_map/all_to_all | solution.py:79
  315.8 7.1 %broadcast_select_fusion = (bf16[32,64,768]{2,1,0:T(8,128)(2,1)}, bf16[32,64,768]{2,1,0:T(8,128)(2,1)}) fusion(bf16[32,64,768]{2,1,0:T(8,128)(2,1)} %gather_fusion.6, bf16[32,64,768]{2,1,0:T(8,128)(2,1)} %param.20, pred[32]{0:T(512)(128)(4,1)S(1)} %fusion.47, bf16[32,64,768]{2,1,0:T(8,128)(2,1)} %gather_fusion.5, bf16[32,64,768]{2,1,0:T(8,128)(2,1)S(1)} %copy-done.2), kind=kLoop, calls=%fused_computation.18 | loop fusion | flops 3145728 | bytes 18874400 | tf_op jit(solution)/shard_map/jit(_where)/select_n | solution.py:116
  (138 shorter events, 98.1 us)
Async XLA Ops:
  0.6 308.6 %copy-start = (bf16[96,2048]{1,0:T(8,128)(2,1)S(1)}, bf16[96,2048]{1,0:T(8,128)(2,1)}, u32[]{:S(2)}) copy-start(bf16[96,2048]{1,0:T(8,128)(2,1)} %param.18) | copy-start | bytes 1179652
  9.5 8.5 %copy-start.18 = (s32[31]{0:T(128)S(1)}, s32[31]{0:T(128)}, u32[]{:S(2)}) copy-start(s32[31]{0:T(128)} %param.25) | copy-start | bytes 376
  9.5 9.2 %copy-start.2 = (bf16[32,64,768]{2,1,0:T(8,128)(2,1)S(1)}, bf16[32,64,768]{2,1,0:T(8,128)(2,1)}, u32[]{:S(2)}) copy-start(bf16[32,64,768]{2,1,0:T(8,128)(2,1)} %param.19) | copy-start | bytes 9437188
  9.5 42.5 %all-to-all-start = ((f32[32,4,2,2305]{3,2,1,0:T(2,128)}), f32[32,4,2,2305]{3,2,1,0:T(2,128)}, u32[]{:S(2)}, u32[]{:S(2)}) async-start(f32[32,4,2,2305]{3,2,1,0:T(2,128)} %copy.240), calls=%async_computation | async-start | bytes 4980736 | tf_op jit(solution)/shard_map/all_to_all | solution.py:206
  18.1 0.7 copy-start.16
  21.2 4.3 %copy-start.1 = (s32[64]{0:T(128)S(1)}, s32[64]{0:T(128)}, u32[]{:S(2)}) copy-start(s32[64]{0:T(128)} %param.21) | copy-start | bytes 772
  26.4 35.6 %copy-start.7 = (f32[8,48]{1,0:T(8,128)}, f32[8,48]{1,0:T(8,128)S(1)}, u32[]{:S(2)}) copy-start(f32[8,48]{1,0:T(8,128)S(1)} %get-tuple-element.36) | copy-start | bytes 4612
  26.4 35.6 %copy-start.8 = (f32[8,48]{1,0:T(8,128)}, f32[8,48]{1,0:T(8,128)S(1)}, u32[]{:S(2)}) copy-start(f32[8,48]{1,0:T(8,128)S(1)} %get-tuple-element.37) | copy-start | bytes 4612
  58.4 0.6 copy-start.5
  64.5 14.8 %all-to-all-start.1 = ((bf16[32,4,2,768]{3,2,1,0:T(2,128)(2,1)}), bf16[32,4,2,768]{3,2,1,0:T(2,128)(2,1)}, u32[]{:S(2)}, u32[]{:S(2)}) async-start(bf16[32,4,2,768]{3,2,1,0:T(2,128)(2,1)} %broadcast_in_dim.186), calls=%async_computation.1 | async-start | bytes 786432 | tf_op jit(solution)/shard_map/all_to_all | solution.py:79
  79.3 82.8 %all-to-all-start.2 = ((bf16[32,2,64,768]{3,2,1,0:T(8,128)(2,1)}), bf16[32,2,64,768]{3,2,1,0:T(8,128)(2,1)}, u32[]{:S(2)}, u32[]{:S(2)}) async-start(bf16[32,2,64,768]{3,2,1,0:T(8,128)(2,1)} %pad_maximum_fusion), calls=%async_computation.2 | async-start | bytes 12582912 | tf_op jit(solution)/shard_map/all_to_all | solution.py:101
  98.8 16.1 %copy-start.12 = (s32[32]{0:T(128)}, s32[32]{0:T(128)S(1)}, u32[]{:S(2)}) copy-start(s32[32]{0:T(128)S(1)} %get-tuple-element.16) | copy-start | bytes 388
  98.8 16.1 %copy-start.11 = (s32[1024]{0:T(1024)}, s32[1024]{0:T(1024)S(1)}, u32[]{:S(2)}) copy-start(s32[1024]{0:T(1024)S(1)} %pad_clamp_fusion.2) | copy-start | bytes 12292
  102.2 12.7 %copy-start.9 = (pred[32,64]{1,0:T(8,128)(4,1)}, pred[32,64]{1,0:T(8,128)(4,1)S(1)}, u32[]{:S(2)}) copy-start(pred[32,64]{1,0:T(8,128)(4,1)S(1)} %fusion.49) | copy-start | bytes 6148
  119.2 7.7 %copy-start.13 = (s32[32]{0:T(128)S(1)}, s32[32]{0:T(128)}, u32[]{:S(2)}) copy-start(s32[32]{0:T(128)} %copy-done.12) | copy-start | bytes 388
  126.9 2.6 copy-start.3
  126.9 2.5 copy-start.4
  127.0 2.5 copy-start.10
  145.2 32.4 %copy-start.6 = (bf16[8,8,96]{2,1,0:T(8,128)(2,1)S(1)}, bf16[8,8,96]{2,1,0:T(8,128)(2,1)}, u32[]{:S(2)}) copy-start(bf16[8,8,96]{2,1,0:T(8,128)(2,1)} %maximum_convert_fusion) | copy-start | bytes 36868
  168.4 21.9 %all-to-all-start.3 = ((f32[32,4,2,8,98]{4,3,2,1,0:T(8,128)}), f32[32,4,2,8,98]{4,3,2,1,0:T(8,128)}, u32[]{:S(2)}, u32[]{:S(2)}) async-start(f32[32,4,2,8,98]{4,3,2,1,0:T(8,128)} %maximum_bitcast_fusion.1), calls=%async_computation.3 | async-start | bytes 2097152 | tf_op jit(solution)/shard_map/all_to_all | solution.py:233
  225.5 21.4 %copy-start.14 = (f32[96]{0:T(128)S(1)}, f32[96]{0:T(128)}, u32[]{:S(2)}) copy-start(f32[96]{0:T(128)} %get-tuple-element.34) | copy-start | bytes 1156
  229.9 13.8 %all-to-all-start.5 = ((f32[4,256,96]{1,2,0:T(8,128)}), f32[4,256,96]{1,2,0:T(8,128)}, u32[]{:S(2)}, u32[]{:S(2)}) async-start(f32[4,256,96]{1,2,0:T(8,128)} %broadcast_in_dim.201), calls=%async_computation.5 | async-start | bytes 786432 | tf_op jit(solution)/shard_map/all_to_all | solution.py:79
  285.7 6.3 %copy-start.15 = (s32[32]{0:T(128)S(1)}, s32[32]{0:T(128)}, u32[]{:S(2)}) copy-start(s32[32]{0:T(128)} %get-tuple-element.47) | copy-start | bytes 388
  285.7 6.3 %copy-start.17 = (s32[31]{0:T(128)S(1)}, s32[31]{0:T(128)}, u32[]{:S(2)}) copy-start(s32[31]{0:T(128)} %copy-done.16) | copy-start | bytes 376
  287.4 21.9 %all-to-all-start.7 = ((bf16[32,8,2048]{2,1,0:T(8,128)(2,1)}), bf16[32,8,2048]{2,1,0:T(8,128)(2,1)}, u32[]{:S(2)}, u32[]{:S(2)}) async-start(bf16[32,8,2048]{2,1,0:T(8,128)(2,1)} %broadcast_in_dim.202), calls=%async_computation.7 | async-start | bytes 2097152 | tf_op jit(solution)/shard_map/all_to_all | solution.py:79
  311.7 12.8 %all-to-all-start.8 = ((f32[4,256,96]{1,2,0:T(8,128)}), f32[4,256,96]{1,2,0:T(8,128)}, u32[]{:S(2)}, u32[]{:S(2)}) async-start(f32[4,256,96]{1,2,0:T(8,128)} %broadcast_in_dim.203), calls=%async_computation.8 | async-start | bytes 786432 | tf_op jit(solution)/shard_map/all_to_all | solution.py:79

commit v9 on v8

--- a/solution.py
+++ b/solution.py
@@ -98,11 +98,10 @@
 
 
 def exchange_pool(both):
-    both = lax.all_to_all(both, "pages", split_axis=0, concat_axis=0, tiled=True)
-    return both[:, 0], both[:, 1]
-
-
-def land_pool(key_local, value_local, key_recv, value_recv, move_slot, move_offset):
+    return lax.all_to_all(both, "pages", split_axis=0, concat_axis=0, tiled=True)
+
+
+def land_pool(key_local, value_local, both_recv, move_slot, move_offset):
     holders = lax.axis_size("pages")
     myself = lax.axis_index("pages")
     mine = lax.dynamic_index_in_dim(move_slot, myself, 0, keepdims=False)
@@ -111,9 +110,10 @@
     landing = slot_ids[:, None] == mine[None, :]
     came_from = jnp.sum(jnp.where(landing, sources[None, :], 0), axis=1)
     arriving = jnp.any(landing, axis=1)[:, None, None]
+    picked = both_recv[came_from]
     return (
-        jnp.where(arriving, key_recv[came_from], key_local),
-        jnp.where(arriving, value_recv[came_from], value_local),
+        jnp.where(arriving, picked[:, 0], key_local),
+        jnp.where(arriving, picked[:, 1], value_local),
     )
 
 
@@ -269,7 +269,7 @@
         lax.dot_general(hidden, w_down, CONTRACT_LAST, preferred_element_type=jnp.float32)
     )
     layer_out = (mixed + feed).astype(jnp.bfloat16).reshape(step_count, req_count, width_here)
-    new_k_cache, new_v_cache = land_pool(k_cache, v_cache, *received, move_slot, move_offset)
+    new_k_cache, new_v_cache = land_pool(k_cache, v_cache, received, move_slot, move_offset)
     return (layer_out, new_k_cache, new_v_cache)
 
 

time: 330 us -> 324 us (0.982)
  local copies, waits for them, and re-layouts: 104 us -> 95.1 us
  waiting for transfers between devices: 66.8 us -> 70.4 us
    squeeze x1 -> x0, local copies, waits for them, and re-layouts: 6.3 us -> none  [exchange_pool(): return (both[:, 0], both[:, 1])]
    all_to_all x4, waiting for transfers between devices: 16 us -> 19.5 us  [gather_blocks(): return lax.all_to_all(spread, axis, split_axis=0, concat_axis=0, tiled=True)]
    gather x2 -> x1, local copies, waits for them, and re-layouts: 8.61 us -> 6.39 us  [land_pool(): picked = both_recv[came_from]]
    select_n x1 -> x2, other arithmetic: 7.13 us -> 5.85 us  [the longest x1 5.84 us: land_pool(): jnp.where(arriving, picked[:, 1], value_local)]
  transfers between devices with their start and end apart: 7 -> 7, of which waited for: 7 -> 7; matrix products, arithmetic and copies ran while one was open for 33% -> 32% of each run, Pallas kernels for 0% -> 0%
where the time goes in v9:
time: 324 us; the launch traced here: 321 us
  local copies, waits for them, and re-layouts  95.1 us (29%)
  waiting for transfers between devices  70.4 us (22%)
  other arithmetic  50.6 us (16%)
  blocking collectives  48.5 us (15%)
  starting transfers between devices  36.4 us (11%)
  matrix products  19 us (6%)
    all_to_all x2, waiting for transfers between devices, shards(): lax.all_to_all(packed, 'pages', split_axis=0, concat_axis=0, tiled=True)  34 us
    all_to_all x1, blocking collectives, reduce_rows(): lax.all_to_all(packed, 'pages', split_axis=0, concat_axis=0, tiled=True)  33.5 us
    all_to_all x4, waiting for transfers between devices, gather_blocks(): return lax.all_to_all(spread, axis, split_axis=0, concat_axis=0, tiled=True)  19.5 us
    all_to_all x4, starting transfers between devices, gather_blocks(): return lax.all_to_all(spread, axis, split_axis=0, concat_axis=0, tiled=True)  18.7 us
    all_to_all x1, waiting for transfers between devices, exchange_pool(): lax.all_to_all(both, 'pages', split_axis=0, concat_axis=0, tiled=True)  16.9 us
    all_to_all x1, blocking collectives, gather_blocks(): return lax.all_to_all(spread, axis, split_axis=0, concat_axis=0, tiled=True)  15 us
    all_to_all x2, starting transfers between devices, shards(): lax.all_to_all(packed, 'pages', split_axis=0, concat_axis=0, tiled=True)  12.7 us
    concatenate x3, local copies, waits for them, and re-layouts, shards(): jnp.concatenate([cache_acc, cache_total[..., None], cache_top[..., None]]...  8.43 us
  transfers between devices with their start and end apart: 7, of which 7 were waited for; matrix products, arithmetic and copies ran while one was open for 32% of the time, Pallas kernels for 0%

profile of v9, /device:TPU:0, one launch (start us, length us, event | category | flops | bytes accessed | tf_op | source)
XLA Modules:
  0.0 321.0 jit_solution(3396908437630422282)
XLA Ops:
  6.2 3.4 %copy.238 = f32[32,4,2,2305]{3,2,1,0:T(2,128)} copy(f32[32,4,2,2305]{3,0,2,1:T(8,128)S(1)} %maximum_bitcast_fusion) | data formatting | bytes 4720640 | tf_op jit(solution)/shard_map/transpose | solution.py:205
  9.6 7.8 %all-to-all-start = ((f32[32,4,2,2305]{3,2,1,0:T(2,128)}), f32[32,4,2,2305]{3,2,1,0:T(2,128)}, u32[]{:S(2)}, u32[]{:S(2)}) async-start(f32[32,4,2,2305]{3,2,1,0:T(2,128)} %copy.238), calls=%async_computation | async-start | bytes 4980736 | tf_op jit(solution)/shard_map/all_to_all | solution.py:206
  21.2 4.3 %gather_fusion.2 = bf16[32,64,768]{2,1,0:T(8,128)(2,1)} fusion(bf16[32,64,768]{2,1,0:T(8,128)(2,1)} %param.20, s32[1024]{0:T(1024)S(1)} %pad_clamp_fusion.1), kind=kCustom, calls=%fused_computation.2 | custom fusion | bytes 6291584 | tf_op jit(solution)/shard_map/gather | solution.py:96
  26.4 25.6 %all-to-all-done = f32[32,4,2,2305]{3,2,1,0:T(2,128)} async-done(((f32[32,4,2,2305]{3,2,1,0:T(2,128)}), f32[32,4,2,2305]{3,2,1,0:T(2,128)}, u32[]{:S(2)}, u32[]{:S(2)}) %all-to-all-start) | async-done | bytes 2360352 | tf_op jit(solution)/shard_map/all_to_all | solution.py:206
  52.1 3.0 reduce_sum.117
  64.5 4.6 %all-to-all-start.1 = ((bf16[32,4,2,768]{3,2,1,0:T(2,128)(2,1)}), bf16[32,4,2,768]{3,2,1,0:T(2,128)(2,1)}, u32[]{:S(2)}, u32[]{:S(2)}) async-start(bf16[32,4,2,768]{3,2,1,0:T(2,128)(2,1)} %broadcast_in_dim.185), calls=%async_computation.1 | async-start | bytes 786432 | tf_op jit(solution)/shard_map/all_to_all | solution.py:79
  69.1 3.3 %bitcast_select_fusion.1 = (bf16[32,1,64,768]{3,2,1,0:T(8,128)(2,1)S(1)}, bf16[32,1,64,768]{3,2,1,0:T(8,128)(2,1)S(1)}) fusion(bf16[32,64,768]{2,1,0:T(8,128)(2,1)} %gather_fusion.1, pred[32]{0:T(512)(128)(4,1)} %fusion.50, bf16[32,64,768]{2,1,0:T(8,128)(2,1)} %gather_fusion.2), kind=kLoop, calls=%fused_computation.18 | loop fusion | flops 3145728 | bytes 12582944 | tf_op jit(solution)/shard_map/jit(_where)/select_n | solution.py:95
  72.4 3.2 %pad_maximum_fusion = bf16[32,2,64,768]{3,2,1,0:T(8,128)(2,1)} fusion(bf16[32,1,64,768]{3,2,1,0:T(8,128)(2,1)S(1)} %get-tuple-element.37, bf16[32,1,64,768]{3,2,1,0:T(8,128)(2,1)S(1)} %get-tuple-element.36), kind=kLoop, calls=%fused_computation.6 | loop fusion | flops 3145728 | bytes 12582912 | tf_op jit(solution)/shard_map/stack | solution.py:97
  75.7 3.6 %all-to-all-done.1 = bf16[32,4,2,768]{3,2,1,0:T(2,128)(2,1)} async-done(((bf16[32,4,2,768]{3,2,1,0:T(2,128)(2,1)}), bf16[32,4,2,768]{3,2,1,0:T(2,128)(2,1)}, u32[]{:S(2)}, u32[]{:S(2)}) %all-to-all-start.1) | async-done | bytes 393248 | tf_op jit(solution)/shard_map/all_to_all | solution.py:79
  79.3 5.1 %all-to-all-start.2 = ((bf16[32,2,64,768]{3,2,1,0:T(8,128)(2,1)}), bf16[32,2,64,768]{3,2,1,0:T(8,128)(2,1)}, u32[]{:S(2)}, u32[]{:S(2)}) async-start(bf16[32,2,64,768]{3,2,1,0:T(8,128)(2,1)} %pad_maximum_fusion), calls=%async_computation.2 | async-start | bytes 12582912 | tf_op jit(solution)/shard_map/all_to_all | solution.py:101
  84.4 5.4 %reshape.369 = bf16[32,64,8,96]{3,2,1,0:T(8,128)(2,1)} reshape(bf16[32,64,768]{2,1,0:T(8,128)(2,1)S(1)} %copy-done.2) | data formatting | bytes 6291456 | tf_op jit(solution)/shard_map/reshape | solution.py:130
  89.8 8.2 %reshape.370 = bf16[32,64,8,96]{3,2,1,0:T(8,128)(2,1)} reshape(bf16[32,64,768]{2,1,0:T(8,128)(2,1)} %param.20) | data formatting | bytes 6291456 | tf_op jit(solution)/shard_map/reshape | solution.py:131
  108.9 6.0 %fusion.72 = (f32[4,32,8]{0,2,1:T(8,128)}, f32[4,32,8,64]{3,0,2,1:T(4,128)}) fusion(bf16[32,64,8,96]{3,2,1,0:T(8,128)(2,1)} %reshape.369, bf16[4,32,8,96]{3,2,0,1:T(8,128)(2,1)} %bitcast.145, pred[32,64]{1,0:T(8,128)(4,1)S(1)} %fusion.51), kind=kOutput, calls=%fused_computation.136 | convolution fusion | flops 12778496 | bytes 3610624 | tf_op jit(solution)/shard_map/tshd,skhd->tshk/dot_general | solution.py:133
  123.2 3.7 %fusion.6 = f32[4,32,8,96]{3,0,2,1:T(4,128)S(1)} fusion(bf16[32,64,8,96]{3,2,1,0:T(8,128)(2,1)} %reshape.370, f32[4,32,8,64]{3,0,2,1:T(4,128)} %get-tuple-element.41, f32[4,32,8]{0,2,1:T(8,128)} %copy.244, pred[32,64]{1,0:T(8,128)(4,1)} %copy-done.9), kind=kOutput, calls=%fused_computation.21 | convolution fusion | flops 12779520 | bytes 3807232 | tf_op jit(solution)/shard_map/tshk,skhd->tshd/dot_general | solution.py:147
  134.8 3.4 %copy.251 = f32[4,32,2,8,1]{4,3,2,0,1:T(8,128)} copy(f32[4,32,2,8,1]{3,2,1,0,4:T(2,128)} %bitcast.141) | data formatting | bytes 16384 | tf_op jit(solution)/shard_map/concatenate | solution.py:228
  138.2 3.4 %copy.252 = f32[4,32,2,8,1]{4,3,2,0,1:T(8,128)} copy(f32[4,32,2,8,1]{3,2,1,0,4:T(2,128)} %bitcast.140) | data formatting | bytes 16384 | tf_op jit(solution)/shard_map/concatenate | solution.py:228
  141.6 3.5 %maximum_bitcast_fusion.1 = f32[32,4,2,8,98]{4,3,2,1,0:T(8,128)} fusion(f32[4,32,2,8,1]{4,3,2,0,1:T(8,128)} %copy.252, f32[4,32,2,8,1]{4,3,2,0,1:T(8,128)} %copy.251, f32[4,32,2,8,96]{4,3,2,0,1:T(8,128)} %copy.250), kind=kLoop, calls=%fused_computation.28 | loop fusion | flops 401408 | bytes 1605632 | tf_op jit(solution)/shard_map/transpose | solution.py:231
  145.2 16.9 %all-to-all-done.2 = bf16[32,2,64,768]{3,2,1,0:T(8,128)(2,1)} async-done(((bf16[32,2,64,768]{3,2,1,0:T(8,128)(2,1)}), bf16[32,2,64,768]{3,2,1,0:T(8,128)(2,1)}, u32[]{:S(2)}, u32[]{:S(2)}) %all-to-all-start.2) | async-done | bytes 6291488 | tf_op jit(solution)/shard_map/all_to_all | solution.py:101
  162.1 4.9 %all-to-all-start.3 = ((f32[32,4,2,8,98]{4,3,2,1,0:T(8,128)}), f32[32,4,2,8,98]{4,3,2,1,0:T(8,128)}, u32[]{:S(2)}, u32[]{:S(2)}) async-start(f32[32,4,2,8,98]{4,3,2,1,0:T(8,128)} %maximum_bitcast_fusion.1), calls=%async_computation.3 | async-start | bytes 2097152 | tf_op jit(solution)/shard_map/all_to_all | solution.py:233
  175.5 8.4 %all-to-all-done.3 = f32[32,4,2,8,98]{4,3,2,1,0:T(8,128)} async-done(((f32[32,4,2,8,98]{4,3,2,1,0:T(8,128)}), f32[32,4,2,8,98]{4,3,2,1,0:T(8,128)}, u32[]{:S(2)}, u32[]{:S(2)}) %all-to-all-start.3) | async-done | bytes 802848 | tf_op jit(solution)/shard_map/all_to_all | solution.py:233
  183.9 4.2 %fusion.70 = (f32[32,4,2,8,1]{4,3,2,1,0:T(8,128)}, f32[4,2,8]{2,1,0:T(2,128)}, f32[32,4,2,8,1]{4,3,2,1,0:T(8,128)}) fusion(f32[32,4,2,8,98]{4,3,2,1,0:T(8,128)} %all-to-all-done.3), kind=kLoop, calls=%fused_computation.134 | loop fusion | flops 1984 | bytes 33024 | tf_op jit(solution)/shard_map/slice | solution.py:235
  203.5 15.0 %all_to_all.45 = bf16[32,4,2,8,96]{4,3,2,1,0:T(8,128)(2,1)S(1)} all-to-all(bf16[32,4,2,8,96]{4,3,2,1,0:T(8,128)(2,1)S(1)} %broadcast_in_dim.199), channel_id=1, replica_groups=mesh['pages'=32,'mp'=4] {'pages'}, dimensions={0} | all-to-all | bytes 786432 | tf_op jit(solution)/shard_map/all_to_all | solution.py:79
  223.6 5.3 %all-to-all-start.5 = ((f32[4,256,96]{1,2,0:T(8,128)}), f32[4,256,96]{1,2,0:T(8,128)}, u32[]{:S(2)}, u32[]{:S(2)}) async-start(f32[4,256,96]{1,2,0:T(8,128)} %broadcast_in_dim.200), calls=%async_computation.5 | async-start | bytes 786432 | tf_op jit(solution)/shard_map/all_to_all | solution.py:79
  229.0 2.8 copy.272
  231.8 3.2 %reshape.428 = bf16[4096,96,1]{0,1,2:T(8,128)(2,1)} reshape(bf16[2,2048,96]{1,0,2:T(2,128)(2,1)} %copy.272) | data formatting | bytes 1572864 | tf_op jit(solution)/shard_map/bd,gdf->bgf/dot_general | solution.py:263
  246.1 33.5 %all_to_all.46 = bf16[32,8,4097]{2,1,0:T(8,128)(2,1)S(1)} all-to-all(bf16[32,8,4097]{2,1,0:T(8,128)(2,1)S(1)} %pad_maximum_fusion.1), channel_id=1, replica_groups=mesh['pages'=32,'mp'=4] {'pages'}, dimensions={0} | all-to-all | bytes 4195328 | tf_op jit(solution)/shard_map/all_to_all | solution.py:60
  281.2 4.7 %all-to-all-start.7 = ((bf16[32,8,2048]{2,1,0:T(8,128)(2,1)}), bf16[32,8,2048]{2,1,0:T(8,128)(2,1)}, u32[]{:S(2)}, u32[]{:S(2)}) async-start(bf16[32,8,2048]{2,1,0:T(8,128)(2,1)} %broadcast_in_dim.201), calls=%async_computation.7 | async-start | bytes 2097152 | tf_op jit(solution)/shard_map/all_to_all | solution.py:79
  286.0 6.4 %gather_fusion.5 = bf16[32,2,64,768]{3,2,1,0:T(8,128)(2,1)} fusion(bf16[32,2,64,768]{3,2,1,0:T(8,128)(2,1)} %all-to-all-done.2, s32[1024]{0:T(1024)S(1)} %pad_clamp_fusion), kind=kCustom, calls=%fused_computation.5 | custom fusion | bytes 12583040 | tf_op jit(solution)/shard_map/gather | solution.py:113
  292.4 10.6 %all-to-all-done.7 = bf16[32,8,2048]{2,1,0:T(8,128)(2,1)} async-done(((bf16[32,8,2048]{2,1,0:T(8,128)(2,1)}), bf16[32,8,2048]{2,1,0:T(8,128)(2,1)}, u32[]{:S(2)}, u32[]{:S(2)}) %all-to-all-start.7) | async-done | bytes 1048608 | tf_op jit(solution)/shard_map/all_to_all | solution.py:79
  305.5 4.1 %all-to-all-start.8 = ((f32[4,256,96]{1,2,0:T(8,128)}), f32[4,256,96]{1,2,0:T(8,128)}, u32[]{:S(2)}, u32[]{:S(2)}) async-start(f32[4,256,96]{1,2,0:T(8,128)} %broadcast_in_dim.202), calls=%async_computation.8 | async-start | bytes 786432 | tf_op jit(solution)/shard_map/all_to_all | solution.py:79
  309.6 5.8 %fusion.4 = (bf16[32,64,768]{2,1,0:T(8,128)(2,1)}, bf16[32,64,768]{2,1,0:T(8,128)(2,1)}) fusion(bf16[32,64,768]{2,1,0:T(8,128)(2,1)} %param.20, bf16[32,2,64,768]{3,2,1,0:T(8,128)(2,1)} %gather_fusion.5, pred[32]{0:T(512)(128)(4,1)S(1)} %fusion.49, bf16[32,64,768]{2,1,0:T(8,128)(2,1)S(1)} %copy-done.2), kind=kLoop, calls=%fused_computation.14 | loop fusion | flops 3145728 | bytes 18874400 | tf_op jit(solution)/shard_map/jit(_where)/select_n | solution.py:116
  315.5 2.8 all-to-all-done.8
  (137 shorter events, 93.7 us)
Async XLA Ops:
  0.6 302.4 %copy-start = (bf16[96,2048]{1,0:T(8,128)(2,1)S(1)}, bf16[96,2048]{1,0:T(8,128)(2,1)}, u32[]{:S(2)}) copy-start(bf16[96,2048]{1,0:T(8,128)(2,1)} %param.18) | copy-start | bytes 1179652
  9.6 8.5 %copy-start.18 = (s32[31]{0:T(128)S(1)}, s32[31]{0:T(128)}, u32[]{:S(2)}) copy-start(s32[31]{0:T(128)} %param.25) | copy-start | bytes 376
  9.6 9.2 %copy-start.2 = (bf16[32,64,768]{2,1,0:T(8,128)(2,1)S(1)}, bf16[32,64,768]{2,1,0:T(8,128)(2,1)}, u32[]{:S(2)}) copy-start(bf16[32,64,768]{2,1,0:T(8,128)(2,1)} %param.19) | copy-start | bytes 9437188
  9.6 42.5 %all-to-all-start = ((f32[32,4,2,2305]{3,2,1,0:T(2,128)}), f32[32,4,2,2305]{3,2,1,0:T(2,128)}, u32[]{:S(2)}, u32[]{:S(2)}) async-start(f32[32,4,2,2305]{3,2,1,0:T(2,128)} %copy.238), calls=%async_computation | async-start | bytes 4980736 | tf_op jit(solution)/shard_map/all_to_all | solution.py:206
  18.1 0.7 copy-start.15
  21.2 4.3 %copy-start.1 = (s32[64]{0:T(128)S(1)}, s32[64]{0:T(128)}, u32[]{:S(2)}) copy-start(s32[64]{0:T(128)} %param.21) | copy-start | bytes 772
  26.4 35.6 %copy-start.7 = (f32[8,48]{1,0:T(8,128)}, f32[8,48]{1,0:T(8,128)S(1)}, u32[]{:S(2)}) copy-start(f32[8,48]{1,0:T(8,128)S(1)} %get-tuple-element.34) | copy-start | bytes 4612
  26.4 35.6 %copy-start.8 = (f32[8,48]{1,0:T(8,128)}, f32[8,48]{1,0:T(8,128)S(1)}, u32[]{:S(2)}) copy-start(f32[8,48]{1,0:T(8,128)S(1)} %get-tuple-element.35) | copy-start | bytes 4612
  58.5 0.6 copy-start.5
  64.5 14.8 %all-to-all-start.1 = ((bf16[32,4,2,768]{3,2,1,0:T(2,128)(2,1)}), bf16[32,4,2,768]{3,2,1,0:T(2,128)(2,1)}, u32[]{:S(2)}, u32[]{:S(2)}) async-start(bf16[32,4,2,768]{3,2,1,0:T(2,128)(2,1)} %broadcast_in_dim.185), calls=%async_computation.1 | async-start | bytes 786432 | tf_op jit(solution)/shard_map/all_to_all | solution.py:79
  79.3 82.8 %all-to-all-start.2 = ((bf16[32,2,64,768]{3,2,1,0:T(8,128)(2,1)}), bf16[32,2,64,768]{3,2,1,0:T(8,128)(2,1)}, u32[]{:S(2)}, u32[]{:S(2)}) async-start(bf16[32,2,64,768]{3,2,1,0:T(8,128)(2,1)} %pad_maximum_fusion), calls=%async_computation.2 | async-start | bytes 12582912 | tf_op jit(solution)/shard_map/all_to_all | solution.py:101
  98.8 16.1 %copy-start.12 = (s32[32]{0:T(128)}, s32[32]{0:T(128)S(1)}, u32[]{:S(2)}) copy-start(s32[32]{0:T(128)S(1)} %get-tuple-element.14) | copy-start | bytes 388
  98.8 16.1 %copy-start.11 = (s32[1024]{0:T(1024)}, s32[1024]{0:T(1024)S(1)}, u32[]{:S(2)}) copy-start(s32[1024]{0:T(1024)S(1)} %pad_clamp_fusion.2) | copy-start | bytes 12292
  102.2 12.7 %copy-start.9 = (pred[32,64]{1,0:T(8,128)(4,1)}, pred[32,64]{1,0:T(8,128)(4,1)S(1)}, u32[]{:S(2)}) copy-start(pred[32,64]{1,0:T(8,128)(4,1)S(1)} %fusion.51) | copy-start | bytes 6148
  119.2 7.7 %copy-start.13 = (s32[32]{0:T(128)S(1)}, s32[32]{0:T(128)}, u32[]{:S(2)}) copy-start(s32[32]{0:T(128)} %copy-done.12) | copy-start | bytes 388
  126.9 2.6 copy-start.3
  126.9 2.5 copy-start.4
  127.0 2.5 copy-start.10
  141.6 29.6 %copy-start.6 = (bf16[8,8,96]{2,1,0:T(8,128)(2,1)S(1)}, bf16[8,8,96]{2,1,0:T(8,128)(2,1)}, u32[]{:S(2)}) copy-start(bf16[8,8,96]{2,1,0:T(8,128)(2,1)} %maximum_convert_fusion) | copy-start | bytes 36868
  162.1 21.9 %all-to-all-start.3 = ((f32[32,4,2,8,98]{4,3,2,1,0:T(8,128)}), f32[32,4,2,8,98]{4,3,2,1,0:T(8,128)}, u32[]{:S(2)}, u32[]{:S(2)}) async-start(f32[32,4,2,8,98]{4,3,2,1,0:T(8,128)} %maximum_bitcast_fusion.1), calls=%async_computation.3 | async-start | bytes 2097152 | tf_op jit(solution)/shard_map/all_to_all | solution.py:233
  219.3 21.4 %copy-start.14 = (f32[96]{0:T(128)S(1)}, f32[96]{0:T(128)}, u32[]{:S(2)}) copy-start(f32[96]{0:T(128)} %get-tuple-element.32) | copy-start | bytes 1156
  223.6 13.8 %all-to-all-start.5 = ((f32[4,256,96]{1,2,0:T(8,128)}), f32[4,256,96]{1,2,0:T(8,128)}, u32[]{:S(2)}, u32[]{:S(2)}) async-start(f32[4,256,96]{1,2,0:T(8,128)} %broadcast_in_dim.200), calls=%async_computation.5 | async-start | bytes 786432 | tf_op jit(solution)/shard_map/all_to_all | solution.py:79
  279.5 6.3 %copy-start.17 = (s32[32]{0:T(128)S(1)}, s32[32]{0:T(128)}, u32[]{:S(2)}) copy-start(s32[32]{0:T(128)} %get-tuple-element.11) | copy-start | bytes 388
  279.5 6.3 %copy-start.16 = (s32[31]{0:T(128)S(1)}, s32[31]{0:T(128)}, u32[]{:S(2)}) copy-start(s32[31]{0:T(128)} %copy-done.15) | copy-start | bytes 376
  281.2 21.9 %all-to-all-start.7 = ((bf16[32,8,2048]{2,1,0:T(8,128)(2,1)}), bf16[32,8,2048]{2,1,0:T(8,128)(2,1)}, u32[]{:S(2)}, u32[]{:S(2)}) async-start(bf16[32,8,2048]{2,1,0:T(8,128)(2,1)} %broadcast_in_dim.201), calls=%async_computation.7 | async-start | bytes 2097152 | tf_op jit(solution)/shard_map/all_to_all | solution.py:79
  305.5 12.8 %all-to-all-start.8 = ((f32[4,256,96]{1,2,0:T(8,128)}), f32[4,256,96]{1,2,0:T(8,128)}, u32[]{:S(2)}, u32[]{:S(2)}) async-start(f32[4,256,96]{1,2,0:T(8,128)} %broadcast_in_dim.202), calls=%async_computation.8 | async-start | bytes 786432 | tf_op jit(solution)/shard_map/all_to_all | solution.py:79
